TPU v7x, 512 devices: a whole 4x8x8 slice. The times are simulated.
512 devices in a mesh: seg: 32 (over x_lo, z, core), tpl: 16 (over x_hi, y).
Axes of the slice: x: 4 (x_hi: 2, x_lo: 2; x = x_hi * 2 + x_lo), y: 8, z: 8, core: 2. Of those that a mesh axis runs over, the one named last changes fastest.
Arguments:
- strain: bfloat16 [1024, 2, 2, 128, 128], P(('seg', 'tpl')), may hold values from -6 to 6
- templates: bfloat16 [64, 2, 128, 128], P('tpl'), may hold values from -6 to 6
- psd: float32 [2, 128, 128], P(None, 'seg'), may hold values from 0.25 to 4
- flags: int32 [1024], P(('seg', 'tpl')), may hold values 0 or 1
- assign: int32 [64], replicated, may hold values from 0 to 7
Outputs:
- peak: float32 [1024, 64], P(('seg', 'tpl'))
- best: float32 [1024, 8], P(('seg', 'tpl'))
All inputs are finite; a program needn't handle non-finite values. No bound on the sum of `flags` on one device may be relied on, other than what follows from the above.
Results may differ from a plain program's by a relative error of at most 0.0015.
Values may be sent and summed in bfloat16 or wider, within the bound.
No kernel may reach another device: no remote copies, remote signals or barrier semaphores. Data moves between devices by JAX's collectives and lax.ppermute only.
A program may use at most 64 MiB of HBM per device.

v0:
```python
import math

import jax
import jax.numpy as jnp
from jax import lax
from jax.sharding import PartitionSpec as P

N1 = 128
N2 = 128
BINS = 16384
BLOCKS = 8


def make_tables():
    row_idx = jnp.arange(N1, dtype=jnp.int32)
    col_idx = jnp.arange(N2, dtype=jnp.int32)
    ang_one = 2.0 * math.pi * (row_idx[:, None] * row_idx[None, :] % N1).astype(jnp.float32) / N1
    cos_one, sin_one = (jnp.cos(ang_one), jnp.sin(ang_one))
    first = jnp.concatenate(
        [jnp.concatenate([cos_one, -sin_one], 1), jnp.concatenate([sin_one, cos_one], 1)], 0
    ).astype(jnp.bfloat16)
    ang_two = 2.0 * math.pi * (col_idx[:, None] * col_idx[None, :] % N2).astype(jnp.float32) / N2
    cos_two, sin_two = (jnp.cos(ang_two), jnp.sin(ang_two))
    second = jnp.concatenate(
        [jnp.concatenate([cos_two, sin_two], 1), jnp.concatenate([-sin_two, cos_two], 1)], 0
    ).astype(jnp.bfloat16)
    ang_tw = 2.0 * math.pi * (row_idx[:, None] * col_idx[None, :] % BINS).astype(jnp.float32) / BINS
    return (first, second, jnp.cos(ang_tw), jnp.sin(ang_tw))


def template_norm(tmpl, weights):
    h_re = tmpl[0].astype(jnp.float32)
    h_im = tmpl[1].astype(jnp.float32)
    return jnp.sum((h_re * h_re + h_im * h_im) * weights, axis=(1, 2))


def power_peak(seg_data, tmpl, sigma2, weights, tables):
    first, second, tw_cos, tw_sin = tables
    count = seg_data.shape[0]
    h_re = tmpl[0].astype(jnp.float32)
    h_im = tmpl[1].astype(jnp.float32)
    d_re = seg_data[:, :, 0].astype(jnp.float32)
    d_im = seg_data[:, :, 1].astype(jnp.float32)
    q_re = (d_re * h_re + d_im * h_im) * weights
    q_im = (d_im * h_re - d_re * h_im) * weights
    stacked = jnp.stack([q_re, q_im], 2).reshape(count * 2, 2 * N1, N2).astype(jnp.bfloat16)
    rotated = jnp.einsum("ij,bjk->bik", first, stacked, preferred_element_type=jnp.float32)
    y_re, y_im = (rotated[:, :N1], rotated[:, N1:])
    z_re = y_re * tw_cos - y_im * tw_sin
    z_im = y_re * tw_sin + y_im * tw_cos
    twisted = jnp.concatenate([z_re, z_im], -1).astype(jnp.bfloat16)
    series = jnp.einsum("bik,kl->bil", twisted, second, preferred_element_type=jnp.float32)
    power = series[:, :, :N2] ** 2 + series[:, :, N2:] ** 2
    power = power.reshape(count, 2, N1, N2)
    rho2 = jnp.sum(power / sigma2[None, :, None, None], axis=1)
    return jnp.max(rho2, axis=(1, 2))


def body(strain, templates, psd, flags, assign):
    full_psd = lax.all_gather(psd, "seg", axis=1, tiled=True)
    weights = 1.0 / full_psd
    tables = make_tables()
    local_norms = jax.vmap(lambda tmpl: template_norm(tmpl, weights))(templates)
    piece = lax.all_gather(strain, "tpl", axis=0, tiled=True)

    def one_template(pair):
        return power_peak(piece, pair[0], pair[1], weights, tables)

    values = lax.map(one_template, (templates, local_norms))
    grouped = values.T
    rho2 = lax.all_to_all(grouped, "tpl", split_axis=0, concat_axis=1, tiled=True)
    peak = jnp.sqrt(rho2) * flags.astype(jnp.float32)[:, None]
    onehot = assign[:, None] == jnp.arange(BLOCKS, dtype=jnp.int32)[None, :]
    best = jnp.max(jnp.where(onehot[None], peak[:, :, None], jnp.float32(0.0)), axis=1)
    return (peak, best)


def solution(mesh):
    placed = (
        P(("seg", "tpl"), None, None, None, None),
        P("tpl", None, None, None),
        P(None, "seg", None),
        P(("seg", "tpl")),
        P(),
    )
    return jax.shard_map(
        body,
        mesh=mesh,
        in_specs=placed,
        out_specs=(P(("seg", "tpl"), None), P(("seg", "tpl"), None)),
        check_vma=False,
    )
```

profile of v0, /device:TPU:2, one launch (start us, length us, event | category | flops | bytes accessed | tf_op | source)
XLA Modules:
  0.0 182.5 jit_solution(759579694405056651)
XLA Ops:
  7.2 0.7 all-gather.2.cloned.1.call-update
  7.9 0.7 copy.39
  8.6 39.9 %all_gather.7 = f32[2,128,128]{2,0,1:T(2,128)S(1)} all-gather(f32[2,4,128]{2,0,1:T(2,128)S(1)} %copy.39), channel_id=1, replica_groups=mesh['seg'=32,'tpl'=16] {'seg'}, dimensions={1}, use_global_device_ids=true | all-gather | bytes 135168 | tf_op jit(solution)/shard_map/all_gather | solution.py:60
  48.6 0.3 fusion.38
  48.8 0.3 negate_convert_fusion
  49.2 1.0 add_bitcast_fusion
  50.3 69.6 %all-gather.2.cloned.1.call-done = bf16[32,2,2,128,128]{4,3,2,1,0:T(8,128)(2,1)} async-done(((bf16[2,2,2,128,128]{4,3,2,1,0:T(8,128)(2,1)}), bf16[32,2,2,128,128]{4,3,2,1,0:T(8,128)(2,1)}) %all-gather.2.cloned.1.call-update) | async-done | bytes 4194320 | tf_op jit(solution)/shard_map/all_gather | solution.py:64
  119.9 39.0 %while.12 = (s32[]{:T(128)}, f32[4,32]{1,0:T(4,128)S(1)}, bf16[32,2,2,128,128]{4,3,2,1,0:T(8,128)(2,1)}, bf16[4,2,128,128]{3,2,1,0:T(8,128)(2,1)}, f32[2,128,128...) while((s32[]{:T(128)}, f32[4,32]{1,0:T(4,128)S(1)}, ...), condition=%wide.region_4.5_spmd.clone.clone, body=%wide.region_1.4_spmd.clone.clone.sunk | while | flops 2184445952 | bytes 68092456 | solution.py:69
  119.9 0.8 fusion.54
  120.8 3.2 %fusion.55 = (bf16[32,2,1,128,128]{4,3,2,1,0:T(8,128)(2,1)S(1)}, bf16[32,2,1,128,128]{4,3,2,1,0:T(8,128)(2,1)S(1)}) fusion(f32[2,128,128]{2,1,0:T(8,128)S(1)} %get-tuple-element.268, f32[128,128]{1,0:T(8,128)S(1)} %get-tuple-element.232, f32[128,128]{1,0:T(8,128)S(1)} %get-tuple-element.233, bf16[32,2,2,128,128]{4,3,2,1,0:T(8,128)(2,1)} %get-tuple-element.266), kind=kLoop, calls=%fused_computation.8.clone.1 | loop fusion | flops 12582912 | bytes 8650752 | tf_op jit(solution)/shard_map/convert.4
  124.0 0.4 pad_maximum_fusion.6
  124.4 1.3 convolution_bitcast_fusion.2
  125.7 0.3 fusion.56
  126.0 1.2 subtract_convert_fusion.2
  127.2 1.3 fusion.57
  128.6 0.8 divide_reduce_fusion.2
  129.3 0.3 reduce_max.23
  129.7 0.8 fusion.54
  130.5 3.2 %fusion.55 = (bf16[32,2,1,128,128]{4,3,2,1,0:T(8,128)(2,1)S(1)}, bf16[32,2,1,128,128]{4,3,2,1,0:T(8,128)(2,1)S(1)}) fusion(f32[2,128,128]{2,1,0:T(8,128)S(1)} %get-tuple-element.268, f32[128,128]{1,0:T(8,128)S(1)} %get-tuple-element.232, f32[128,128]{1,0:T(8,128)S(1)} %get-tuple-element.233, bf16[32,2,2,128,128]{4,3,2,1,0:T(8,128)(2,1)} %get-tuple-element.266), kind=kLoop, calls=%fused_computation.8.clone.1 | loop fusion | flops 12582912 | bytes 8650752 | tf_op jit(solution)/shard_map/convert.4
  133.8 0.4 pad_maximum_fusion.6
  134.2 1.3 convolution_bitcast_fusion.2
  135.5 0.3 fusion.56
  135.8 1.2 subtract_convert_fusion.2
  137.0 1.3 fusion.57
  138.3 0.8 divide_reduce_fusion.2
  139.1 0.3 reduce_max.23
  139.5 0.8 fusion.54
  140.2 3.2 %fusion.55 = (bf16[32,2,1,128,128]{4,3,2,1,0:T(8,128)(2,1)S(1)}, bf16[32,2,1,128,128]{4,3,2,1,0:T(8,128)(2,1)S(1)}) fusion(f32[2,128,128]{2,1,0:T(8,128)S(1)} %get-tuple-element.268, f32[128,128]{1,0:T(8,128)S(1)} %get-tuple-element.232, f32[128,128]{1,0:T(8,128)S(1)} %get-tuple-element.233, bf16[32,2,2,128,128]{4,3,2,1,0:T(8,128)(2,1)} %get-tuple-element.266), kind=kLoop, calls=%fused_computation.8.clone.1 | loop fusion | flops 12582912 | bytes 8650752 | tf_op jit(solution)/shard_map/convert.4
  143.5 0.4 pad_maximum_fusion.6
  143.9 1.3 convolution_bitcast_fusion.2
  145.2 0.3 fusion.56
  145.5 1.2 subtract_convert_fusion.2
  146.7 1.3 fusion.57
  148.0 0.8 divide_reduce_fusion.2
  148.8 0.3 reduce_max.23
  149.2 0.8 fusion.54
  150.0 3.2 %fusion.55 = (bf16[32,2,1,128,128]{4,3,2,1,0:T(8,128)(2,1)S(1)}, bf16[32,2,1,128,128]{4,3,2,1,0:T(8,128)(2,1)S(1)}) fusion(f32[2,128,128]{2,1,0:T(8,128)S(1)} %get-tuple-element.268, f32[128,128]{1,0:T(8,128)S(1)} %get-tuple-element.232, f32[128,128]{1,0:T(8,128)S(1)} %get-tuple-element.233, bf16[32,2,2,128,128]{4,3,2,1,0:T(8,128)(2,1)} %get-tuple-element.266), kind=kLoop, calls=%fused_computation.8.clone.1 | loop fusion | flops 12582912 | bytes 8650752 | tf_op jit(solution)/shard_map/convert.4
  153.2 0.4 pad_maximum_fusion.6
  153.7 1.3 convolution_bitcast_fusion.2
  155.0 0.3 fusion.56
  155.3 1.2 subtract_convert_fusion.2
  156.5 1.3 fusion.57
  157.8 0.8 divide_reduce_fusion.2
  158.6 0.3 reduce_max.23
  158.9 0.7 copy.42
  159.6 5.2 %all-to-all-start = ((f32[16,2,4]{2,1,0:T(2,128)}), f32[16,2,4]{2,1,0:T(2,128)S(1)}, u32[]{:S(2)}, u32[]{:S(2)}) async-start(f32[16,2,4]{2,1,0:T(2,128)} %bitcast.2), calls=%async_computation | async-start | bytes 32768 | tf_op jit(solution)/shard_map/all_to_all | solution.py:71
  164.9 9.9 %all-to-all-done = f32[16,2,4]{2,1,0:T(2,128)S(1)} async-done(((f32[16,2,4]{2,1,0:T(2,128)}), f32[16,2,4]{2,1,0:T(2,128)S(1)}, u32[]{:S(2)}, u32[]{:S(2)}) %all-to-all-start) | async-done | bytes 544 | tf_op jit(solution)/shard_map/all_to_all | solution.py:71
  175.0 0.7 select_reduce_fusion
  (26 shorter events, 0.7 us)
Async XLA Ops:
  7.2 112.8 %all-gather.2.cloned.1.call-start = ((), (), s32[]{:S(2)}) async-start(), calls=%async_computation.1 | async-start | bytes 4456448 | tf_op jit(solution)/shard_map/all_gather | solution.py:64
  119.9 44.9 %copy-start.1 = (s32[64]{0:T(128)S(1)}, s32[64]{0:T(128)}, u32[]{:S(2)}) copy-start(s32[64]{0:T(128)} %param.11) | copy-start | bytes 772
  119.9 44.9 %copy-start.2 = (s32[2]{0:T(128)S(1)}, s32[2]{0:T(128)}, u32[]{:S(2)}) copy-start(s32[2]{0:T(128)} %param.10) | copy-start | bytes 28
  159.6 15.2 %all-to-all-start = ((f32[16,2,4]{2,1,0:T(2,128)}), f32[16,2,4]{2,1,0:T(2,128)S(1)}, u32[]{:S(2)}, u32[]{:S(2)}) async-start(f32[16,2,4]{2,1,0:T(2,128)} %bitcast.2), calls=%async_computation | async-start | bytes 32768 | tf_op jit(solution)/shard_map/all_to_all | solution.py:71
  175.0 0.7 copy-start
Sparse Core Ops, SparseCore 0:
  11.1 108.7 all-gather.1
where the time goes:
time: 183 us
  waiting for transfers between devices  80.2 us (44%)
  blocking collectives  39.9 us (22%)
  other arithmetic  30.7 us (17%)
  between operations  14.1 us (8%)
  matrix products  10.5 us (6%)
  starting transfers between devices  5.24 us (3%)
    all_gather x1, waiting for transfers between devices, body(): piece = lax.all_gather(strain, 'tpl', axis=0, tiled=True)  69.6 us
    all_gather x1, blocking collectives, body(): full_psd = lax.all_gather(psd, 'seg', axis=1, tiled=True)  39.9 us
    another operation x10, other arithmetic  18.3 us
    all_to_all x1, waiting for transfers between devices, body(): lax.all_to_all(grouped, 'tpl', split_axis=0, concat_axis=1, tiled=True)  9.95 us
    dot_general x4, matrix products, power_peak(): jnp.einsum('ij,bjk->bik', first, stacked, preferred_element_type=jnp.floa...  5.26 us
    dot_general x4, matrix products, power_peak(): jnp.einsum('bik,kl->bil', twisted, second, preferred_element_type=jnp.flo...  5.22 us
    all_to_all x1, starting transfers between devices, body(): lax.all_to_all(grouped, 'tpl', split_axis=0, concat_axis=1, tiled=True)  5.2 us
  transfers between devices with their start and end apart: 2, of which 2 were waited for; matrix products, arithmetic and copies ran while one was open for 1% of the time, Pallas kernels for 0%

commit v1 on v0

v1 whole, which is shorter than its diff:
```python
import functools
import math

import jax
import jax.numpy as jnp
from jax import lax
from jax.experimental import pallas as pl
from jax.experimental.pallas import tpu as pltpu
from jax.sharding import Mesh
from jax.sharding import PartitionSpec as P

N1 = 128
N2 = 128
BINS = 16384
BLOCKS = 8
TB = 4


def make_tables():
    row_idx = jnp.arange(N1, dtype=jnp.int32)
    col_idx = jnp.arange(N2, dtype=jnp.int32)
    ang_one = 2.0 * math.pi * (row_idx[:, None] * row_idx[None, :] % N1).astype(jnp.float32) / N1
    cos_one, sin_one = (jnp.cos(ang_one), jnp.sin(ang_one))
    first = jnp.concatenate(
        [jnp.concatenate([cos_one, -sin_one], 1), jnp.concatenate([sin_one, cos_one], 1)], 0
    ).astype(jnp.bfloat16)
    ang_two = 2.0 * math.pi * (col_idx[:, None] * col_idx[None, :] % N2).astype(jnp.float32) / N2
    cos_two, sin_two = (jnp.cos(ang_two), jnp.sin(ang_two))
    second = jnp.concatenate(
        [jnp.concatenate([cos_two, sin_two], 1), jnp.concatenate([-sin_two, cos_two], 1)], 0
    ).astype(jnp.bfloat16)
    ang_tw = 2.0 * math.pi * (row_idx[:, None] * col_idx[None, :] % BINS).astype(jnp.float32) / BINS
    return (first, second, jnp.cos(ang_tw), jnp.sin(ang_tw))


def template_norm(tmpl, weights):
    h_re = tmpl[0].astype(jnp.float32)
    h_im = tmpl[1].astype(jnp.float32)
    return jnp.sum((h_re * h_re + h_im * h_im) * weights, axis=(1, 2))


def search_kernel(n_tb, sidx_ref, isig_ref, strain_ref, tmpl_ref, w_ref, m1_ref, m2_ref,
                  tc_ref, ts_ref, out_ref, q_ref, y_ref, z_ref):
    nb = 2 * TB

    def step(i, carry):
        s = i // n_tb
        tb = i % n_tb
        seg = sidx_ref[s]
        for k in range(TB):
            t = tb * TB + k
            h_re = tmpl_ref[t, 0].astype(jnp.float32)
            h_im = tmpl_ref[t, 1].astype(jnp.float32)
            for d in range(2):
                d_re = strain_ref[seg, d, 0].astype(jnp.float32)
                d_im = strain_ref[seg, d, 1].astype(jnp.float32)
                w = w_ref[d]
                q_re = (d_re * h_re + d_im * h_im) * w
                q_im = (d_im * h_re - d_re * h_im) * w
                col = (2 * k + d) * N2
                q_ref[0:N1, col:col + N2] = q_re.astype(jnp.bfloat16)
                q_ref[N1:2 * N1, col:col + N2] = q_im.astype(jnp.bfloat16)
        y_ref[...] = jnp.dot(m1_ref[...], q_ref[...], preferred_element_type=jnp.float32)
        tc = tc_ref[...]
        ts = ts_ref[...]
        for b in range(nb):
            col = b * N2
            y_re = y_ref[0:N1, col:col + N2]
            y_im = y_ref[N1:2 * N1, col:col + N2]
            z_re = y_re * tc - y_im * ts
            z_im = y_re * ts + y_im * tc
            z_ref[col:col + N2, 0:N2] = z_re.astype(jnp.bfloat16)
            z_ref[col:col + N2, N2:2 * N2] = z_im.astype(jnp.bfloat16)
        x = jnp.dot(z_ref[...], m2_ref[...], preferred_element_type=jnp.float32)
        for k in range(TB):
            t = tb * TB + k
            acc = None
            for d in range(2):
                r0 = (2 * k + d) * N1
                x_re = x[r0:r0 + N1, 0:N2]
                x_im = x[r0:r0 + N1, N2:2 * N2]
                p = (x_re * x_re + x_im * x_im) * isig_ref[2 * t + d]
                acc = p if acc is None else acc + p
            out_ref[s, pl.ds(t, 1), :] = jnp.max(acc, axis=0, keepdims=True)
        return carry

    lax.fori_loop(0, sidx_ref.shape[0] * n_tb, step, 0)


def run_search(sidx, isig, strain, tmpl, weights, tables):
    m1, m2, tc, ts = tables
    n_s = sidx.shape[0]
    n_t = tmpl.shape[0]
    n_tb = n_t // TB
    vmem = pltpu.VMEM
    smem = pltpu.SMEM
    ffts = n_s * n_t * 2
    cost = pl.CostEstimate(
        flops=ffts * 2 * (2 * 256 * 256 * 128),
        transcendentals=0,
        bytes_accessed=strain.size * 2 + tmpl.size * 2 + weights.size * 4,
    )
    out = pl.pallas_call(
        functools.partial(search_kernel, n_tb),
        out_shape=jax.ShapeDtypeStruct((n_s, n_t, N2), jnp.float32),
        in_specs=[pl.BlockSpec(memory_space=smem), pl.BlockSpec(memory_space=smem)]
        + [pl.BlockSpec(memory_space=vmem)] * 7,
        out_specs=pl.BlockSpec(memory_space=vmem),
        scratch_shapes=[
            pltpu.VMEM((2 * N1, 2 * TB * N2), jnp.bfloat16),
            pltpu.VMEM((2 * N1, 2 * TB * N2), jnp.float32),
            pltpu.VMEM((2 * TB * N1, 2 * N2), jnp.bfloat16),
        ],
        cost_estimate=cost,
    )(sidx, isig, strain, tmpl, weights, m1, m2, tc, ts)
    return jnp.max(out, axis=-1)


def body(strain, templates, psd, flags, assign):
    ya = lax.axis_index("ya")
    n_ya = lax.axis_size("ya")
    rows_here = psd.shape[1]
    psd_t = jnp.transpose(psd, (1, 0, 2)).reshape(rows_here, -1)
    gathered = lax.all_gather(psd_t, "seg", axis=0, tiled=True)
    full_psd = jnp.transpose(gathered.reshape(-1, 2, N2), (1, 0, 2))
    weights = 1.0 / full_psd
    tables = make_tables()
    tmpl_all = lax.all_gather(templates, ("xh", "yb"), axis=0, tiled=True)
    piece = lax.all_gather(strain, "ya", axis=0, tiled=True)
    sigma2 = jax.vmap(lambda tmpl: template_norm(tmpl, weights))(tmpl_all)
    isig = (1.0 / sigma2).reshape(-1)

    own_count = strain.shape[0]
    own_idx = jnp.arange(own_count, dtype=jnp.int32)
    own_rows = run_search(own_idx, isig, strain, tmpl_all, weights, tables)

    own_rows, piece = lax.optimization_barrier((own_rows, piece))
    shifts = jnp.arange(1, n_ya, dtype=jnp.int32)
    other_blocks = (ya + shifts) % n_ya
    other_idx = (other_blocks[:, None] * own_count + own_idx[None, :]).reshape(-1)
    other_rows = run_search(other_idx, isig, piece, tmpl_all, weights, tables)

    rolled = jnp.concatenate([own_rows, other_rows], 0).reshape(n_ya, own_count, -1)
    grouped = jnp.roll(rolled, ya, axis=0)
    got = lax.all_to_all(grouped, "ya", split_axis=0, concat_axis=0, tiled=True)
    n_xh = lax.axis_size("xh")
    n_yb = lax.axis_size("yb")
    got = got.reshape(n_ya, own_count, n_xh, n_yb, -1)
    rho2 = jnp.transpose(got, (1, 2, 0, 3, 4)).reshape(own_count, -1)

    peak = jnp.sqrt(rho2) * flags.astype(jnp.float32)[:, None]
    onehot = assign[:, None] == jnp.arange(BLOCKS, dtype=jnp.int32)[None, :]
    best = jnp.max(jnp.where(onehot[None], peak[:, :, None], jnp.float32(0.0)), axis=1)
    return (peak, best)


def solution(mesh):
    n_seg, n_tpl = mesh.devices.shape
    n_y = 8
    n_xh = n_tpl // n_y
    sub = Mesh(
        mesh.devices.reshape(n_seg, n_xh, n_y // 2, 2),
        ("seg", "xh", "ya", "yb"),
    )
    rows = ("seg", "xh", "ya", "yb")
    placed = (
        P(rows, None, None, None, None),
        P(("xh", "ya", "yb"), None, None, None),
        P(None, "seg", None),
        P(rows),
        P(),
    )
    return jax.shard_map(
        body,
        mesh=sub,
        in_specs=placed,
        out_specs=(P(rows, None), P(rows, None)),
        check_vma=False,
    )
```

time: 183 us -> 132 us (0.72)
  waiting for transfers between devices: 80.2 us -> 35.9 us
  Pallas kernels: 0 us -> 28.6 us
  other arithmetic: 30.7 us -> 6.98 us
  matrix products: 10.5 us -> 0 us
    all_gather x1 -> x2, waiting for transfers between devices: 69.6 us -> 26.8 us  [the longest x1 26.8 us: body(): piece = lax.all_gather(strain, 'ya', axis=0, tiled=True)]
    pallas_call x0 -> x2, Pallas kernels: none -> 28.6 us  [run_search(): pl.pallas_call(functools.partial(search_kernel, n_tb), out_shape=jax.Shap...]
    another operation x14 -> x2, other arithmetic: 19.9 us -> 0.54 us
    dot_general x8 -> x0, matrix products: 10.5 us -> none  [the longest x4 5.26 us: power_peak(): jnp.einsum('ij,bjk->bik', first, stacked, preferred_element_type=jnp.floa...]
    mul x4 -> x1, other arithmetic: 3.18 us -> 0.01 us  [body(): other_blocks[:, None] * own_count + own_idx[None, :]]
    reduce_sum x4 -> x0, other arithmetic: 3.1 us -> none  [power_peak(): rho2 = jnp.sum(power / sigma2[None, :, None, None], axis=1)]
    all_to_all x1, waiting for transfers between devices: 9.95 us -> 7.68 us  [body(): got = lax.all_to_all(grouped, 'ya', split_axis=0, concat_axis=0, tiled=True)]
  transfers between devices with their start and end apart: 2 -> 3, of which waited for: 2 -> 2; matrix products, arithmetic and copies ran while one was open for 1% -> 5% of each run, Pallas kernels for 0% -> 6%
where the time goes in v1:
time: 132 us; the launch traced here: 131 us
  blocking collectives  40.1 us (30%)
  waiting for transfers between devices  35.9 us (27%)
  Pallas kernels  28.6 us (22%)
  between operations  14.2 us (11%)
  other arithmetic  6.98 us (5%)
  starting transfers between devices  3.59 us (3%)
  local copies, waits for them, and re-layouts  2.12 us (2%)
    all_gather x1, blocking collectives, body(): gathered = lax.all_gather(psd_t, 'seg', axis=0, tiled=True)  40.1 us
    pallas_call x2, Pallas kernels, run_search(): pl.pallas_call(functools.partial(search_kernel, n_tb), out_shape=jax.Shap...  28.6 us
    all_gather x1, waiting for transfers between devices, body(): piece = lax.all_gather(strain, 'ya', axis=0, tiled=True)  26.8 us
    all_to_all x1, waiting for transfers between devices, body(): got = lax.all_to_all(grouped, 'ya', split_axis=0, concat_axis=0, tiled=True)  7.68 us
    all_to_all x1, starting transfers between devices, body(): got = lax.all_to_all(grouped, 'ya', split_axis=0, concat_axis=0, tiled=True)  3.51 us
  transfers between devices with their start and end apart: 3, of which 2 were waited for; matrix products, arithmetic and copies ran while one was open for 5% of the time, Pallas kernels for 6%

profile of v1, /device:TPU:2, one launch (start us, length us, event | category | flops | bytes accessed | tf_op | source)
XLA Modules:
  0.0 131.3 jit_solution(3866874880758580075)
XLA Ops:
  7.2 0.0 all-gather.4.cloned.1.call-start
  7.2 0.7 all-gather.4.cloned.1.call-update
  7.9 0.0 all-gather.6.cloned.1.call-start
  7.9 0.7 all-gather.6.cloned.1.call-update
  8.7 40.1 %all-gather = f32[32,4,256]{2,1,0:T(4,128)S(1)} all-gather(f32[1,4,256]{2,1,0:T(4,128)} %bitcast.15), channel_id=1, replica_groups=mesh['seg'=32,'xh'=2,'ya'=4,'yb'=2] {'seg'}, dimensions={0}, use_global_device_ids=true | all-gather | bytes 135168 | tf_op jit(solution)/shard_map/all_gather | solution.py:124
  48.8 0.1 div.55
  48.9 0.0 copy-start
  48.9 0.1 iota_add_fusion
  49.0 0.6 add.100.sidx_ref
  49.6 0.3 fusion.16
  49.8 0.3 negate_convert_fusion
  50.1 0.9 fusion.13
  51.0 0.7 fusion.1
  51.8 0.0 all-gather.4.cloned.1.call-done.tmpl_ref
  51.8 1.4 %add_bitcast_fusion = f32[16,128,128]{2,1,0:T(8,128)S(1)} fusion(bf16[16,2,128,128]{3,2,1,0:T(8,128)(2,1)} %all-gather.4.cloned.1.call-done.tmpl_ref), kind=kLoop, calls=%fused_computation.1 | loop fusion | flops 1310720 | bytes 2097152 | tf_op jit(solution)/shard_map/vmap()/mul | solution.py:39
  53.2 0.0 copy-done
  53.2 0.3 multiply_reduce_fusion
  53.4 0.6 div.58.isig_ref
  54.0 0.6 iota.27.sidx_ref
  54.6 8.1 %shard_map.68 = f32[2,16,128]{2,1,0:T(8,128)} custom-call(s32[2]{0:T(128)} %iota.27.sidx_ref, f32[32]{0:T(128)} %div.58.isig_ref, bf16[2,2,2,128,128]{4,3,2,1,0:T(8,128)(2,1)} %strain_ref.1, bf16[16,2,128,128]{3,2,1,0:T(8,128)(2,1)} %all-gather.4.cloned.1.call-done.tmpl_ref, f32[2,128,128]{2,1,0:T(8,128)} %bitcast.11, ...), custom_call_target="tpu_custom_call" | custom-call | flops 2147483648 | bytes 1441792 | tf_op jit(solution)/shard_map/pallas_call | solution.py:103
  62.7 0.8 reduce_max.27
  63.5 0.0 copy-start.2
  63.5 0.0 copy-start.3
  63.5 26.8 %all-gather.6.cloned.1.call-done.strain_ref = bf16[8,2,2,128,128]{4,3,2,1,0:T(8,128)(2,1)} async-done(((bf16[2,2,2,128,128]{4,3,2,1,0:T(8,128)(2,1)}), bf16[8,2,2,128,128]{4,3,2,1,0:T(8,128)(2,1)}) %all-gather.6.cloned.1.call-update) | async-done | bytes 1048592 | tf_op jit(solution)/shard_map/all_gather | solution.py:129
  90.3 20.5 %shard_map.69 = f32[6,16,128]{2,1,0:T(8,128)} custom-call(s32[6]{0:T(128)} %add.100.sidx_ref, f32[32]{0:T(128)} %div.58.isig_ref, bf16[8,2,2,128,128]{4,3,2,1,0:T(8,128)(2,1)} %all-gather.6.cloned.1.call-done.strain_ref, bf16[16,2,128,128]{3,2,1,0:T(8,128)(2,1)} %all-gather.4.cloned.1.call-done.tmpl_ref, f32[2,128,128]{2,1,0:T(8,128)} %bitcast.12, ...), custom_call_target="tpu_custom_call" | custom-call | flops 6442450944 | bytes 2228224 | tf_op jit(solution)/shard_map/pallas_call | solution.py:103
  110.8 0.9 reduce_max.28
  111.7 0.6 fusion.17
  112.3 3.5 %all-to-all-start = ((f32[4,2,16]{2,1,0:T(2,128)}), f32[4,2,16]{2,1,0:T(2,128)S(1)}, u32[]{:S(2)}, u32[]{:S(2)}) async-start(f32[4,2,16]{2,1,0:T(2,128)} %fusion.17), calls=%async_computation | async-start | bytes 8192 | tf_op jit(solution)/shard_map/all_to_all | solution.py:145
  115.8 0.0 copy-done.2
  115.9 0.0 copy-done.3
  115.9 7.7 %all-to-all-done = f32[4,2,16]{2,1,0:T(2,128)S(1)} async-done(((f32[4,2,16]{2,1,0:T(2,128)}), f32[4,2,16]{2,1,0:T(2,128)S(1)}, u32[]{:S(2)}, u32[]{:S(2)}) %all-to-all-start) | async-done | bytes 544 | tf_op jit(solution)/shard_map/all_to_all | solution.py:145
  123.6 0.1 sqrt.17
  123.7 0.1 sqrt.19
  123.8 0.1 broadcast_multiply_fusion
  123.8 0.0 copy-start.1
  123.8 0.7 select_reduce_fusion
  124.5 0.0 copy-done.1
  (9 shorter events, 0.1 us)
Async XLA Ops:
  7.2 44.6 %all-gather.4.cloned.1.call-start = ((), (), s32[]{:S(2)}) async-start(), calls=%async_computation.1 | async-start | bytes 1310720 | tf_op jit(solution)/shard_map/all_gather | solution.py:128
  7.9 82.4 %all-gather.6.cloned.1.call-start = ((), (), s32[]{:S(2)}) async-start(), calls=%async_computation.2 | async-start | bytes 1310720 | tf_op jit(solution)/shard_map/all_gather | solution.py:129
  48.9 4.2 %copy-start = (f32[128,2,128]{2,0,1:T(8,128)}, f32[128,2,128]{2,0,1:T(8,128)S(1)}, u32[]{:S(2)}) copy-start(f32[128,2,128]{2,0,1:T(8,128)S(1)} %copy.15) | copy-start | bytes 393220
  63.5 52.3 %copy-start.2 = (s32[64]{0:T(128)S(1)}, s32[64]{0:T(128)}, u32[]{:S(2)}) copy-start(s32[64]{0:T(128)} %param.9) | copy-start | bytes 772
  63.5 52.3 %copy-start.3 = (s32[2]{0:T(128)S(1)}, s32[2]{0:T(128)}, u32[]{:S(2)}) copy-start(s32[2]{0:T(128)} %param.8) | copy-start | bytes 28
  112.3 11.2 %all-to-all-start = ((f32[4,2,16]{2,1,0:T(2,128)}), f32[4,2,16]{2,1,0:T(2,128)S(1)}, u32[]{:S(2)}, u32[]{:S(2)}) async-start(f32[4,2,16]{2,1,0:T(2,128)} %fusion.17), calls=%async_computation | async-start | bytes 8192 | tf_op jit(solution)/shard_map/all_to_all | solution.py:145
  123.8 0.7 copy-start.1
Sparse Core Ops, SparseCore 0:
  10.1 40.4 all-gather.3
  52.7 37.6 all-gather.5

commit v2 on v1

--- a/solution.py
+++ b/solution.py
@@ -116,37 +116,48 @@
     return jnp.max(out, axis=-1)
 
 
+def shifted(x, axes, size, k):
+    return lax.ppermute(x, axes, [(i, (i + k) % size) for i in range(size)])
+
+
 def body(strain, templates, psd, flags, assign):
     ya = lax.axis_index("ya")
     n_ya = lax.axis_size("ya")
+    n_xh = lax.axis_size("xh")
+    n_yb = lax.axis_size("yb")
+    n_g = n_xh * n_yb
+    g = lax.axis_index("xh") * n_yb + lax.axis_index("yb")
+
     rows_here = psd.shape[1]
-    psd_t = jnp.transpose(psd, (1, 0, 2)).reshape(rows_here, -1)
-    gathered = lax.all_gather(psd_t, "seg", axis=0, tiled=True)
+    gathered = jnp.transpose(psd, (1, 0, 2)).reshape(rows_here, -1)
+    for axis in ("sc", "sz", "sx"):
+        gathered = lax.all_gather(gathered, axis, axis=0, tiled=True)
     full_psd = jnp.transpose(gathered.reshape(-1, 2, N2), (1, 0, 2))
     weights = 1.0 / full_psd
     tables = make_tables()
-    tmpl_all = lax.all_gather(templates, ("xh", "yb"), axis=0, tiled=True)
-    piece = lax.all_gather(strain, "ya", axis=0, tiled=True)
-    sigma2 = jax.vmap(lambda tmpl: template_norm(tmpl, weights))(tmpl_all)
+
+    tmpl_rel = jnp.concatenate(
+        [templates] + [shifted(templates, ("xh", "yb"), n_g, k) for k in range(1, n_g)], 0
+    )
+    piece = jnp.concatenate([shifted(strain, "ya", n_ya, k) for k in range(1, n_ya)], 0)
+    sigma2 = jax.vmap(lambda tmpl: template_norm(tmpl, weights))(tmpl_rel)
     isig = (1.0 / sigma2).reshape(-1)
 
     own_count = strain.shape[0]
     own_idx = jnp.arange(own_count, dtype=jnp.int32)
-    own_rows = run_search(own_idx, isig, strain, tmpl_all, weights, tables)
+    own_rows = run_search(own_idx, isig, strain, tmpl_rel, weights, tables)
+    own_rows, piece = lax.optimization_barrier((own_rows, piece))
+    other_idx = jnp.arange(piece.shape[0], dtype=jnp.int32)
+    other_rows = run_search(other_idx, isig, piece, tmpl_rel, weights, tables)
+    other_rows = other_rows.reshape(n_ya - 1, own_count, -1)
 
-    own_rows, piece = lax.optimization_barrier((own_rows, piece))
-    shifts = jnp.arange(1, n_ya, dtype=jnp.int32)
-    other_blocks = (ya + shifts) % n_ya
-    other_idx = (other_blocks[:, None] * own_count + own_idx[None, :]).reshape(-1)
-    other_rows = run_search(other_idx, isig, piece, tmpl_all, weights, tables)
-
-    rolled = jnp.concatenate([own_rows, other_rows], 0).reshape(n_ya, own_count, -1)
-    grouped = jnp.roll(rolled, ya, axis=0)
-    got = lax.all_to_all(grouped, "ya", split_axis=0, concat_axis=0, tiled=True)
-    n_xh = lax.axis_size("xh")
-    n_yb = lax.axis_size("yb")
-    got = got.reshape(n_ya, own_count, n_xh, n_yb, -1)
-    rho2 = jnp.transpose(got, (1, 2, 0, 3, 4)).reshape(own_count, -1)
+    blocks = [own_rows] + [shifted(other_rows[k - 1], "ya", n_ya, -k) for k in range(1, n_ya)]
+    blocks = jnp.stack(blocks, 0).reshape(n_ya, own_count, n_g, -1)
+    src_k = (jnp.arange(n_ya, dtype=jnp.int32) - ya) % n_ya
+    src_t = (g - jnp.arange(n_g, dtype=jnp.int32)) % n_g
+    ordered = jnp.take(jnp.take(blocks, src_k, axis=0), src_t, axis=2)
+    ordered = ordered.reshape(n_ya, own_count, n_xh, n_yb, -1)
+    rho2 = jnp.transpose(ordered, (1, 2, 0, 3, 4)).reshape(own_count, -1)
 
     peak = jnp.sqrt(rho2) * flags.astype(jnp.float32)[:, None]
     onehot = assign[:, None] == jnp.arange(BLOCKS, dtype=jnp.int32)[None, :]
@@ -158,15 +169,18 @@
     n_seg, n_tpl = mesh.devices.shape
     n_y = 8
     n_xh = n_tpl // n_y
+    n_sz = 8
+    n_sx = n_seg // (n_sz * 2)
     sub = Mesh(
-        mesh.devices.reshape(n_seg, n_xh, n_y // 2, 2),
-        ("seg", "xh", "ya", "yb"),
+        mesh.devices.reshape(n_sx, n_sz, 2, n_xh, n_y // 2, 2),
+        ("sx", "sz", "sc", "xh", "ya", "yb"),
     )
-    rows = ("seg", "xh", "ya", "yb")
+    seg = ("sx", "sz", "sc")
+    rows = seg + ("xh", "ya", "yb")
     placed = (
         P(rows, None, None, None, None),
         P(("xh", "ya", "yb"), None, None, None),
-        P(None, "seg", None),
+        P(None, seg, None),
         P(rows),
         P(),
     )

time: 132 us -> 122 us (0.924)
  the two profiles are of different devices: /device:TPU:2 before, /device:TPU:64 now
where the time goes in v2:
time: 122 us; the launch traced here: 121 us
  starting transfers between devices  37.9 us (31%)
  blocking collectives  36.9 us (30%)
  Pallas kernels  28.5 us (23%)
  other arithmetic  6.34 us (5%)
  waiting for transfers between devices  5.42 us (4%)
  local copies, waits for them, and re-layouts  5.29 us (4%)
    ppermute x9, starting transfers between devices, shifted(): return lax.ppermute(x, axes, [(i, (i + k) % size) for i in range(size)])  37.9 us
    all_gather x3, blocking collectives, body(): gathered = lax.all_gather(gathered, axis, axis=0, tiled=True)  36.9 us
    pallas_call x2, Pallas kernels, run_search(): pl.pallas_call(functools.partial(search_kernel, n_tb), out_shape=jax.Shap...  28.5 us
    ppermute x9, waiting for transfers between devices, shifted(): return lax.ppermute(x, axes, [(i, (i + k) % size) for i in range(size)])  5.42 us
  transfers between devices with their start and end apart: 9, of which 2 were waited for; matrix products, arithmetic and copies ran while one was open for 5% of the time, Pallas kernels for 7%

profile of v2, /device:TPU:64, one launch (start us, length us, event | category | flops | bytes accessed | tf_op | source)
XLA Modules:
  0.0 121.3 jit_solution(3522680599876376540)
XLA Ops:
  0.6 0.0 copy-start.3
  0.7 3.6 %collective-permute-start = (bf16[4,2,128,128]{3,2,1,0:T(8,128)(2,1)}, bf16[4,2,128,128]{3,2,1,0:T(8,128)(2,1)S(1)}, u32[]{:S(2)}, u32[]{:S(2)}) collective-permute-start(bf16[4,2,128,128]{3,2,1,0:T(8,128)(2,1)} %param.6), channel_id=1, source_target_pairs={{0,1},{1,8},{8,9},{9,0},{2,3},{3,10},{10,11},{11,2},{4,5},{5,12},{... | collective-permute-start | bytes 786440 | tf_op jit(solution)/shard_map/ppermute | solution.py:120
  4.3 4.9 %collective-permute-start.1 = (bf16[4,2,128,128]{3,2,1,0:T(8,128)(2,1)}, bf16[4,2,128,128]{3,2,1,0:T(8,128)(2,1)S(1)}, u32[]{:S(2)}, u32[]{:S(2)}) collective-permute-start(bf16[4,2,128,128]{3,2,1,0:T(8,128)(2,1)} %param.6), channel_id=1, source_target_pairs={{0,8},{1,9},{8,0},{9,1},{2,10},{3,11},{10,2},{11,3},{4,12},{5,13},... | collective-permute-start | bytes 786440 | tf_op jit(solution)/shard_map/ppermute | solution.py:120
  9.2 4.8 %collective-permute-start.2 = (bf16[4,2,128,128]{3,2,1,0:T(8,128)(2,1)}, bf16[4,2,128,128]{3,2,1,0:T(8,128)(2,1)S(1)}, u32[]{:S(2)}, u32[]{:S(2)}) collective-permute-start(bf16[4,2,128,128]{3,2,1,0:T(8,128)(2,1)} %param.6), channel_id=1, source_target_pairs={{0,9},{1,0},{8,1},{9,8},{2,11},{3,2},{10,3},{11,10},{4,13},{5,4},{... | collective-permute-start | bytes 786440 | tf_op jit(solution)/shard_map/ppermute | solution.py:120
  14.0 4.5 %collective-permute-start.3 = (bf16[2,2,2,128,128]{4,3,2,1,0:T(8,128)(2,1)}, bf16[2,2,2,128,128]{4,3,2,1,0:T(8,128)(2,1)S(1)}, u32[]{:S(2)}, u32[]{:S(2)}) collective-permute-start(bf16[2,2,2,128,128]{4,3,2,1,0:T(8,128)(2,1)} %strain_ref.1), channel_id=1, source_target_pairs={{0,2},{2,4},{4,6},{6,0},{1,3},{3,5},{5,7},{7,1},{8,10},{10,12},{12... | collective-permute-start | bytes 786440 | tf_op jit(solution)/shard_map/ppermute | solution.py:120
  18.5 5.9 %collective-permute-start.4 = (bf16[2,2,2,128,128]{4,3,2,1,0:T(8,128)(2,1)}, bf16[2,2,2,128,128]{4,3,2,1,0:T(8,128)(2,1)S(1)}, u32[]{:S(2)}, u32[]{:S(2)}) collective-permute-start(bf16[2,2,2,128,128]{4,3,2,1,0:T(8,128)(2,1)} %strain_ref.1), channel_id=1, source_target_pairs={{0,4},{2,6},{4,0},{6,2},{1,5},{3,7},{5,1},{7,3},{8,12},{10,14},{12... | collective-permute-start | bytes 786440 | tf_op jit(solution)/shard_map/ppermute | solution.py:120
  24.4 1.0 constant_dynamic-update-slice_fusion.3
  25.4 0.3 negate_convert_fusion
  25.7 0.3 fusion.16
  26.0 0.9 fusion.13
  26.9 1.9 %all-gather = f32[2,4,256]{2,1,0:T(4,128)S(1)} all-gather(f32[1,4,256]{2,1,0:T(4,128)} %bitcast.21), channel_id=1, replica_groups=mesh['sx'=2,'sz'=8,'sc'=2,'xh'=2,'ya'=4,'yb'=2] {'sc'}, dimensions={0}, use_global_device_ids=true | all-gather | bytes 12288 | tf_op jit(solution)/shard_map/all_gather | solution.py:134
  28.8 30.0 %all_gather.10 = f32[64,256]{1,0:T(8,128)S(1)} all-gather(f32[8,256]{1,0:T(8,128)S(1)} %reshape.201), channel_id=1, replica_groups=mesh['sx'=2,'sz'=8,'sc'=2,'xh'=2,'ya'=4,'yb'=2] {'sz'}, dimensions={0}, use_global_device_ids=true | all-gather | bytes 73728 | tf_op jit(solution)/shard_map/all_gather | solution.py:134
  58.9 4.9 %all_gather.11 = f32[128,256]{1,0:T(8,128)S(1)} all-gather(f32[64,256]{1,0:T(8,128)S(1)} %all_gather.10), channel_id=1, replica_groups=mesh['sx'=2,'sz'=8,'sc'=2,'xh'=2,'ya'=4,'yb'=2] {'sx'}, dimensions={0}, use_global_device_ids=true | all-gather | bytes 196608 | tf_op jit(solution)/shard_map/all_gather | solution.py:134
  63.9 0.7 fusion.1
  64.7 0.1 copy.21
  64.8 0.1 copy.22
  64.9 0.0 collective-permute-done
  65.0 5.3 %collective-permute-start.5 = (bf16[2,2,2,128,128]{4,3,2,1,0:T(8,128)(2,1)S(1)}, bf16[2,2,2,128,128]{4,3,2,1,0:T(8,128)(2,1)S(1)}, u32[]{:S(2)}, u32[]{:S(2)}) collective-permute-start(bf16[2,2,2,128,128]{4,3,2,1,0:T(8,128)(2,1)S(1)} %copy-done.3), channel_id=1, source_target_pairs={{0,6},{2,0},{4,2},{6,4},{1,7},{3,1},{5,3},{7,5},{8,14},{10,8},{12,... | collective-permute-start | bytes 786440 | tf_op jit(solution)/shard_map/ppermute | solution.py:120
  70.3 0.0 collective-permute-done.1
  70.3 0.0 collective-permute-done.2
  70.4 0.2 add_bitcast_fusion
  70.6 0.8 copy-done
  71.3 0.3 multiply_reduce_fusion
  71.6 0.6 div.58.isig_ref
  72.2 0.5 iota.51.sidx_ref
  72.7 8.1 %shard_map.68 = f32[2,16,128]{2,1,0:T(8,128)} custom-call(s32[2]{0:T(128)} %iota.51.sidx_ref, f32[32]{0:T(128)} %div.58.isig_ref, bf16[2,2,2,128,128]{4,3,2,1,0:T(8,128)(2,1)} %strain_ref.1, bf16[16,2,128,128]{3,2,1,0:T(8,128)(2,1)} %copy-done, f32[2,128,128]{2,1,0:T(8,128)} %bitcast.16, bf16[256,256]{1,0:T(8,128)(2,1)} %get-tuple-element.7.m1_ref, ...), custom_call_target="tpu_custom_call" | custom-call | flops 2147483648 | bytes 1441792 | tf_op jit(solution)/shard_map/pallas_call | solution.py:103
  80.8 0.8 reduce_max.27
  81.6 1.0 pad_maximum_fusion.strain_ref
  82.6 0.5 iota.52.sidx_ref
  83.2 20.4 %shard_map.69 = f32[6,16,128]{2,1,0:T(8,128)} custom-call(s32[6]{0:T(128)} %iota.52.sidx_ref, f32[32]{0:T(128)} %div.58.isig_ref, bf16[6,2,2,128,128]{4,3,2,1,0:T(8,128)(2,1)} %pad_maximum_fusion.strain_ref, bf16[16,2,128,128]{3,2,1,0:T(8,128)(2,1)} %copy-done, f32[2,128,128]{2,1,0:T(8,128)} %bitcast.17, bf16[256,256]{1,0:T(8,128)(2,1)} %get-tuple-element.7.m1_ref, ...), custom_call_target="tpu_custom_call" | custom-call | flops 6442450944 | bytes 1966080 | tf_op jit(solution)/shard_map/pallas_call | solution.py:103
  103.5 0.9 reduce_max.28
  104.4 1.9 %collective-permute-start.6 = (f32[2,16]{1,0:T(2,128)S(1)}, f32[2,16]{1,0:T(2,128)S(1)}, u32[]{:S(2)}, u32[]{:S(2)}) collective-permute-start(f32[2,16]{1,0:T(2,128)S(1)} %get-tuple-element.8), channel_id=1, source_target_pairs={{0,6},{2,0},{4,2},{6,4},{1,7},{3,1},{5,3},{7,5},{8,14},{10,8},{12,... | collective-permute-start | bytes 392 | tf_op jit(solution)/shard_map/ppermute | solution.py:120
  106.4 5.0 %collective-permute-start.7 = (f32[2,16]{1,0:T(2,128)S(1)}, f32[2,16]{1,0:T(2,128)S(1)}, u32[]{:S(2)}, u32[]{:S(2)}) collective-permute-start(f32[2,16]{1,0:T(2,128)S(1)} %get-tuple-element.10), channel_id=1, source_target_pairs={{0,4},{2,6},{4,0},{6,2},{1,5},{3,7},{5,1},{7,3},{8,12},{10,14},{12... | collective-permute-start | bytes 392 | tf_op jit(solution)/shard_map/ppermute | solution.py:120
  111.4 1.9 %collective-permute-start.8 = (f32[2,16]{1,0:T(2,128)S(1)}, f32[2,16]{1,0:T(2,128)S(1)}, u32[]{:S(2)}, u32[]{:S(2)}) collective-permute-start(f32[2,16]{1,0:T(2,128)S(1)} %get-tuple-element.9), channel_id=1, source_target_pairs={{0,2},{2,4},{4,6},{6,0},{1,3},{3,5},{5,7},{7,1},{8,10},{10,12},{12... | collective-permute-start | bytes 392 | tf_op jit(solution)/shard_map/ppermute | solution.py:120
  113.3 0.1 stack.15
  113.4 0.0 collective-permute-done.6
  113.4 0.1 stack.16
  113.5 2.2 %collective-permute-done.7 = f32[2,16]{1,0:T(2,128)S(1)} collective-permute-done((f32[2,16]{1,0:T(2,128)S(1)}, f32[2,16]{1,0:T(2,128)S(1)}, u32[]{:S(2)}, u32[]{:S(2)}) %collective-permute-start.7) | collective-permute-done | bytes 160 | tf_op jit(solution)/shard_map/ppermute | solution.py:120
  115.7 0.1 stack.17
  115.8 3.2 %collective-permute-done.8 = f32[2,16]{1,0:T(2,128)S(1)} collective-permute-done((f32[2,16]{1,0:T(2,128)S(1)}, f32[2,16]{1,0:T(2,128)S(1)}, u32[]{:S(2)}, u32[]{:S(2)}) %collective-permute-start.8) | collective-permute-done | bytes 160 | tf_op jit(solution)/shard_map/ppermute | solution.py:120
  119.0 0.1 stack.18
  119.1 0.6 gather_fusion
  119.7 0.1 broadcast_select_fusion
  119.7 0.6 gather_fusion.1
  120.3 0.1 sqrt_bitcast_fusion
  120.4 0.1 sqrt.15
  120.5 0.1 broadcast_multiply_fusion
  120.6 0.7 select_reduce_fusion
  (32 shorter events, 0.3 us)
Async XLA Ops:
  0.6 64.3 %copy-start.3 = (bf16[2,2,2,128,128]{4,3,2,1,0:T(8,128)(2,1)S(1)}, bf16[2,2,2,128,128]{4,3,2,1,0:T(8,128)(2,1)}, u32[]{:S(2)}) copy-start(bf16[2,2,2,128,128]{4,3,2,1,0:T(8,128)(2,1)} %strain_ref.1) | copy-start | bytes 786436
  0.6 63.3 %copy-start.4 = (s32[64]{0:T(128)S(1)}, s32[64]{0:T(128)}, u32[]{:S(2)}) copy-start(s32[64]{0:T(128)} %param.9) | copy-start | bytes 772
  0.7 64.3 %copy-start.5 = (s32[2]{0:T(128)S(1)}, s32[2]{0:T(128)}, u32[]{:S(2)}) copy-start(s32[2]{0:T(128)} %param.8) | copy-start | bytes 28
  0.7 64.3 %collective-permute-start = (bf16[4,2,128,128]{3,2,1,0:T(8,128)(2,1)}, bf16[4,2,128,128]{3,2,1,0:T(8,128)(2,1)S(1)}, u32[]{:S(2)}, u32[]{:S(2)}) collective-permute-start(bf16[4,2,128,128]{3,2,1,0:T(8,128)(2,1)} %param.6), channel_id=1, source_target_pairs={{0,1},{1,8},{8,9},{9,0},{2,3},{3,10},{10,11},{11,2},{4,5},{5,12},{... | collective-permute-start | bytes 786440 | tf_op jit(solution)/shard_map/ppermute | solution.py:120
  4.3 66.0 %collective-permute-start.1 = (bf16[4,2,128,128]{3,2,1,0:T(8,128)(2,1)}, bf16[4,2,128,128]{3,2,1,0:T(8,128)(2,1)S(1)}, u32[]{:S(2)}, u32[]{:S(2)}) collective-permute-start(bf16[4,2,128,128]{3,2,1,0:T(8,128)(2,1)} %param.6), channel_id=1, source_target_pairs={{0,8},{1,9},{8,0},{9,1},{2,10},{3,11},{10,2},{11,3},{4,12},{5,13},... | collective-permute-start | bytes 786440 | tf_op jit(solution)/shard_map/ppermute | solution.py:120
  9.2 61.1 %collective-permute-start.2 = (bf16[4,2,128,128]{3,2,1,0:T(8,128)(2,1)}, bf16[4,2,128,128]{3,2,1,0:T(8,128)(2,1)S(1)}, u32[]{:S(2)}, u32[]{:S(2)}) collective-permute-start(bf16[4,2,128,128]{3,2,1,0:T(8,128)(2,1)} %param.6), channel_id=1, source_target_pairs={{0,9},{1,0},{8,1},{9,8},{2,11},{3,2},{10,3},{11,10},{4,13},{5,4},{... | collective-permute-start | bytes 786440 | tf_op jit(solution)/shard_map/ppermute | solution.py:120
  14.0 67.6 %collective-permute-start.3 = (bf16[2,2,2,128,128]{4,3,2,1,0:T(8,128)(2,1)}, bf16[2,2,2,128,128]{4,3,2,1,0:T(8,128)(2,1)S(1)}, u32[]{:S(2)}, u32[]{:S(2)}) collective-permute-start(bf16[2,2,2,128,128]{4,3,2,1,0:T(8,128)(2,1)} %strain_ref.1), channel_id=1, source_target_pairs={{0,2},{2,4},{4,6},{6,0},{1,3},{3,5},{5,7},{7,1},{8,10},{10,12},{12... | collective-permute-start | bytes 786440 | tf_op jit(solution)/shard_map/ppermute | solution.py:120
  18.5 63.1 %collective-permute-start.4 = (bf16[2,2,2,128,128]{4,3,2,1,0:T(8,128)(2,1)}, bf16[2,2,2,128,128]{4,3,2,1,0:T(8,128)(2,1)S(1)}, u32[]{:S(2)}, u32[]{:S(2)}) collective-permute-start(bf16[2,2,2,128,128]{4,3,2,1,0:T(8,128)(2,1)} %strain_ref.1), channel_id=1, source_target_pairs={{0,4},{2,6},{4,0},{6,2},{1,5},{3,7},{5,1},{7,3},{8,12},{10,14},{12... | collective-permute-start | bytes 786440 | tf_op jit(solution)/shard_map/ppermute | solution.py:120
  64.9 5.7 %copy-start.1 = (f32[128,2,128]{2,0,1:T(8,128)}, f32[128,2,128]{2,0,1:T(8,128)S(1)}, u32[]{:S(2)}) copy-start(f32[128,2,128]{2,0,1:T(8,128)S(1)} %copy.22) | copy-start | bytes 393220
  65.0 16.7 %collective-permute-start.5 = (bf16[2,2,2,128,128]{4,3,2,1,0:T(8,128)(2,1)S(1)}, bf16[2,2,2,128,128]{4,3,2,1,0:T(8,128)(2,1)S(1)}, u32[]{:S(2)}, u32[]{:S(2)}) collective-permute-start(bf16[2,2,2,128,128]{4,3,2,1,0:T(8,128)(2,1)S(1)} %copy-done.3), channel_id=1, source_target_pairs={{0,6},{2,0},{4,2},{6,4},{1,7},{3,1},{5,3},{7,5},{8,14},{10,8},{12,... | collective-permute-start | bytes 786440 | tf_op jit(solution)/shard_map/ppermute | solution.py:120
  70.4 1.0 copy-start
  104.4 9.0 %collective-permute-start.6 = (f32[2,16]{1,0:T(2,128)S(1)}, f32[2,16]{1,0:T(2,128)S(1)}, u32[]{:S(2)}, u32[]{:S(2)}) collective-permute-start(f32[2,16]{1,0:T(2,128)S(1)} %get-tuple-element.8), channel_id=1, source_target_pairs={{0,6},{2,0},{4,2},{6,4},{1,7},{3,1},{5,3},{7,5},{8,14},{10,8},{12,... | collective-permute-start | bytes 392 | tf_op jit(solution)/shard_map/ppermute | solution.py:120
  106.4 9.4 %collective-permute-start.7 = (f32[2,16]{1,0:T(2,128)S(1)}, f32[2,16]{1,0:T(2,128)S(1)}, u32[]{:S(2)}, u32[]{:S(2)}) collective-permute-start(f32[2,16]{1,0:T(2,128)S(1)} %get-tuple-element.10), channel_id=1, source_target_pairs={{0,4},{2,6},{4,0},{6,2},{1,5},{3,7},{5,1},{7,3},{8,12},{10,14},{12... | collective-permute-start | bytes 392 | tf_op jit(solution)/shard_map/ppermute | solution.py:120
  111.4 7.6 %collective-permute-start.8 = (f32[2,16]{1,0:T(2,128)S(1)}, f32[2,16]{1,0:T(2,128)S(1)}, u32[]{:S(2)}, u32[]{:S(2)}) collective-permute-start(f32[2,16]{1,0:T(2,128)S(1)} %get-tuple-element.9), channel_id=1, source_target_pairs={{0,2},{2,4},{4,6},{6,0},{1,3},{3,5},{5,7},{7,1},{8,10},{10,12},{12... | collective-permute-start | bytes 392 | tf_op jit(solution)/shard_map/ppermute | solution.py:120
  120.6 0.7 copy-start.2

commit v3 on v2

--- a/solution.py
+++ b/solution.py
@@ -116,8 +116,8 @@
     return jnp.max(out, axis=-1)
 
 
-def shifted(x, axes, size, k):
-    return lax.ppermute(x, axes, [(i, (i + k) % size) for i in range(size)])
+def swapped(x, axes, size, k):
+    return lax.ppermute(x, axes, [(i, i ^ k) for i in range(size)])
 
 
 def body(strain, templates, psd, flags, assign):
@@ -132,14 +132,15 @@
     gathered = jnp.transpose(psd, (1, 0, 2)).reshape(rows_here, -1)
     for axis in ("sc", "sz", "sx"):
         gathered = lax.all_gather(gathered, axis, axis=0, tiled=True)
+    gathered, strain, templates = lax.optimization_barrier((gathered, strain, templates))
     full_psd = jnp.transpose(gathered.reshape(-1, 2, N2), (1, 0, 2))
     weights = 1.0 / full_psd
     tables = make_tables()
 
     tmpl_rel = jnp.concatenate(
-        [templates] + [shifted(templates, ("xh", "yb"), n_g, k) for k in range(1, n_g)], 0
+        [templates] + [swapped(templates, ("xh", "yb"), n_g, k) for k in range(1, n_g)], 0
     )
-    piece = jnp.concatenate([shifted(strain, "ya", n_ya, k) for k in range(1, n_ya)], 0)
+    piece = jnp.concatenate([swapped(strain, "ya", n_ya, k) for k in range(1, n_ya)], 0)
     sigma2 = jax.vmap(lambda tmpl: template_norm(tmpl, weights))(tmpl_rel)
     isig = (1.0 / sigma2).reshape(-1)
 
@@ -149,13 +150,17 @@
     own_rows, piece = lax.optimization_barrier((own_rows, piece))
     other_idx = jnp.arange(piece.shape[0], dtype=jnp.int32)
     other_rows = run_search(other_idx, isig, piece, tmpl_rel, weights, tables)
-    other_rows = other_rows.reshape(n_ya - 1, own_count, -1)
+    slots = jnp.concatenate([own_rows, other_rows], 0).reshape(n_ya, own_count, -1)
 
-    blocks = [own_rows] + [shifted(other_rows[k - 1], "ya", n_ya, -k) for k in range(1, n_ya)]
-    blocks = jnp.stack(blocks, 0).reshape(n_ya, own_count, n_g, -1)
-    src_k = (jnp.arange(n_ya, dtype=jnp.int32) - ya) % n_ya
-    src_t = (g - jnp.arange(n_g, dtype=jnp.int32)) % n_g
-    ordered = jnp.take(jnp.take(blocks, src_k, axis=0), src_t, axis=2)
+    got1 = swapped(slots[2:4], "ya", n_ya, 2)
+    got2 = swapped(jnp.stack([slots[1], got1[1]], 0), "ya", n_ya, 1)
+    blocks = jnp.stack([slots[0], got1[0], got2[0], got2[1]], 0)
+    blocks = blocks.reshape(n_ya, own_count, n_g, -1)
+    order = jnp.array([0, 2, 1, 3], dtype=jnp.int32)
+    lanes = jnp.arange(n_ya, dtype=jnp.int32)
+    src_c = jnp.take(order, ya ^ lanes)
+    src_t = g ^ jnp.arange(n_g, dtype=jnp.int32)
+    ordered = jnp.take(jnp.take(blocks, src_c, axis=0), src_t, axis=2)
     ordered = ordered.reshape(n_ya, own_count, n_xh, n_yb, -1)
     rho2 = jnp.transpose(ordered, (1, 2, 0, 3, 4)).reshape(own_count, -1)
 

time: 122 us -> 122 us (level)
  the two profiles are of different devices: /device:TPU:64 before, /device:TPU:8 now
where the time goes in v3:
time: 122 us; the launch traced here: 121 us
  blocking collectives  37.8 us (31%)
  starting transfers between devices  29.9 us (25%)
  Pallas kernels  28.5 us (23%)
  waiting for transfers between devices  11.6 us (10%)
  other arithmetic  6.36 us (5%)
  local copies, waits for them, and re-layouts  5.86 us (5%)
    all_gather x3, blocking collectives, body(): gathered = lax.all_gather(gathered, axis, axis=0, tiled=True)  37.8 us
    ppermute x8, starting transfers between devices, swapped(): return lax.ppermute(x, axes, [(i, i ^ k) for i in range(size)])  29.9 us
    pallas_call x2, Pallas kernels, run_search(): pl.pallas_call(functools.partial(search_kernel, n_tb), out_shape=jax.Shap...  28.5 us
    ppermute x8, waiting for transfers between devices, swapped(): return lax.ppermute(x, axes, [(i, i ^ k) for i in range(size)])  11.6 us
  transfers between devices with their start and end apart: 8, of which 3 were waited for; matrix products, arithmetic and copies ran while one was open for 6% of the time, Pallas kernels for 7%

profile of v3, /device:TPU:8, one launch (start us, length us, event | category | flops | bytes accessed | tf_op | source)
XLA Modules:
  0.0 121.1 jit_solution(15676730691771724834)
XLA Ops:
  0.6 0.0 copy-start
  0.7 2.0 %all-gather = f32[2,4,256]{2,1,0:T(4,128)S(1)} all-gather(f32[1,4,256]{2,1,0:T(4,128)} %bitcast.30), channel_id=1, replica_groups=mesh['sx'=2,'sz'=8,'sc'=2,'xh'=2,'ya'=4,'yb'=2] {'sc'}, dimensions={0}, use_global_device_ids=true | all-gather | bytes 12288 | tf_op jit(solution)/shard_map/all_gather | solution.py:134
  2.6 30.9 %all_gather.10 = f32[64,256]{1,0:T(8,128)S(1)} all-gather(f32[8,256]{1,0:T(8,128)S(1)} %reshape.168), channel_id=1, replica_groups=mesh['sx'=2,'sz'=8,'sc'=2,'xh'=2,'ya'=4,'yb'=2] {'sz'}, dimensions={0}, use_global_device_ids=true | all-gather | bytes 73728 | tf_op jit(solution)/shard_map/all_gather | solution.py:134
  33.6 4.9 %all_gather.11 = f32[128,256]{1,0:T(8,128)S(1)} all-gather(f32[64,256]{1,0:T(8,128)S(1)} %all_gather.10), channel_id=1, replica_groups=mesh['sx'=2,'sz'=8,'sc'=2,'xh'=2,'ya'=4,'yb'=2] {'sx'}, dimensions={0}, use_global_device_ids=true | all-gather | bytes 196608 | tf_op jit(solution)/shard_map/all_gather | solution.py:134
  38.5 2.3 %collective-permute-start = (bf16[4,2,128,128]{3,2,1,0:T(8,128)(2,1)}, bf16[4,2,128,128]{3,2,1,0:T(8,128)(2,1)S(1)}, u32[]{:S(2)}, u32[]{:S(2)}) collective-permute-start(bf16[4,2,128,128]{3,2,1,0:T(8,128)(2,1)} %param.7), channel_id=1, source_target_pairs={{0,1},{1,0},{8,9},{9,8},{2,3},{3,2},{10,11},{11,10},{4,5},{5,4},{1... | collective-permute-start | bytes 786440 | tf_op jit(solution)/shard_map/ppermute | solution.py:120
  40.8 4.9 %collective-permute-start.1 = (bf16[4,2,128,128]{3,2,1,0:T(8,128)(2,1)}, bf16[4,2,128,128]{3,2,1,0:T(8,128)(2,1)S(1)}, u32[]{:S(2)}, u32[]{:S(2)}) collective-permute-start(bf16[4,2,128,128]{3,2,1,0:T(8,128)(2,1)} %param.7), channel_id=1, source_target_pairs={{0,8},{1,9},{8,0},{9,1},{2,10},{3,11},{10,2},{11,3},{4,12},{5,13},... | collective-permute-start | bytes 786440 | tf_op jit(solution)/shard_map/ppermute | solution.py:120
  45.8 3.4 %collective-permute-start.2 = (bf16[4,2,128,128]{3,2,1,0:T(8,128)(2,1)}, bf16[4,2,128,128]{3,2,1,0:T(8,128)(2,1)S(1)}, u32[]{:S(2)}, u32[]{:S(2)}) collective-permute-start(bf16[4,2,128,128]{3,2,1,0:T(8,128)(2,1)} %param.7), channel_id=1, source_target_pairs={{0,9},{1,8},{8,1},{9,0},{2,11},{3,10},{10,3},{11,2},{4,13},{5,12},... | collective-permute-start | bytes 786440 | tf_op jit(solution)/shard_map/ppermute | solution.py:120
  49.2 4.5 %collective-permute-start.3 = (bf16[2,2,2,128,128]{4,3,2,1,0:T(8,128)(2,1)}, bf16[2,2,2,128,128]{4,3,2,1,0:T(8,128)(2,1)S(1)}, u32[]{:S(2)}, u32[]{:S(2)}) collective-permute-start(bf16[2,2,2,128,128]{4,3,2,1,0:T(8,128)(2,1)} %strain_ref), channel_id=1, source_target_pairs={{0,2},{2,0},{4,6},{6,4},{1,3},{3,1},{5,7},{7,5},{8,10},{10,8},{12,... | collective-permute-start | bytes 786440 | tf_op jit(solution)/shard_map/ppermute | solution.py:120
  53.7 5.0 %collective-permute-start.4 = (bf16[2,2,2,128,128]{4,3,2,1,0:T(8,128)(2,1)}, bf16[2,2,2,128,128]{4,3,2,1,0:T(8,128)(2,1)S(1)}, u32[]{:S(2)}, u32[]{:S(2)}) collective-permute-start(bf16[2,2,2,128,128]{4,3,2,1,0:T(8,128)(2,1)} %strain_ref), channel_id=1, source_target_pairs={{0,4},{2,6},{4,0},{6,2},{1,5},{3,7},{5,1},{7,3},{8,12},{10,14},{12... | collective-permute-start | bytes 786440 | tf_op jit(solution)/shard_map/ppermute | solution.py:120
  58.8 1.0 constant_dynamic-update-slice_fusion.3
  59.8 0.0 copy-start.4
  59.8 0.3 negate_convert_fusion
  60.0 0.3 fusion.16
  60.4 0.6 gather_fusion
  61.1 0.8 fusion.1
  61.9 0.9 fusion.13
  62.8 0.1 copy.22
  62.9 0.1 copy.23
  63.0 0.0 collective-permute-done
  63.0 2.7 %collective-permute-start.5 = (bf16[2,2,2,128,128]{4,3,2,1,0:T(8,128)(2,1)S(1)}, bf16[2,2,2,128,128]{4,3,2,1,0:T(8,128)(2,1)S(1)}, u32[]{:S(2)}, u32[]{:S(2)}) collective-permute-start(bf16[2,2,2,128,128]{4,3,2,1,0:T(8,128)(2,1)S(1)} %copy-done.4), channel_id=1, source_target_pairs={{0,6},{2,4},{4,2},{6,0},{1,7},{3,5},{5,3},{7,1},{8,14},{10,12},{12... | collective-permute-start | bytes 786440 | tf_op jit(solution)/shard_map/ppermute | solution.py:120
  65.8 0.0 collective-permute-done.1
  65.8 0.0 collective-permute-done.2
  65.9 0.2 add_bitcast_fusion
  66.1 0.8 copy-done.1
  66.9 0.3 multiply_reduce_fusion
  67.1 0.6 div.58.isig_ref
  67.7 0.5 iota.53.sidx_ref
  68.2 8.1 %shard_map.77 = f32[2,16,128]{2,1,0:T(8,128)} custom-call(s32[2]{0:T(128)} %iota.53.sidx_ref, f32[32]{0:T(128)} %div.58.isig_ref, bf16[2,2,2,128,128]{4,3,2,1,0:T(8,128)(2,1)} %strain_ref, bf16[16,2,128,128]{3,2,1,0:T(8,128)(2,1)} %copy-done.1, f32[2,128,128]{2,1,0:T(8,128)} %bitcast.25, bf16[256,256]{1,0:T(8,128)(2,1)} %get-tuple-element.13.m1_ref, ...), custom_call_target="tpu_custom_call" | custom-call | flops 2147483648 | bytes 1441792 | tf_op jit(solution)/shard_map/pallas_call | solution.py:103
  76.3 0.8 reduce_max.27
  77.1 3.1 %collective-permute-done.5 = bf16[2,2,2,128,128]{4,3,2,1,0:T(8,128)(2,1)S(1)} collective-permute-done((bf16[2,2,2,128,128]{4,3,2,1,0:T(8,128)(2,1)S(1)}, bf16[2,2,2,128,128]{4,3,2,1,0:T(8,128)(2,1)S(1)}, u32[]{:S(2)}, u32[]{:S(2)}) %collective-permute-start.5) | collective-permute-done | bytes 262176 | tf_op jit(solution)/shard_map/ppermute | solution.py:120
  80.2 1.0 pad_maximum_fusion.strain_ref
  81.2 0.5 iota.54.sidx_ref
  81.7 20.4 %shard_map.78 = f32[6,16,128]{2,1,0:T(8,128)} custom-call(s32[6]{0:T(128)} %iota.54.sidx_ref, f32[32]{0:T(128)} %div.58.isig_ref, bf16[6,2,2,128,128]{4,3,2,1,0:T(8,128)(2,1)} %pad_maximum_fusion.strain_ref, bf16[16,2,128,128]{3,2,1,0:T(8,128)(2,1)} %copy-done.1, f32[2,128,128]{2,1,0:T(8,128)} %bitcast.26, bf16[256,256]{1,0:T(8,128)(2,1)} %get-tuple-element.13.m1_ref, ...), custom_call_target="tpu_custom_call" | custom-call | flops 6442450944 | bytes 1966080 | tf_op jit(solution)/shard_map/pallas_call | solution.py:103
  102.1 0.9 reduce_max.28
  103.0 5.1 %collective-permute-start.6 = (f32[2,2,16]{2,1,0:T(2,128)S(1)}, f32[2,2,16]{2,1,0:T(2,128)S(1)}, u32[]{:S(2)}, u32[]{:S(2)}) collective-permute-start(f32[2,2,16]{2,1,0:T(2,128)S(1)} %bitcast.31), channel_id=1, source_target_pairs={{0,4},{2,6},{4,0},{6,2},{1,5},{3,7},{5,1},{7,3},{8,12},{10,14},{12... | collective-permute-start | bytes 776 | tf_op jit(solution)/shard_map/ppermute | solution.py:120
  108.2 4.3 %collective-permute-done.6 = f32[2,2,16]{2,1,0:T(2,128)S(1)} collective-permute-done((f32[2,2,16]{2,1,0:T(2,128)S(1)}, f32[2,2,16]{2,1,0:T(2,128)S(1)}, u32[]{:S(2)}, u32[]{:S(2)}) %collective-permute-start.6) | collective-permute-done | bytes 288 | tf_op jit(solution)/shard_map/ppermute | solution.py:120
  112.4 1.9 %collective-permute-start.7 = (f32[2,2,16]{2,1,0:T(2,128)S(1)}, f32[2,2,16]{2,1,0:T(2,128)S(1)}, u32[]{:S(2)}, u32[]{:S(2)}) collective-permute-start(f32[2,2,16]{2,1,0:T(2,128)S(1)} %pad_maximum_fusion.6), channel_id=1, source_target_pairs={{0,2},{2,0},{4,6},{6,4},{1,3},{3,1},{5,7},{7,5},{8,10},{10,8},{12,... | collective-permute-start | bytes 776 | tf_op jit(solution)/shard_map/ppermute | solution.py:120
  114.4 0.1 stack.13
  114.5 0.1 stack.14
  114.5 4.3 %collective-permute-done.7 = f32[2,2,16]{2,1,0:T(2,128)S(1)} collective-permute-done((f32[2,2,16]{2,1,0:T(2,128)S(1)}, f32[2,2,16]{2,1,0:T(2,128)S(1)}, u32[]{:S(2)}, u32[]{:S(2)}) %collective-permute-start.7) | collective-permute-done | bytes 288 | tf_op jit(solution)/shard_map/ppermute | solution.py:120
  118.8 0.1 stack.16
  118.9 0.6 gather_fusion.1
  119.5 0.1 broadcast_select_fusion
  119.6 0.6 gather_fusion.2
  120.1 0.1 sqrt_bitcast_fusion
  120.2 0.1 sqrt.15
  120.3 0.1 broadcast_multiply_fusion
  120.4 0.7 select_reduce_fusion
  (36 shorter events, 0.3 us)
Async XLA Ops:
  0.6 59.7 %copy-start = (s32[4]{0:T(128)S(1)}, s32[4]{0:T(128)}, u32[]{:S(2)}) copy-start(s32[4]{0:T(128)} %constant.101.clone) | copy-start | bytes 52
  0.6 60.4 %copy-start.5 = (s32[64]{0:T(128)S(1)}, s32[64]{0:T(128)}, u32[]{:S(2)}) copy-start(s32[64]{0:T(128)} %param.10) | copy-start | bytes 772
  38.5 24.5 %collective-permute-start = (bf16[4,2,128,128]{3,2,1,0:T(8,128)(2,1)}, bf16[4,2,128,128]{3,2,1,0:T(8,128)(2,1)S(1)}, u32[]{:S(2)}, u32[]{:S(2)}) collective-permute-start(bf16[4,2,128,128]{3,2,1,0:T(8,128)(2,1)} %param.7), channel_id=1, source_target_pairs={{0,1},{1,0},{8,9},{9,8},{2,3},{3,2},{10,11},{11,10},{4,5},{5,4},{1... | collective-permute-start | bytes 786440 | tf_op jit(solution)/shard_map/ppermute | solution.py:120
  40.8 24.9 %collective-permute-start.1 = (bf16[4,2,128,128]{3,2,1,0:T(8,128)(2,1)}, bf16[4,2,128,128]{3,2,1,0:T(8,128)(2,1)S(1)}, u32[]{:S(2)}, u32[]{:S(2)}) collective-permute-start(bf16[4,2,128,128]{3,2,1,0:T(8,128)(2,1)} %param.7), channel_id=1, source_target_pairs={{0,8},{1,9},{8,0},{9,1},{2,10},{3,11},{10,2},{11,3},{4,12},{5,13},... | collective-permute-start | bytes 786440 | tf_op jit(solution)/shard_map/ppermute | solution.py:120
  45.8 20.1 %collective-permute-start.2 = (bf16[4,2,128,128]{3,2,1,0:T(8,128)(2,1)}, bf16[4,2,128,128]{3,2,1,0:T(8,128)(2,1)S(1)}, u32[]{:S(2)}, u32[]{:S(2)}) collective-permute-start(bf16[4,2,128,128]{3,2,1,0:T(8,128)(2,1)} %param.7), channel_id=1, source_target_pairs={{0,9},{1,8},{8,1},{9,0},{2,11},{3,10},{10,3},{11,2},{4,13},{5,12},... | collective-permute-start | bytes 786440 | tf_op jit(solution)/shard_map/ppermute | solution.py:120
  49.2 27.9 %collective-permute-start.3 = (bf16[2,2,2,128,128]{4,3,2,1,0:T(8,128)(2,1)}, bf16[2,2,2,128,128]{4,3,2,1,0:T(8,128)(2,1)S(1)}, u32[]{:S(2)}, u32[]{:S(2)}) collective-permute-start(bf16[2,2,2,128,128]{4,3,2,1,0:T(8,128)(2,1)} %strain_ref), channel_id=1, source_target_pairs={{0,2},{2,0},{4,6},{6,4},{1,3},{3,1},{5,7},{7,5},{8,10},{10,8},{12,... | collective-permute-start | bytes 786440 | tf_op jit(solution)/shard_map/ppermute | solution.py:120
  53.7 23.4 %collective-permute-start.4 = (bf16[2,2,2,128,128]{4,3,2,1,0:T(8,128)(2,1)}, bf16[2,2,2,128,128]{4,3,2,1,0:T(8,128)(2,1)S(1)}, u32[]{:S(2)}, u32[]{:S(2)}) collective-permute-start(bf16[2,2,2,128,128]{4,3,2,1,0:T(8,128)(2,1)} %strain_ref), channel_id=1, source_target_pairs={{0,4},{2,6},{4,0},{6,2},{1,5},{3,7},{5,1},{7,3},{8,12},{10,14},{12... | collective-permute-start | bytes 786440 | tf_op jit(solution)/shard_map/ppermute | solution.py:120
  59.8 3.3 %copy-start.4 = (bf16[2,2,2,128,128]{4,3,2,1,0:T(8,128)(2,1)S(1)}, bf16[2,2,2,128,128]{4,3,2,1,0:T(8,128)(2,1)}, u32[]{:S(2)}) copy-start(bf16[2,2,2,128,128]{4,3,2,1,0:T(8,128)(2,1)} %strain_ref) | copy-start | bytes 786436
  63.0 3.1 %copy-start.2 = (f32[128,2,128]{2,0,1:T(8,128)}, f32[128,2,128]{2,0,1:T(8,128)S(1)}, u32[]{:S(2)}) copy-start(f32[128,2,128]{2,0,1:T(8,128)S(1)} %copy.23) | copy-start | bytes 393220
  63.0 17.2 %collective-permute-start.5 = (bf16[2,2,2,128,128]{4,3,2,1,0:T(8,128)(2,1)S(1)}, bf16[2,2,2,128,128]{4,3,2,1,0:T(8,128)(2,1)S(1)}, u32[]{:S(2)}, u32[]{:S(2)}) collective-permute-start(bf16[2,2,2,128,128]{4,3,2,1,0:T(8,128)(2,1)S(1)} %copy-done.4), channel_id=1, source_target_pairs={{0,6},{2,4},{4,2},{6,0},{1,7},{3,5},{5,3},{7,1},{8,14},{10,12},{12... | collective-permute-start | bytes 786440 | tf_op jit(solution)/shard_map/ppermute | solution.py:120
  65.9 1.0 copy-start.1
  81.7 32.6 %copy-start.6 = (s32[2]{0:T(128)S(1)}, s32[2]{0:T(128)}, u32[]{:S(2)}) copy-start(s32[2]{0:T(128)} %param.9) | copy-start | bytes 28
  103.0 9.4 %collective-permute-start.6 = (f32[2,2,16]{2,1,0:T(2,128)S(1)}, f32[2,2,16]{2,1,0:T(2,128)S(1)}, u32[]{:S(2)}, u32[]{:S(2)}) collective-permute-start(f32[2,2,16]{2,1,0:T(2,128)S(1)} %bitcast.31), channel_id=1, source_target_pairs={{0,4},{2,6},{4,0},{6,2},{1,5},{3,7},{5,1},{7,3},{8,12},{10,14},{12... | collective-permute-start | bytes 776 | tf_op jit(solution)/shard_map/ppermute | solution.py:120
  112.4 6.4 %collective-permute-start.7 = (f32[2,2,16]{2,1,0:T(2,128)S(1)}, f32[2,2,16]{2,1,0:T(2,128)S(1)}, u32[]{:S(2)}, u32[]{:S(2)}) collective-permute-start(f32[2,2,16]{2,1,0:T(2,128)S(1)} %pad_maximum_fusion.6), channel_id=1, source_target_pairs={{0,2},{2,0},{4,6},{6,4},{1,3},{3,1},{5,7},{7,5},{8,10},{10,8},{12,... | collective-permute-start | bytes 776 | tf_op jit(solution)/shard_map/ppermute | solution.py:120
  120.4 0.7 copy-start.3

commit v4 on v3

--- a/solution.py
+++ b/solution.py
@@ -131,7 +131,18 @@
     rows_here = psd.shape[1]
     gathered = jnp.transpose(psd, (1, 0, 2)).reshape(rows_here, -1)
     for axis in ("sc", "sz", "sx"):
-        gathered = lax.all_gather(gathered, axis, axis=0, tiled=True)
+        size = lax.axis_size(axis)
+        here = lax.axis_index(axis)
+        bit = 1
+        while bit < size:
+            other = swapped(gathered, axis, size, bit)
+            low = (here & bit) == 0
+            gathered = jnp.where(
+                low,
+                jnp.concatenate([gathered, other], 0),
+                jnp.concatenate([other, gathered], 0),
+            )
+            bit *= 2
     gathered, strain, templates = lax.optimization_barrier((gathered, strain, templates))
     full_psd = jnp.transpose(gathered.reshape(-1, 2, N2), (1, 0, 2))
     weights = 1.0 / full_psd

time: 122 us -> 124 us (1.016)
  the two profiles are of different devices: /device:TPU:8 before, /device:TPU:134 now
where the time goes in v4:
time: 124 us
  starting transfers between devices  47.4 us (38%)
  waiting for transfers between devices  32.9 us (27%)
  Pallas kernels  28.5 us (23%)
  other arithmetic  8.07 us (7%)
  local copies, waits for them, and re-layouts  5.66 us (5%)
    ppermute x13, starting transfers between devices, swapped(): return lax.ppermute(x, axes, [(i, i ^ k) for i in range(size)])  47.4 us
    ppermute x13, waiting for transfers between devices, swapped(): return lax.ppermute(x, axes, [(i, i ^ k) for i in range(size)])  32.9 us
    pallas_call x2, Pallas kernels, run_search(): pl.pallas_call(functools.partial(search_kernel, n_tb), out_shape=jax.Shap...  28.5 us
  transfers between devices with their start and end apart: 13, of which 8 were waited for; matrix products, arithmetic and copies ran while one was open for 6% of the time, Pallas kernels for 7%

profile of v4, /device:TPU:134, one launch (start us, length us, event | category | flops | bytes accessed | tf_op | source)
XLA Modules:
  0.0 123.5 jit_solution(779986281876641926)
XLA Ops:
  0.6 1.9 %collective-permute-start = (f32[4,256]{1,0:T(4,128)}, f32[4,256]{1,0:T(4,128)S(1)}, u32[]{:S(2)}, u32[]{:S(2)}) collective-permute-start(f32[4,256]{1,0:T(4,128)} %bitcast.30), channel_id=1, source_target_pairs={{0,16},{16,0},{1,17},{17,1},{2,18},{18,2},{3,19},{19,3},{4,20},{20... | collective-permute-start | bytes 12296 | tf_op jit(solution)/shard_map/ppermute | solution.py:120
  2.6 0.3 negate_convert_fusion
  2.9 1.3 %gather_fusion = s32[4]{0:T(128)S(1)} fusion(s32[4]{0:T(128)} %constant.118.clone, s32[1024]{0:T(1024)S(1)} %get-tuple-element.23), kind=kCustom, calls=%fused_computation | custom fusion | bytes 48 | tf_op jit(solution)/shard_map/jit(_take)/gather | solution.py:172
  4.2 0.7 iota_compare_fusion
  4.9 0.3 fusion.16
  5.2 0.8 maximum_select_fusion.3
  5.9 4.3 %collective-permute-start.1 = (f32[8,256]{1,0:T(8,128)S(1)}, f32[8,256]{1,0:T(8,128)S(1)}, u32[]{:S(2)}, u32[]{:S(2)}) collective-permute-start(f32[8,256]{1,0:T(8,128)S(1)} %maximum_select_fusion.3), channel_id=1, source_target_pairs={{0,32},{32,0},{64,96},{96,64},{128,160},{160,128},{192,224},{224,1... | collective-permute-start | bytes 24584 | tf_op jit(solution)/shard_map/ppermute | solution.py:120
  10.2 0.7 fusion.1
  11.0 0.9 collective-permute-done.1
  11.8 1.9 %collective-permute-start.2 = (f32[16,256]{1,0:T(8,128)S(1)}, f32[16,256]{1,0:T(8,128)S(1)}, u32[]{:S(2)}, u32[]{:S(2)}) collective-permute-start(f32[16,256]{1,0:T(8,128)S(1)} %maximum_select_fusion.2), channel_id=1, source_target_pairs={{0,64},{32,96},{64,0},{96,32},{128,192},{160,224},{192,128},{224,1... | collective-permute-start | bytes 49160 | tf_op jit(solution)/shard_map/ppermute | solution.py:120
  13.8 0.9 fusion.13
  14.7 3.7 %collective-permute-done.2 = f32[16,256]{1,0:T(8,128)S(1)} collective-permute-done((f32[16,256]{1,0:T(8,128)S(1)}, f32[16,256]{1,0:T(8,128)S(1)}, u32[]{:S(2)}, u32[]{:S(2)}) %collective-permute-start.2) | collective-permute-done | bytes 16416 | tf_op jit(solution)/shard_map/ppermute | solution.py:120
  18.4 0.1 copy.24
  18.5 0.1 copy.25
  18.6 8.8 %collective-permute-start.3 = (f32[32,256]{0,1:T(8,128)S(1)}, f32[32,256]{0,1:T(8,128)S(1)}, u32[]{:S(2)}, u32[]{:S(2)}) collective-permute-start(f32[32,256]{0,1:T(8,128)S(1)} %broadcast_select_fusion), channel_id=1, source_target_pairs={{0,128},{32,160},{64,192},{96,224},{128,0},{160,32},{192,64},{224,... | collective-permute-start | bytes 98312 | tf_op jit(solution)/shard_map/ppermute | solution.py:120
  27.4 4.7 %collective-permute-done.3 = f32[32,256]{0,1:T(8,128)S(1)} collective-permute-done((f32[32,256]{0,1:T(8,128)S(1)}, f32[32,256]{0,1:T(8,128)S(1)}, u32[]{:S(2)}, u32[]{:S(2)}) %collective-permute-start.3) | collective-permute-done | bytes 32800 | tf_op jit(solution)/shard_map/ppermute | solution.py:120
  32.1 0.1 maximum_select_fusion
  32.2 2.7 %collective-permute-start.4 = (f32[64,256]{0,1:T(8,128)S(1)}, f32[64,256]{0,1:T(8,128)S(1)}, u32[]{:S(2)}, u32[]{:S(2)}) collective-permute-start(f32[64,256]{0,1:T(8,128)S(1)} %maximum_select_fusion), channel_id=1, source_target_pairs={{0,256},{256,0},{1,257},{257,1},{2,258},{258,2},{3,259},{259,3},{4... | collective-permute-start | bytes 196616 | tf_op jit(solution)/shard_map/ppermute | solution.py:120
  35.0 4.1 %collective-permute-done.4 = f32[64,256]{0,1:T(8,128)S(1)} collective-permute-done((f32[64,256]{0,1:T(8,128)S(1)}, f32[64,256]{0,1:T(8,128)S(1)}, u32[]{:S(2)}, u32[]{:S(2)}) %collective-permute-start.4) | collective-permute-done | bytes 65568 | tf_op jit(solution)/shard_map/ppermute | solution.py:120
  39.1 0.1 maximum_select_fusion.1
  39.2 3.5 %collective-permute-start.5 = (bf16[4,2,128,128]{3,2,1,0:T(8,128)(2,1)S(1)}, bf16[4,2,128,128]{3,2,1,0:T(8,128)(2,1)S(1)}, u32[]{:S(2)}, u32[]{:S(2)}) collective-permute-start(bf16[4,2,128,128]{3,2,1,0:T(8,128)(2,1)S(1)} %copy-done.2), channel_id=1, source_target_pairs={{0,1},{1,0},{8,9},{9,8},{2,3},{3,2},{10,11},{11,10},{4,5},{5,4},{1... | collective-permute-start | bytes 786440 | tf_op jit(solution)/shard_map/ppermute | solution.py:120
  42.8 3.3 %collective-permute-start.6 = (bf16[4,2,128,128]{3,2,1,0:T(8,128)(2,1)S(1)}, bf16[4,2,128,128]{3,2,1,0:T(8,128)(2,1)S(1)}, u32[]{:S(2)}, u32[]{:S(2)}) collective-permute-start(bf16[4,2,128,128]{3,2,1,0:T(8,128)(2,1)S(1)} %copy-done.2), channel_id=1, source_target_pairs={{0,8},{1,9},{8,0},{9,1},{2,10},{3,11},{10,2},{11,3},{4,12},{5,13},... | collective-permute-start | bytes 786440 | tf_op jit(solution)/shard_map/ppermute | solution.py:120
  46.1 3.9 %collective-permute-start.7 = (bf16[4,2,128,128]{3,2,1,0:T(8,128)(2,1)S(1)}, bf16[4,2,128,128]{3,2,1,0:T(8,128)(2,1)S(1)}, u32[]{:S(2)}, u32[]{:S(2)}) collective-permute-start(bf16[4,2,128,128]{3,2,1,0:T(8,128)(2,1)S(1)} %copy-done.2), channel_id=1, source_target_pairs={{0,9},{1,8},{8,1},{9,0},{2,11},{3,10},{10,3},{11,2},{4,13},{5,12},... | collective-permute-start | bytes 786440 | tf_op jit(solution)/shard_map/ppermute | solution.py:120
  50.0 6.2 %collective-permute-start.10 = (bf16[2,2,2,128,128]{4,3,2,1,0:T(8,128)(2,1)S(1)}, bf16[2,2,2,128,128]{4,3,2,1,0:T(8,128)(2,1)S(1)}, u32[]{:S(2)}, u32[]{:S(2)}) collective-permute-start(bf16[2,2,2,128,128]{4,3,2,1,0:T(8,128)(2,1)S(1)} %copy-done.4), channel_id=1, source_target_pairs={{0,6},{2,4},{4,2},{6,0},{1,7},{3,5},{5,3},{7,1},{8,14},{10,12},{12... | collective-permute-start | bytes 786440 | tf_op jit(solution)/shard_map/ppermute | solution.py:120
  56.2 4.0 %collective-permute-start.8 = (bf16[2,2,2,128,128]{4,3,2,1,0:T(8,128)(2,1)S(1)}, bf16[2,2,2,128,128]{4,3,2,1,0:T(8,128)(2,1)S(1)}, u32[]{:S(2)}, u32[]{:S(2)}) collective-permute-start(bf16[2,2,2,128,128]{4,3,2,1,0:T(8,128)(2,1)S(1)} %copy-done.4), channel_id=1, source_target_pairs={{0,2},{2,0},{4,6},{6,4},{1,3},{3,1},{5,7},{7,5},{8,10},{10,8},{12,... | collective-permute-start | bytes 786440 | tf_op jit(solution)/shard_map/ppermute | solution.py:120
  60.3 0.1 copy.26
  60.4 2.1 %collective-permute-start.9 = (bf16[2,2,2,128,128]{4,3,2,1,0:T(8,128)(2,1)S(1)}, bf16[2,2,2,128,128]{4,3,2,1,0:T(8,128)(2,1)S(1)}, u32[]{:S(2)}, u32[]{:S(2)}) collective-permute-start(bf16[2,2,2,128,128]{4,3,2,1,0:T(8,128)(2,1)S(1)} %copy-done.4), channel_id=1, source_target_pairs={{0,4},{2,6},{4,0},{6,2},{1,5},{3,7},{5,1},{7,3},{8,12},{10,14},{12... | collective-permute-start | bytes 786440 | tf_op jit(solution)/shard_map/ppermute | solution.py:120
  62.7 0.2 add_bitcast_fusion
  62.9 0.8 copy-done
  63.7 0.3 multiply_reduce_fusion
  64.0 0.6 div.58.isig_ref
  64.6 0.5 iota.53.sidx_ref
  65.1 8.1 %shard_map.77 = f32[2,16,128]{2,1,0:T(8,128)} custom-call(s32[2]{0:T(128)} %iota.53.sidx_ref, f32[32]{0:T(128)} %div.58.isig_ref, bf16[2,2,2,128,128]{4,3,2,1,0:T(8,128)(2,1)} %strain_ref, bf16[16,2,128,128]{3,2,1,0:T(8,128)(2,1)} %copy-done, f32[2,128,128]{2,1,0:T(8,128)} %bitcast.25, bf16[256,256]{1,0:T(8,128)(2,1)} %get-tuple-element.13.m1_ref, ...), custom_call_target="tpu_custom_call" | custom-call | flops 2147483648 | bytes 1441792 | tf_op jit(solution)/shard_map/pallas_call | solution.py:103
  73.2 0.8 reduce_max.27
  74.0 7.8 %collective-permute-done.8 = bf16[2,2,2,128,128]{4,3,2,1,0:T(8,128)(2,1)S(1)} collective-permute-done((bf16[2,2,2,128,128]{4,3,2,1,0:T(8,128)(2,1)S(1)}, bf16[2,2,2,128,128]{4,3,2,1,0:T(8,128)(2,1)S(1)}, u32[]{:S(2)}, u32[]{:S(2)}) %collective-permute-start.8) | collective-permute-done | bytes 262176 | tf_op jit(solution)/shard_map/ppermute | solution.py:120
  81.8 0.9 collective-permute-done.9
  82.6 1.0 pad_maximum_fusion.strain_ref
  83.7 0.5 iota.54.sidx_ref
  84.2 20.4 %shard_map.78 = f32[6,16,128]{2,1,0:T(8,128)} custom-call(s32[6]{0:T(128)} %iota.54.sidx_ref, f32[32]{0:T(128)} %div.58.isig_ref, bf16[6,2,2,128,128]{4,3,2,1,0:T(8,128)(2,1)} %pad_maximum_fusion.strain_ref, bf16[16,2,128,128]{3,2,1,0:T(8,128)(2,1)} %copy-done, f32[2,128,128]{2,1,0:T(8,128)} %bitcast.26, bf16[256,256]{1,0:T(8,128)(2,1)} %get-tuple-element.13.m1_ref, ...), custom_call_target="tpu_custom_call" | custom-call | flops 6442450944 | bytes 1966080 | tf_op jit(solution)/shard_map/pallas_call | solution.py:103
  104.6 0.9 reduce_max.28
  105.5 2.8 %collective-permute-start.11 = (f32[2,2,16]{2,1,0:T(2,128)S(1)}, f32[2,2,16]{2,1,0:T(2,128)S(1)}, u32[]{:S(2)}, u32[]{:S(2)}) collective-permute-start(f32[2,2,16]{2,1,0:T(2,128)S(1)} %bitcast.32), channel_id=1, source_target_pairs={{0,4},{2,6},{4,0},{6,2},{1,5},{3,7},{5,1},{7,3},{8,12},{10,14},{12... | collective-permute-start | bytes 776 | tf_op jit(solution)/shard_map/ppermute | solution.py:120
  108.3 6.6 %collective-permute-done.11 = f32[2,2,16]{2,1,0:T(2,128)S(1)} collective-permute-done((f32[2,2,16]{2,1,0:T(2,128)S(1)}, f32[2,2,16]{2,1,0:T(2,128)S(1)}, u32[]{:S(2)}, u32[]{:S(2)}) %collective-permute-start.11) | collective-permute-done | bytes 288 | tf_op jit(solution)/shard_map/ppermute | solution.py:120
  114.9 1.9 %collective-permute-start.12 = (f32[2,2,16]{2,1,0:T(2,128)S(1)}, f32[2,2,16]{2,1,0:T(2,128)S(1)}, u32[]{:S(2)}, u32[]{:S(2)}) collective-permute-start(f32[2,2,16]{2,1,0:T(2,128)S(1)} %pad_maximum_fusion.8), channel_id=1, source_target_pairs={{0,2},{2,0},{4,6},{6,4},{1,3},{3,1},{5,7},{7,5},{8,10},{10,8},{12,... | collective-permute-start | bytes 776 | tf_op jit(solution)/shard_map/ppermute | solution.py:120
  117.0 4.3 %collective-permute-done.12 = f32[2,2,16]{2,1,0:T(2,128)S(1)} collective-permute-done((f32[2,2,16]{2,1,0:T(2,128)S(1)}, f32[2,2,16]{2,1,0:T(2,128)S(1)}, u32[]{:S(2)}, u32[]{:S(2)}) %collective-permute-start.12) | collective-permute-done | bytes 288 | tf_op jit(solution)/shard_map/ppermute | solution.py:120
  121.3 0.6 gather_fusion.1
  122.0 0.6 gather_fusion.2
  122.7 0.1 sqrt.15
  122.9 0.7 select_reduce_fusion
  (47 shorter events, 0.8 us)
Async XLA Ops:
  0.6 4.5 %collective-permute-start = (f32[4,256]{1,0:T(4,128)}, f32[4,256]{1,0:T(4,128)S(1)}, u32[]{:S(2)}, u32[]{:S(2)}) collective-permute-start(f32[4,256]{1,0:T(4,128)} %bitcast.30), channel_id=1, source_target_pairs={{0,16},{16,0},{1,17},{17,1},{2,18},{18,2},{3,19},{19,3},{4,20},{20... | collective-permute-start | bytes 12296 | tf_op jit(solution)/shard_map/ppermute | solution.py:120
  5.9 5.9 %collective-permute-start.1 = (f32[8,256]{1,0:T(8,128)S(1)}, f32[8,256]{1,0:T(8,128)S(1)}, u32[]{:S(2)}, u32[]{:S(2)}) collective-permute-start(f32[8,256]{1,0:T(8,128)S(1)} %maximum_select_fusion.3), channel_id=1, source_target_pairs={{0,32},{32,0},{64,96},{96,64},{128,160},{160,128},{192,224},{224,1... | collective-permute-start | bytes 24584 | tf_op jit(solution)/shard_map/ppermute | solution.py:120
  10.2 29.0 %copy-start.2 = (bf16[4,2,128,128]{3,2,1,0:T(8,128)(2,1)S(1)}, bf16[4,2,128,128]{3,2,1,0:T(8,128)(2,1)}, u32[]{:S(2)}) copy-start(bf16[4,2,128,128]{3,2,1,0:T(8,128)(2,1)} %param.7) | copy-start | bytes 786436
  11.8 6.5 %collective-permute-start.2 = (f32[16,256]{1,0:T(8,128)S(1)}, f32[16,256]{1,0:T(8,128)S(1)}, u32[]{:S(2)}, u32[]{:S(2)}) collective-permute-start(f32[16,256]{1,0:T(8,128)S(1)} %maximum_select_fusion.2), channel_id=1, source_target_pairs={{0,64},{32,96},{64,0},{96,32},{128,192},{160,224},{192,128},{224,1... | collective-permute-start | bytes 49160 | tf_op jit(solution)/shard_map/ppermute | solution.py:120
  18.4 31.7 %copy-start.4 = (bf16[2,2,2,128,128]{4,3,2,1,0:T(8,128)(2,1)S(1)}, bf16[2,2,2,128,128]{4,3,2,1,0:T(8,128)(2,1)}, u32[]{:S(2)}) copy-start(bf16[2,2,2,128,128]{4,3,2,1,0:T(8,128)(2,1)} %strain_ref) | copy-start | bytes 786436
  18.6 13.5 %collective-permute-start.3 = (f32[32,256]{0,1:T(8,128)S(1)}, f32[32,256]{0,1:T(8,128)S(1)}, u32[]{:S(2)}, u32[]{:S(2)}) collective-permute-start(f32[32,256]{0,1:T(8,128)S(1)} %broadcast_select_fusion), channel_id=1, source_target_pairs={{0,128},{32,160},{64,192},{96,224},{128,0},{160,32},{192,64},{224,... | collective-permute-start | bytes 98312 | tf_op jit(solution)/shard_map/ppermute | solution.py:120
  32.2 6.9 %collective-permute-start.4 = (f32[64,256]{0,1:T(8,128)S(1)}, f32[64,256]{0,1:T(8,128)S(1)}, u32[]{:S(2)}, u32[]{:S(2)}) collective-permute-start(f32[64,256]{0,1:T(8,128)S(1)} %maximum_select_fusion), channel_id=1, source_target_pairs={{0,256},{256,0},{1,257},{257,1},{2,258},{258,2},{3,259},{259,3},{4... | collective-permute-start | bytes 196616 | tf_op jit(solution)/shard_map/ppermute | solution.py:120
  39.2 21.1 %collective-permute-start.5 = (bf16[4,2,128,128]{3,2,1,0:T(8,128)(2,1)S(1)}, bf16[4,2,128,128]{3,2,1,0:T(8,128)(2,1)S(1)}, u32[]{:S(2)}, u32[]{:S(2)}) collective-permute-start(bf16[4,2,128,128]{3,2,1,0:T(8,128)(2,1)S(1)} %copy-done.2), channel_id=1, source_target_pairs={{0,1},{1,0},{8,9},{9,8},{2,3},{3,2},{10,11},{11,10},{4,5},{5,4},{1... | collective-permute-start | bytes 786440 | tf_op jit(solution)/shard_map/ppermute | solution.py:120
  42.8 19.8 %collective-permute-start.6 = (bf16[4,2,128,128]{3,2,1,0:T(8,128)(2,1)S(1)}, bf16[4,2,128,128]{3,2,1,0:T(8,128)(2,1)S(1)}, u32[]{:S(2)}, u32[]{:S(2)}) collective-permute-start(bf16[4,2,128,128]{3,2,1,0:T(8,128)(2,1)S(1)} %copy-done.2), channel_id=1, source_target_pairs={{0,8},{1,9},{8,0},{9,1},{2,10},{3,11},{10,2},{11,3},{4,12},{5,13},... | collective-permute-start | bytes 786440 | tf_op jit(solution)/shard_map/ppermute | solution.py:120
  46.1 16.6 %collective-permute-start.7 = (bf16[4,2,128,128]{3,2,1,0:T(8,128)(2,1)S(1)}, bf16[4,2,128,128]{3,2,1,0:T(8,128)(2,1)S(1)}, u32[]{:S(2)}, u32[]{:S(2)}) collective-permute-start(bf16[4,2,128,128]{3,2,1,0:T(8,128)(2,1)S(1)} %copy-done.2), channel_id=1, source_target_pairs={{0,9},{1,8},{8,1},{9,0},{2,11},{3,10},{10,3},{11,2},{4,13},{5,12},... | collective-permute-start | bytes 786440 | tf_op jit(solution)/shard_map/ppermute | solution.py:120
  50.0 23.9 %collective-permute-start.10 = (bf16[2,2,2,128,128]{4,3,2,1,0:T(8,128)(2,1)S(1)}, bf16[2,2,2,128,128]{4,3,2,1,0:T(8,128)(2,1)S(1)}, u32[]{:S(2)}, u32[]{:S(2)}) collective-permute-start(bf16[2,2,2,128,128]{4,3,2,1,0:T(8,128)(2,1)S(1)} %copy-done.4), channel_id=1, source_target_pairs={{0,6},{2,4},{4,2},{6,0},{1,7},{3,5},{5,3},{7,1},{8,14},{10,12},{12... | collective-permute-start | bytes 786440 | tf_op jit(solution)/shard_map/ppermute | solution.py:120
  56.2 25.6 %collective-permute-start.8 = (bf16[2,2,2,128,128]{4,3,2,1,0:T(8,128)(2,1)S(1)}, bf16[2,2,2,128,128]{4,3,2,1,0:T(8,128)(2,1)S(1)}, u32[]{:S(2)}, u32[]{:S(2)}) collective-permute-start(bf16[2,2,2,128,128]{4,3,2,1,0:T(8,128)(2,1)S(1)} %copy-done.4), channel_id=1, source_target_pairs={{0,2},{2,0},{4,6},{6,4},{1,3},{3,1},{5,7},{7,5},{8,10},{10,8},{12,... | collective-permute-start | bytes 786440 | tf_op jit(solution)/shard_map/ppermute | solution.py:120
  60.4 3.3 %copy-start.1 = (f32[128,2,128]{2,0,1:T(8,128)}, f32[128,2,128]{2,0,1:T(8,128)S(1)}, u32[]{:S(2)}) copy-start(f32[128,2,128]{2,0,1:T(8,128)S(1)} %copy.26) | copy-start | bytes 393220
  60.4 22.2 %collective-permute-start.9 = (bf16[2,2,2,128,128]{4,3,2,1,0:T(8,128)(2,1)S(1)}, bf16[2,2,2,128,128]{4,3,2,1,0:T(8,128)(2,1)S(1)}, u32[]{:S(2)}, u32[]{:S(2)}) collective-permute-start(bf16[2,2,2,128,128]{4,3,2,1,0:T(8,128)(2,1)S(1)} %copy-done.4), channel_id=1, source_target_pairs={{0,4},{2,6},{4,0},{6,2},{1,5},{3,7},{5,1},{7,3},{8,12},{10,14},{12... | collective-permute-start | bytes 786440 | tf_op jit(solution)/shard_map/ppermute | solution.py:120
  62.7 1.0 copy-start
  84.2 32.6 %copy-start.5 = (s32[2]{0:T(128)S(1)}, s32[2]{0:T(128)}, u32[]{:S(2)}) copy-start(s32[2]{0:T(128)} %param.9) | copy-start | bytes 28
  105.5 9.4 %collective-permute-start.11 = (f32[2,2,16]{2,1,0:T(2,128)S(1)}, f32[2,2,16]{2,1,0:T(2,128)S(1)}, u32[]{:S(2)}, u32[]{:S(2)}) collective-permute-start(f32[2,2,16]{2,1,0:T(2,128)S(1)} %bitcast.32), channel_id=1, source_target_pairs={{0,4},{2,6},{4,0},{6,2},{1,5},{3,7},{5,1},{7,3},{8,12},{10,14},{12... | collective-permute-start | bytes 776 | tf_op jit(solution)/shard_map/ppermute | solution.py:120
  114.9 6.4 %collective-permute-start.12 = (f32[2,2,16]{2,1,0:T(2,128)S(1)}, f32[2,2,16]{2,1,0:T(2,128)S(1)}, u32[]{:S(2)}, u32[]{:S(2)}) collective-permute-start(f32[2,2,16]{2,1,0:T(2,128)S(1)} %pad_maximum_fusion.8), channel_id=1, source_target_pairs={{0,2},{2,0},{4,6},{6,4},{1,3},{3,1},{5,7},{7,5},{8,10},{10,8},{12,... | collective-permute-start | bytes 776 | tf_op jit(solution)/shard_map/ppermute | solution.py:120
  122.9 0.7 copy-start.3

commit v5 on v3

--- a/solution.py
+++ b/solution.py
@@ -43,7 +43,7 @@
                   tc_ref, ts_ref, out_ref, q_ref, y_ref, z_ref):
     nb = 2 * TB
 
-    def step(i, carry):
+    def batch(i, slot):
         s = i // n_tb
         tb = i % n_tb
         seg = sidx_ref[s]
@@ -58,20 +58,20 @@
                 q_re = (d_re * h_re + d_im * h_im) * w
                 q_im = (d_im * h_re - d_re * h_im) * w
                 col = (2 * k + d) * N2
-                q_ref[0:N1, col:col + N2] = q_re.astype(jnp.bfloat16)
-                q_ref[N1:2 * N1, col:col + N2] = q_im.astype(jnp.bfloat16)
-        y_ref[...] = jnp.dot(m1_ref[...], q_ref[...], preferred_element_type=jnp.float32)
+                q_ref[slot, 0:N1, col:col + N2] = q_re.astype(jnp.bfloat16)
+                q_ref[slot, N1:2 * N1, col:col + N2] = q_im.astype(jnp.bfloat16)
+        y_ref[slot] = jnp.dot(m1_ref[...], q_ref[slot], preferred_element_type=jnp.float32)
         tc = tc_ref[...]
         ts = ts_ref[...]
         for b in range(nb):
             col = b * N2
-            y_re = y_ref[0:N1, col:col + N2]
-            y_im = y_ref[N1:2 * N1, col:col + N2]
+            y_re = y_ref[slot, 0:N1, col:col + N2]
+            y_im = y_ref[slot, N1:2 * N1, col:col + N2]
             z_re = y_re * tc - y_im * ts
             z_im = y_re * ts + y_im * tc
-            z_ref[col:col + N2, 0:N2] = z_re.astype(jnp.bfloat16)
-            z_ref[col:col + N2, N2:2 * N2] = z_im.astype(jnp.bfloat16)
-        x = jnp.dot(z_ref[...], m2_ref[...], preferred_element_type=jnp.float32)
+            z_ref[slot, col:col + N2, 0:N2] = z_re.astype(jnp.bfloat16)
+            z_ref[slot, col:col + N2, N2:2 * N2] = z_im.astype(jnp.bfloat16)
+        x = jnp.dot(z_ref[slot], m2_ref[...], preferred_element_type=jnp.float32)
         for k in range(TB):
             t = tb * TB + k
             acc = None
@@ -82,9 +82,13 @@
                 p = (x_re * x_re + x_im * x_im) * isig_ref[2 * t + d]
                 acc = p if acc is None else acc + p
             out_ref[s, pl.ds(t, 1), :] = jnp.max(acc, axis=0, keepdims=True)
+
+    def step(j, carry):
+        batch(2 * j, 0)
+        batch(2 * j + 1, 1)
         return carry
 
-    lax.fori_loop(0, sidx_ref.shape[0] * n_tb, step, 0)
+    lax.fori_loop(0, sidx_ref.shape[0] * n_tb // 2, step, 0)
 
 
 def run_search(sidx, isig, strain, tmpl, weights, tables):
@@ -107,9 +111,9 @@
         + [pl.BlockSpec(memory_space=vmem)] * 7,
         out_specs=pl.BlockSpec(memory_space=vmem),
         scratch_shapes=[
-            pltpu.VMEM((2 * N1, 2 * TB * N2), jnp.bfloat16),
-            pltpu.VMEM((2 * N1, 2 * TB * N2), jnp.float32),
-            pltpu.VMEM((2 * TB * N1, 2 * N2), jnp.bfloat16),
+            pltpu.VMEM((2, 2 * N1, 2 * TB * N2), jnp.bfloat16),
+            pltpu.VMEM((2, 2 * N1, 2 * TB * N2), jnp.float32),
+            pltpu.VMEM((2, 2 * TB * N1, 2 * N2), jnp.bfloat16),
         ],
         cost_estimate=cost,
     )(sidx, isig, strain, tmpl, weights, m1, m2, tc, ts)
@@ -152,15 +156,12 @@
     other_rows = run_search(other_idx, isig, piece, tmpl_rel, weights, tables)
     slots = jnp.concatenate([own_rows, other_rows], 0).reshape(n_ya, own_count, -1)
 
-    got1 = swapped(slots[2:4], "ya", n_ya, 2)
-    got2 = swapped(jnp.stack([slots[1], got1[1]], 0), "ya", n_ya, 1)
-    blocks = jnp.stack([slots[0], got1[0], got2[0], got2[1]], 0)
+    lanes = jnp.arange(n_ya, dtype=jnp.int32)
+    grouped = jnp.take(slots, ya ^ lanes, axis=0)
+    blocks = lax.all_to_all(grouped, "ya", split_axis=0, concat_axis=0, tiled=True)
     blocks = blocks.reshape(n_ya, own_count, n_g, -1)
-    order = jnp.array([0, 2, 1, 3], dtype=jnp.int32)
-    lanes = jnp.arange(n_ya, dtype=jnp.int32)
-    src_c = jnp.take(order, ya ^ lanes)
     src_t = g ^ jnp.arange(n_g, dtype=jnp.int32)
-    ordered = jnp.take(jnp.take(blocks, src_c, axis=0), src_t, axis=2)
+    ordered = jnp.take(blocks, src_t, axis=2)
     ordered = ordered.reshape(n_ya, own_count, n_xh, n_yb, -1)
     rho2 = jnp.transpose(ordered, (1, 2, 0, 3, 4)).reshape(own_count, -1)
 

time: 122 us -> 118 us (0.967)
  starting transfers between devices: 29.9 us -> 27.4 us
    all_to_all x0 -> x1, waiting for transfers between devices: none -> 7.68 us  [body(): lax.all_to_all(grouped, 'ya', split_axis=0, concat_axis=0, tiled=True)]
    ppermute x8 -> x6, waiting for transfers between devices: 11.6 us -> 4.04 us  [swapped(): return lax.ppermute(x, axes, [(i, i ^ k) for i in range(size)])]
    ppermute x8 -> x6, starting transfers between devices: 29.9 us -> 22.9 us  [swapped(): return lax.ppermute(x, axes, [(i, i ^ k) for i in range(size)])]
    all_to_all x0 -> x1, starting transfers between devices: none -> 4.46 us  [body(): lax.all_to_all(grouped, 'ya', split_axis=0, concat_axis=0, tiled=True)]
  transfers between devices with their start and end apart: 8 -> 7, of which waited for: 3 -> 2; matrix products, arithmetic and copies ran while one was open for 6% -> 5% of each run, Pallas kernels for 7% -> 7%
where the time goes in v5:
time: 118 us; the launch traced here: 117 us
  blocking collectives  38 us (32%)
  Pallas kernels  27.5 us (23%)
  starting transfers between devices  27.4 us (23%)
  waiting for transfers between devices  11.7 us (10%)
  other arithmetic  6.91 us (6%)
  local copies, waits for them, and re-layouts  5.06 us (4%)
    all_gather x3, blocking collectives, body(): gathered = lax.all_gather(gathered, axis, axis=0, tiled=True)  38 us
    pallas_call x2, Pallas kernels, run_search(): pl.pallas_call(functools.partial(search_kernel, n_tb), out_shape=jax.Shap...  27.5 us
    ppermute x6, starting transfers between devices, swapped(): return lax.ppermute(x, axes, [(i, i ^ k) for i in range(size)])  22.9 us
    all_to_all x1, waiting for transfers between devices, body(): lax.all_to_all(grouped, 'ya', split_axis=0, concat_axis=0, tiled=True)  7.68 us
    all_to_all x1, starting transfers between devices, body(): lax.all_to_all(grouped, 'ya', split_axis=0, concat_axis=0, tiled=True)  4.46 us
    ppermute x6, waiting for transfers between devices, swapped(): return lax.ppermute(x, axes, [(i, i ^ k) for i in range(size)])  4.04 us
  transfers between devices with their start and end apart: 7, of which 2 were waited for; matrix products, arithmetic and copies ran while one was open for 5% of the time, Pallas kernels for 7%

profile of v5, /device:TPU:8, one launch (start us, length us, event | category | flops | bytes accessed | tf_op | source)
XLA Modules:
  0.0 117.5 jit_solution(4762130544416215499)
XLA Ops:
  0.6 0.0 copy-start.4
  0.6 2.0 %all-gather = f32[2,4,256]{2,1,0:T(4,128)S(1)} all-gather(f32[1,4,256]{2,1,0:T(4,128)} %bitcast.23), channel_id=1, replica_groups=mesh['sx'=2,'sz'=8,'sc'=2,'xh'=2,'ya'=4,'yb'=2] {'sc'}, dimensions={0}, use_global_device_ids=true | all-gather | bytes 12288 | tf_op jit(solution)/shard_map/all_gather | solution.py:138
  2.6 30.9 %all_gather.10 = f32[64,256]{1,0:T(8,128)S(1)} all-gather(f32[8,256]{1,0:T(8,128)S(1)} %reshape.127), channel_id=1, replica_groups=mesh['sx'=2,'sz'=8,'sc'=2,'xh'=2,'ya'=4,'yb'=2] {'sz'}, dimensions={0}, use_global_device_ids=true | all-gather | bytes 73728 | tf_op jit(solution)/shard_map/all_gather | solution.py:138
  33.6 5.1 %all_gather.11 = f32[128,256]{1,0:T(8,128)S(1)} all-gather(f32[64,256]{1,0:T(8,128)S(1)} %all_gather.10), channel_id=1, replica_groups=mesh['sx'=2,'sz'=8,'sc'=2,'xh'=2,'ya'=4,'yb'=2] {'sx'}, dimensions={0}, use_global_device_ids=true | all-gather | bytes 196608 | tf_op jit(solution)/shard_map/all_gather | solution.py:138
  38.6 2.3 %collective-permute-start = (bf16[4,2,128,128]{3,2,1,0:T(8,128)(2,1)}, bf16[4,2,128,128]{3,2,1,0:T(8,128)(2,1)S(1)}, u32[]{:S(2)}, u32[]{:S(2)}) collective-permute-start(bf16[4,2,128,128]{3,2,1,0:T(8,128)(2,1)} %param.6), channel_id=1, source_target_pairs={{0,1},{1,0},{8,9},{9,8},{2,3},{3,2},{10,11},{11,10},{4,5},{5,4},{1... | collective-permute-start | bytes 786440 | tf_op jit(solution)/shard_map/ppermute | solution.py:124
  41.0 4.9 %collective-permute-start.1 = (bf16[4,2,128,128]{3,2,1,0:T(8,128)(2,1)}, bf16[4,2,128,128]{3,2,1,0:T(8,128)(2,1)S(1)}, u32[]{:S(2)}, u32[]{:S(2)}) collective-permute-start(bf16[4,2,128,128]{3,2,1,0:T(8,128)(2,1)} %param.6), channel_id=1, source_target_pairs={{0,8},{1,9},{8,0},{9,1},{2,10},{3,11},{10,2},{11,3},{4,12},{5,13},... | collective-permute-start | bytes 786440 | tf_op jit(solution)/shard_map/ppermute | solution.py:124
  45.9 3.4 %collective-permute-start.2 = (bf16[4,2,128,128]{3,2,1,0:T(8,128)(2,1)}, bf16[4,2,128,128]{3,2,1,0:T(8,128)(2,1)S(1)}, u32[]{:S(2)}, u32[]{:S(2)}) collective-permute-start(bf16[4,2,128,128]{3,2,1,0:T(8,128)(2,1)} %param.6), channel_id=1, source_target_pairs={{0,9},{1,8},{8,1},{9,0},{2,11},{3,10},{10,3},{11,2},{4,13},{5,12},... | collective-permute-start | bytes 786440 | tf_op jit(solution)/shard_map/ppermute | solution.py:124
  49.3 4.5 %collective-permute-start.3 = (bf16[2,2,2,128,128]{4,3,2,1,0:T(8,128)(2,1)}, bf16[2,2,2,128,128]{4,3,2,1,0:T(8,128)(2,1)S(1)}, u32[]{:S(2)}, u32[]{:S(2)}) collective-permute-start(bf16[2,2,2,128,128]{4,3,2,1,0:T(8,128)(2,1)} %strain_ref), channel_id=1, source_target_pairs={{0,2},{2,0},{4,6},{6,4},{1,3},{3,1},{5,7},{7,5},{8,10},{10,8},{12,... | collective-permute-start | bytes 786440 | tf_op jit(solution)/shard_map/ppermute | solution.py:124
  53.9 5.0 %collective-permute-start.4 = (bf16[2,2,2,128,128]{4,3,2,1,0:T(8,128)(2,1)}, bf16[2,2,2,128,128]{4,3,2,1,0:T(8,128)(2,1)S(1)}, u32[]{:S(2)}, u32[]{:S(2)}) collective-permute-start(bf16[2,2,2,128,128]{4,3,2,1,0:T(8,128)(2,1)} %strain_ref), channel_id=1, source_target_pairs={{0,4},{2,6},{4,0},{6,2},{1,5},{3,7},{5,1},{7,3},{8,12},{10,14},{12... | collective-permute-start | bytes 786440 | tf_op jit(solution)/shard_map/ppermute | solution.py:124
  58.9 1.0 constant_dynamic-update-slice_fusion.3
  59.9 0.3 negate_convert_fusion
  60.2 0.3 fusion.16
  60.4 0.9 fusion.13
  61.4 0.0 copy-done.4
  61.4 0.7 fusion.1
  62.2 0.1 copy.22
  62.3 0.1 copy.23
  62.4 0.0 copy-start.1
  62.4 0.0 collective-permute-done
  62.4 0.0 copy-done.3
  62.4 2.7 %collective-permute-start.5 = (bf16[2,2,2,128,128]{4,3,2,1,0:T(8,128)(2,1)S(1)}, bf16[2,2,2,128,128]{4,3,2,1,0:T(8,128)(2,1)S(1)}, u32[]{:S(2)}, u32[]{:S(2)}) collective-permute-start(bf16[2,2,2,128,128]{4,3,2,1,0:T(8,128)(2,1)S(1)} %copy-done.3), channel_id=1, source_target_pairs={{0,6},{2,4},{4,2},{6,0},{1,7},{3,5},{5,3},{7,1},{8,14},{10,12},{12... | collective-permute-start | bytes 786440 | tf_op jit(solution)/shard_map/ppermute | solution.py:124
  65.2 0.0 collective-permute-done.1
  65.2 0.0 collective-permute-done.2
  65.3 0.2 add_bitcast_fusion
  65.5 0.8 copy-done
  66.3 0.0 copy-done.1
  66.3 0.3 multiply_reduce_fusion
  66.5 0.6 div.58.isig_ref
  67.1 0.5 iota.51.sidx_ref
  67.7 7.8 %shard_map.68 = f32[2,16,128]{2,1,0:T(8,128)} custom-call(s32[2]{0:T(128)} %iota.51.sidx_ref, f32[32]{0:T(128)} %div.58.isig_ref, bf16[2,2,2,128,128]{4,3,2,1,0:T(8,128)(2,1)} %strain_ref, bf16[16,2,128,128]{3,2,1,0:T(8,128)(2,1)} %copy-done, f32[2,128,128]{2,1,0:T(8,128)} %bitcast.17, bf16[256,256]{1,0:T(8,128)(2,1)} %get-tuple-element.13.m1_ref, ...), custom_call_target="tpu_custom_call" | custom-call | flops 2147483648 | bytes 1441792 | tf_op jit(solution)/shard_map/pallas_call | solution.py:107
  75.5 0.8 reduce_max.27
  76.3 0.0 collective-permute-done.3
  76.3 0.0 collective-permute-done.4
  76.3 4.0 %collective-permute-done.5 = bf16[2,2,2,128,128]{4,3,2,1,0:T(8,128)(2,1)S(1)} collective-permute-done((bf16[2,2,2,128,128]{4,3,2,1,0:T(8,128)(2,1)S(1)}, bf16[2,2,2,128,128]{4,3,2,1,0:T(8,128)(2,1)S(1)}, u32[]{:S(2)}, u32[]{:S(2)}) %collective-permute-start.5) | collective-permute-done | bytes 262176 | tf_op jit(solution)/shard_map/ppermute | solution.py:124
  80.3 1.0 pad_maximum_fusion.strain_ref
  81.3 0.5 iota.52.sidx_ref
  81.9 19.7 %shard_map.69 = f32[6,16,128]{2,1,0:T(8,128)} custom-call(s32[6]{0:T(128)} %iota.52.sidx_ref, f32[32]{0:T(128)} %div.58.isig_ref, bf16[6,2,2,128,128]{4,3,2,1,0:T(8,128)(2,1)} %pad_maximum_fusion.strain_ref, bf16[16,2,128,128]{3,2,1,0:T(8,128)(2,1)} %copy-done, f32[2,128,128]{2,1,0:T(8,128)} %bitcast.18, bf16[256,256]{1,0:T(8,128)(2,1)} %get-tuple-element.13.m1_ref, ...), custom_call_target="tpu_custom_call" | custom-call | flops 6442450944 | bytes 1966080 | tf_op jit(solution)/shard_map/pallas_call | solution.py:107
  101.5 0.9 reduce_max.28
  102.4 0.6 gather_fusion
  103.0 0.7 broadcast_select_fusion
  103.7 4.5 %all-to-all-start = ((f32[4,2,16]{2,1,0:T(2,128)}), f32[4,2,16]{2,1,0:T(2,128)S(1)}, u32[]{:S(2)}, u32[]{:S(2)}) async-start(f32[4,2,16]{2,1,0:T(2,128)} %broadcast_select_fusion), calls=%async_computation | async-start | bytes 8192 | tf_op jit(solution)/shard_map/all_to_all | solution.py:161
  108.2 7.7 %all-to-all-done = f32[4,2,16]{2,1,0:T(2,128)S(1)} async-done(((f32[4,2,16]{2,1,0:T(2,128)}), f32[4,2,16]{2,1,0:T(2,128)S(1)}, u32[]{:S(2)}, u32[]{:S(2)}) %all-to-all-start) | async-done | bytes 544 | tf_op jit(solution)/shard_map/all_to_all | solution.py:161
  115.9 0.1 reshape.109
  115.9 0.6 gather_fusion.1
  116.5 0.1 sqrt_bitcast_fusion
  116.6 0.1 sqrt.15
  116.7 0.1 broadcast_multiply_fusion
  116.8 0.7 select_reduce_fusion
  (24 shorter events, 0.3 us)
Async XLA Ops:
  0.6 60.8 %copy-start.4 = (s32[64]{0:T(128)S(1)}, s32[64]{0:T(128)}, u32[]{:S(2)}) copy-start(s32[64]{0:T(128)} %param.9) | copy-start | bytes 772
  33.6 28.9 %copy-start.3 = (bf16[2,2,2,128,128]{4,3,2,1,0:T(8,128)(2,1)S(1)}, bf16[2,2,2,128,128]{4,3,2,1,0:T(8,128)(2,1)}, u32[]{:S(2)}) copy-start(bf16[2,2,2,128,128]{4,3,2,1,0:T(8,128)(2,1)} %strain_ref) | copy-start | bytes 786436
  38.6 23.8 %collective-permute-start = (bf16[4,2,128,128]{3,2,1,0:T(8,128)(2,1)}, bf16[4,2,128,128]{3,2,1,0:T(8,128)(2,1)S(1)}, u32[]{:S(2)}, u32[]{:S(2)}) collective-permute-start(bf16[4,2,128,128]{3,2,1,0:T(8,128)(2,1)} %param.6), channel_id=1, source_target_pairs={{0,1},{1,0},{8,9},{9,8},{2,3},{3,2},{10,11},{11,10},{4,5},{5,4},{1... | collective-permute-start | bytes 786440 | tf_op jit(solution)/shard_map/ppermute | solution.py:124
  41.0 24.2 %collective-permute-start.1 = (bf16[4,2,128,128]{3,2,1,0:T(8,128)(2,1)}, bf16[4,2,128,128]{3,2,1,0:T(8,128)(2,1)S(1)}, u32[]{:S(2)}, u32[]{:S(2)}) collective-permute-start(bf16[4,2,128,128]{3,2,1,0:T(8,128)(2,1)} %param.6), channel_id=1, source_target_pairs={{0,8},{1,9},{8,0},{9,1},{2,10},{3,11},{10,2},{11,3},{4,12},{5,13},... | collective-permute-start | bytes 786440 | tf_op jit(solution)/shard_map/ppermute | solution.py:124
  45.9 19.3 %collective-permute-start.2 = (bf16[4,2,128,128]{3,2,1,0:T(8,128)(2,1)}, bf16[4,2,128,128]{3,2,1,0:T(8,128)(2,1)S(1)}, u32[]{:S(2)}, u32[]{:S(2)}) collective-permute-start(bf16[4,2,128,128]{3,2,1,0:T(8,128)(2,1)} %param.6), channel_id=1, source_target_pairs={{0,9},{1,8},{8,1},{9,0},{2,11},{3,10},{10,3},{11,2},{4,13},{5,12},... | collective-permute-start | bytes 786440 | tf_op jit(solution)/shard_map/ppermute | solution.py:124
  49.3 27.0 %collective-permute-start.3 = (bf16[2,2,2,128,128]{4,3,2,1,0:T(8,128)(2,1)}, bf16[2,2,2,128,128]{4,3,2,1,0:T(8,128)(2,1)S(1)}, u32[]{:S(2)}, u32[]{:S(2)}) collective-permute-start(bf16[2,2,2,128,128]{4,3,2,1,0:T(8,128)(2,1)} %strain_ref), channel_id=1, source_target_pairs={{0,2},{2,0},{4,6},{6,4},{1,3},{3,1},{5,7},{7,5},{8,10},{10,8},{12,... | collective-permute-start | bytes 786440 | tf_op jit(solution)/shard_map/ppermute | solution.py:124
  53.9 22.5 %collective-permute-start.4 = (bf16[2,2,2,128,128]{4,3,2,1,0:T(8,128)(2,1)}, bf16[2,2,2,128,128]{4,3,2,1,0:T(8,128)(2,1)S(1)}, u32[]{:S(2)}, u32[]{:S(2)}) collective-permute-start(bf16[2,2,2,128,128]{4,3,2,1,0:T(8,128)(2,1)} %strain_ref), channel_id=1, source_target_pairs={{0,4},{2,6},{4,0},{6,2},{1,5},{3,7},{5,1},{7,3},{8,12},{10,14},{12... | collective-permute-start | bytes 786440 | tf_op jit(solution)/shard_map/ppermute | solution.py:124
  62.4 3.9 %copy-start.1 = (f32[128,2,128]{2,0,1:T(8,128)}, f32[128,2,128]{2,0,1:T(8,128)S(1)}, u32[]{:S(2)}) copy-start(f32[128,2,128]{2,0,1:T(8,128)S(1)} %copy.23) | copy-start | bytes 393220
  62.4 17.9 %collective-permute-start.5 = (bf16[2,2,2,128,128]{4,3,2,1,0:T(8,128)(2,1)S(1)}, bf16[2,2,2,128,128]{4,3,2,1,0:T(8,128)(2,1)S(1)}, u32[]{:S(2)}, u32[]{:S(2)}) collective-permute-start(bf16[2,2,2,128,128]{4,3,2,1,0:T(8,128)(2,1)S(1)} %copy-done.3), channel_id=1, source_target_pairs={{0,6},{2,4},{4,2},{6,0},{1,7},{3,5},{5,3},{7,1},{8,14},{10,12},{12... | collective-permute-start | bytes 786440 | tf_op jit(solution)/shard_map/ppermute | solution.py:124
  65.3 1.0 copy-start
  81.9 26.3 %copy-start.5 = (s32[2]{0:T(128)S(1)}, s32[2]{0:T(128)}, u32[]{:S(2)}) copy-start(s32[2]{0:T(128)} %param.8) | copy-start | bytes 28
  103.7 12.2 %all-to-all-start = ((f32[4,2,16]{2,1,0:T(2,128)}), f32[4,2,16]{2,1,0:T(2,128)S(1)}, u32[]{:S(2)}, u32[]{:S(2)}) async-start(f32[4,2,16]{2,1,0:T(2,128)} %broadcast_select_fusion), calls=%async_computation | async-start | bytes 8192 | tf_op jit(solution)/shard_map/all_to_all | solution.py:161
  116.8 0.7 copy-start.2

commit v6 on v5

--- a/solution.py
+++ b/solution.py
@@ -40,23 +40,32 @@
 
 
 def search_kernel(n_tb, sidx_ref, isig_ref, strain_ref, tmpl_ref, w_ref, m1_ref, m2_ref,
-                  tc_ref, ts_ref, out_ref, q_ref, y_ref, z_ref):
+                  tc_ref, ts_ref, out_ref, q_ref, y_ref, z_ref, hw_ref, sd_ref):
     nb = 2 * TB
+
+    def weigh(t, carry):
+        h_re = tmpl_ref[t, 0].astype(jnp.float32)
+        h_im = tmpl_ref[t, 1].astype(jnp.float32)
+        for d in range(2):
+            w = w_ref[d]
+            hw_ref[t, d, 0] = h_re * w
+            hw_ref[t, d, 1] = h_im * w
+        return carry
+
+    lax.fori_loop(0, tmpl_ref.shape[0], weigh, 0)
 
     def batch(i, slot):
         s = i // n_tb
         tb = i % n_tb
-        seg = sidx_ref[s]
         for k in range(TB):
             t = tb * TB + k
-            h_re = tmpl_ref[t, 0].astype(jnp.float32)
-            h_im = tmpl_ref[t, 1].astype(jnp.float32)
             for d in range(2):
-                d_re = strain_ref[seg, d, 0].astype(jnp.float32)
-                d_im = strain_ref[seg, d, 1].astype(jnp.float32)
-                w = w_ref[d]
-                q_re = (d_re * h_re + d_im * h_im) * w
-                q_im = (d_im * h_re - d_re * h_im) * w
+                d_re = sd_ref[d, 0]
+                d_im = sd_ref[d, 1]
+                hw_re = hw_ref[t, d, 0]
+                hw_im = hw_ref[t, d, 1]
+                q_re = d_re * hw_re + d_im * hw_im
+                q_im = d_im * hw_re - d_re * hw_im
                 col = (2 * k + d) * N2
                 q_ref[slot, 0:N1, col:col + N2] = q_re.astype(jnp.bfloat16)
                 q_ref[slot, N1:2 * N1, col:col + N2] = q_im.astype(jnp.bfloat16)
@@ -84,8 +93,17 @@
             out_ref[s, pl.ds(t, 1), :] = jnp.max(acc, axis=0, keepdims=True)
 
     def step(j, carry):
-        batch(2 * j, 0)
-        batch(2 * j + 1, 1)
+        i = 2 * j
+
+        @pl.when(i % n_tb == 0)
+        def _():
+            seg = sidx_ref[i // n_tb]
+            for d in range(2):
+                for part in range(2):
+                    sd_ref[d, part] = strain_ref[seg, d, part].astype(jnp.float32)
+
+        batch(i, 0)
+        batch(i + 1, 1)
         return carry
 
     lax.fori_loop(0, sidx_ref.shape[0] * n_tb // 2, step, 0)
@@ -114,6 +132,8 @@
             pltpu.VMEM((2, 2 * N1, 2 * TB * N2), jnp.bfloat16),
             pltpu.VMEM((2, 2 * N1, 2 * TB * N2), jnp.float32),
             pltpu.VMEM((2, 2 * TB * N1, 2 * N2), jnp.bfloat16),
+            pltpu.VMEM((n_t, 2, 2, N1, N2), jnp.float32),
+            pltpu.VMEM((2, 2, N1, N2), jnp.float32),
         ],
         cost_estimate=cost,
     )(sidx, isig, strain, tmpl, weights, m1, m2, tc, ts)
@@ -134,7 +154,7 @@
 
     rows_here = psd.shape[1]
     gathered = jnp.transpose(psd, (1, 0, 2)).reshape(rows_here, -1)
-    for axis in ("sc", "sz", "sx"):
+    for axis in ("sc", "zl", "zh", "sx"):
         gathered = lax.all_gather(gathered, axis, axis=0, tiled=True)
     gathered, strain, templates = lax.optimization_barrier((gathered, strain, templates))
     full_psd = jnp.transpose(gathered.reshape(-1, 2, N2), (1, 0, 2))
@@ -175,13 +195,14 @@
     n_seg, n_tpl = mesh.devices.shape
     n_y = 8
     n_xh = n_tpl // n_y
-    n_sz = 8
-    n_sx = n_seg // (n_sz * 2)
+    n_zl = 4
+    n_zh = 2
+    n_sx = n_seg // (n_zh * n_zl * 2)
     sub = Mesh(
-        mesh.devices.reshape(n_sx, n_sz, 2, n_xh, n_y // 2, 2),
-        ("sx", "sz", "sc", "xh", "ya", "yb"),
-    )
-    seg = ("sx", "sz", "sc")
+        mesh.devices.reshape(n_sx, n_zh, n_zl, 2, n_xh, n_y // 2, 2),
+        ("sx", "zh", "zl", "sc", "xh", "ya", "yb"),
+    )
+    seg = ("sx", "zh", "zl", "sc")
     rows = seg + ("xh", "ya", "yb")
     placed = (
         P(rows, None, None, None, None),

time: 118 us -> 112 us (0.949)
  blocking collectives: 38 us -> 31.9 us
  Pallas kernels: 27.5 us -> 25.5 us
  waiting for transfers between devices: 11.7 us -> 13.1 us
    all_gather x3 -> x4, blocking collectives: 38 us -> 31.9 us  [body(): gathered = lax.all_gather(gathered, axis, axis=0, tiled=True)]
    pallas_call x2, Pallas kernels: 27.5 us -> 25.5 us  [run_search(): pl.pallas_call(functools.partial(search_kernel, n_tb), out_shape=jax.Shap...]
    ppermute x6, waiting for transfers between devices: 4.04 us -> 5.45 us  [swapped(): return lax.ppermute(x, axes, [(i, i ^ k) for i in range(size)])]
  transfers between devices with their start and end apart: 7 -> 7, of which waited for: 2 -> 3; matrix products, arithmetic and copies ran while one was open for 5% -> 5% of each run, Pallas kernels for 7% -> 7%
where the time goes in v6:
time: 112 us; the launch traced here: 111 us
  blocking collectives  31.9 us (28%)
  starting transfers between devices  27.6 us (25%)
  Pallas kernels  25.5 us (23%)
  waiting for transfers between devices  13.1 us (12%)
  other arithmetic  6.91 us (6%)
  local copies, waits for them, and re-layouts  5.04 us (4%)
    all_gather x4, blocking collectives, body(): gathered = lax.all_gather(gathered, axis, axis=0, tiled=True)  31.9 us
    pallas_call x2, Pallas kernels, run_search(): pl.pallas_call(functools.partial(search_kernel, n_tb), out_shape=jax.Shap...  25.5 us
    ppermute x6, starting transfers between devices, swapped(): return lax.ppermute(x, axes, [(i, i ^ k) for i in range(size)])  23.4 us
    all_to_all x1, waiting for transfers between devices, body(): lax.all_to_all(grouped, 'ya', split_axis=0, concat_axis=0, tiled=True)  7.68 us
    ppermute x6, waiting for transfers between devices, swapped(): return lax.ppermute(x, axes, [(i, i ^ k) for i in range(size)])  5.45 us
    all_to_all x1, starting transfers between devices, body(): lax.all_to_all(grouped, 'ya', split_axis=0, concat_axis=0, tiled=True)  4.15 us
  transfers between devices with their start and end apart: 7, of which 3 were waited for; matrix products, arithmetic and copies ran while one was open for 5% of the time, Pallas kernels for 7%

profile of v6, /device:TPU:8, one launch (start us, length us, event | category | flops | bytes accessed | tf_op | source)
XLA Modules:
  0.0 111.0 jit_solution(4977778664434195800)
XLA Ops:
  0.6 0.0 copy-start.4
  0.6 2.0 %all-gather = f32[2,4,256]{2,1,0:T(4,128)S(1)} all-gather(f32[1,4,256]{2,1,0:T(4,128)} %bitcast.23), channel_id=1, replica_groups=mesh['sx'=2,'zh'=2,'zl'=4,'sc'=2,'xh'=2,'ya'=4,'yb'=2] {'sc'}, dimensions={0}, use_global_device_ids=true | all-gather | bytes 12288 | tf_op jit(solution)/shard_map/all_gather | solution.py:158
  2.6 15.3 %all_gather.13 = f32[32,256]{1,0:T(8,128)S(1)} all-gather(f32[8,256]{1,0:T(8,128)S(1)} %reshape.127), channel_id=1, replica_groups=mesh['sx'=2,'zh'=2,'zl'=4,'sc'=2,'xh'=2,'ya'=4,'yb'=2] {'zl'}, dimensions={0}, use_global_device_ids=true | all-gather | bytes 40960 | tf_op jit(solution)/shard_map/all_gather | solution.py:158
  17.9 9.6 %all_gather.14 = f32[64,256]{1,0:T(8,128)S(1)} all-gather(f32[32,256]{1,0:T(8,128)S(1)} %all_gather.13), channel_id=1, replica_groups=mesh['sx'=2,'zh'=2,'zl'=4,'sc'=2,'xh'=2,'ya'=4,'yb'=2] {'zh'}, dimensions={0}, use_global_device_ids=true | all-gather | bytes 98304 | tf_op jit(solution)/shard_map/all_gather | solution.py:158
  27.5 5.1 %all_gather.15 = f32[128,256]{1,0:T(8,128)S(1)} all-gather(f32[64,256]{1,0:T(8,128)S(1)} %all_gather.14), channel_id=1, replica_groups=mesh['sx'=2,'zh'=2,'zl'=4,'sc'=2,'xh'=2,'ya'=4,'yb'=2] {'sx'}, dimensions={0}, use_global_device_ids=true | all-gather | bytes 196608 | tf_op jit(solution)/shard_map/all_gather | solution.py:158
  32.6 4.4 %collective-permute-start = (bf16[4,2,128,128]{3,2,1,0:T(8,128)(2,1)}, bf16[4,2,128,128]{3,2,1,0:T(8,128)(2,1)S(1)}, u32[]{:S(2)}, u32[]{:S(2)}) collective-permute-start(bf16[4,2,128,128]{3,2,1,0:T(8,128)(2,1)} %param.6), channel_id=1, source_target_pairs={{0,1},{1,0},{8,9},{9,8},{2,3},{3,2},{10,11},{11,10},{4,5},{5,4},{1... | collective-permute-start | bytes 786440 | tf_op jit(solution)/shard_map/ppermute | solution.py:144
  37.0 2.9 %collective-permute-start.1 = (bf16[4,2,128,128]{3,2,1,0:T(8,128)(2,1)}, bf16[4,2,128,128]{3,2,1,0:T(8,128)(2,1)S(1)}, u32[]{:S(2)}, u32[]{:S(2)}) collective-permute-start(bf16[4,2,128,128]{3,2,1,0:T(8,128)(2,1)} %param.6), channel_id=1, source_target_pairs={{0,8},{1,9},{8,0},{9,1},{2,10},{3,11},{10,2},{11,3},{4,12},{5,13},... | collective-permute-start | bytes 786440 | tf_op jit(solution)/shard_map/ppermute | solution.py:144
  39.9 3.9 %collective-permute-start.2 = (bf16[4,2,128,128]{3,2,1,0:T(8,128)(2,1)}, bf16[4,2,128,128]{3,2,1,0:T(8,128)(2,1)S(1)}, u32[]{:S(2)}, u32[]{:S(2)}) collective-permute-start(bf16[4,2,128,128]{3,2,1,0:T(8,128)(2,1)} %param.6), channel_id=1, source_target_pairs={{0,9},{1,8},{8,1},{9,0},{2,11},{3,10},{10,3},{11,2},{4,13},{5,12},... | collective-permute-start | bytes 786440 | tf_op jit(solution)/shard_map/ppermute | solution.py:144
  43.8 4.0 %collective-permute-start.3 = (bf16[2,2,2,128,128]{4,3,2,1,0:T(8,128)(2,1)}, bf16[2,2,2,128,128]{4,3,2,1,0:T(8,128)(2,1)S(1)}, u32[]{:S(2)}, u32[]{:S(2)}) collective-permute-start(bf16[2,2,2,128,128]{4,3,2,1,0:T(8,128)(2,1)} %strain_ref), channel_id=1, source_target_pairs={{0,2},{2,0},{4,6},{6,4},{1,3},{3,1},{5,7},{7,5},{8,10},{10,8},{12,... | collective-permute-start | bytes 786440 | tf_op jit(solution)/shard_map/ppermute | solution.py:144
  47.8 5.0 %collective-permute-start.4 = (bf16[2,2,2,128,128]{4,3,2,1,0:T(8,128)(2,1)}, bf16[2,2,2,128,128]{4,3,2,1,0:T(8,128)(2,1)S(1)}, u32[]{:S(2)}, u32[]{:S(2)}) collective-permute-start(bf16[2,2,2,128,128]{4,3,2,1,0:T(8,128)(2,1)} %strain_ref), channel_id=1, source_target_pairs={{0,4},{2,6},{4,0},{6,2},{1,5},{3,7},{5,1},{7,3},{8,12},{10,14},{12... | collective-permute-start | bytes 786440 | tf_op jit(solution)/shard_map/ppermute | solution.py:144
  52.9 1.0 constant_dynamic-update-slice_fusion.3
  53.8 0.3 negate_convert_fusion
  54.1 0.3 fusion.16
  54.4 0.9 fusion.13
  55.4 0.0 copy-done.4
  55.4 0.7 fusion.1
  56.2 0.1 copy.22
  56.3 0.1 copy.23
  56.4 0.0 copy-start.1
  56.4 0.0 collective-permute-done
  56.4 0.0 copy-done.3
  56.4 3.2 %collective-permute-start.5 = (bf16[2,2,2,128,128]{4,3,2,1,0:T(8,128)(2,1)S(1)}, bf16[2,2,2,128,128]{4,3,2,1,0:T(8,128)(2,1)S(1)}, u32[]{:S(2)}, u32[]{:S(2)}) collective-permute-start(bf16[2,2,2,128,128]{4,3,2,1,0:T(8,128)(2,1)S(1)} %copy-done.3), channel_id=1, source_target_pairs={{0,6},{2,4},{4,2},{6,0},{1,7},{3,5},{5,3},{7,1},{8,14},{10,12},{12... | collective-permute-start | bytes 786440 | tf_op jit(solution)/shard_map/ppermute | solution.py:144
  59.6 0.0 collective-permute-done.1
  59.7 0.0 collective-permute-done.2
  59.8 0.2 add_bitcast_fusion
  60.0 0.8 copy-done
  60.7 0.3 multiply_reduce_fusion
  61.0 0.6 div.58.isig_ref
  61.6 0.5 iota.51.sidx_ref
  62.1 7.5 %shard_map.68 = f32[2,16,128]{2,1,0:T(8,128)} custom-call(s32[2]{0:T(128)} %iota.51.sidx_ref, f32[32]{0:T(128)} %div.58.isig_ref, bf16[2,2,2,128,128]{4,3,2,1,0:T(8,128)(2,1)} %strain_ref, bf16[16,2,128,128]{3,2,1,0:T(8,128)(2,1)} %copy-done, f32[2,128,128]{2,1,0:T(8,128)} %bitcast.17, bf16[256,256]{1,0:T(8,128)(2,1)} %get-tuple-element.13.m1_ref, ...), custom_call_target="tpu_custom_call" | custom-call | flops 2147483648 | bytes 1441792 | tf_op jit(solution)/shard_map/pallas_call | solution.py:125
  69.6 0.8 reduce_max.27
  70.4 0.0 collective-permute-done.3
  70.4 0.6 collective-permute-done.4
  71.0 4.9 %collective-permute-done.5 = bf16[2,2,2,128,128]{4,3,2,1,0:T(8,128)(2,1)S(1)} collective-permute-done((bf16[2,2,2,128,128]{4,3,2,1,0:T(8,128)(2,1)S(1)}, bf16[2,2,2,128,128]{4,3,2,1,0:T(8,128)(2,1)S(1)}, u32[]{:S(2)}, u32[]{:S(2)}) %collective-permute-start.5) | collective-permute-done | bytes 262176 | tf_op jit(solution)/shard_map/ppermute | solution.py:144
  75.9 1.0 pad_maximum_fusion.strain_ref
  76.9 0.5 iota.52.sidx_ref
  77.4 18.0 %shard_map.69 = f32[6,16,128]{2,1,0:T(8,128)} custom-call(s32[6]{0:T(128)} %iota.52.sidx_ref, f32[32]{0:T(128)} %div.58.isig_ref, bf16[6,2,2,128,128]{4,3,2,1,0:T(8,128)(2,1)} %pad_maximum_fusion.strain_ref, bf16[16,2,128,128]{3,2,1,0:T(8,128)(2,1)} %copy-done, f32[2,128,128]{2,1,0:T(8,128)} %bitcast.18, bf16[256,256]{1,0:T(8,128)(2,1)} %get-tuple-element.13.m1_ref, ...), custom_call_target="tpu_custom_call" | custom-call | flops 6442450944 | bytes 1966080 | tf_op jit(solution)/shard_map/pallas_call | solution.py:125
  95.3 0.9 reduce_max.28
  96.2 0.6 gather_fusion
  96.8 0.7 broadcast_select_fusion
  97.5 4.1 %all-to-all-start = ((f32[4,2,16]{2,1,0:T(2,128)}), f32[4,2,16]{2,1,0:T(2,128)S(1)}, u32[]{:S(2)}, u32[]{:S(2)}) async-start(f32[4,2,16]{2,1,0:T(2,128)} %broadcast_select_fusion), calls=%async_computation | async-start | bytes 8192 | tf_op jit(solution)/shard_map/all_to_all | solution.py:181
  101.7 7.7 %all-to-all-done = f32[4,2,16]{2,1,0:T(2,128)S(1)} async-done(((f32[4,2,16]{2,1,0:T(2,128)}), f32[4,2,16]{2,1,0:T(2,128)S(1)}, u32[]{:S(2)}, u32[]{:S(2)}) %all-to-all-start) | async-done | bytes 544 | tf_op jit(solution)/shard_map/all_to_all | solution.py:181
  109.3 0.1 reshape.109
  109.4 0.6 gather_fusion.1
  110.0 0.1 sqrt_bitcast_fusion
  110.1 0.1 sqrt.15
  110.2 0.1 broadcast_multiply_fusion
  110.3 0.7 select_reduce_fusion
  (25 shorter events, 0.3 us)
Async XLA Ops:
  0.6 54.7 %copy-start.4 = (s32[64]{0:T(128)S(1)}, s32[64]{0:T(128)}, u32[]{:S(2)}) copy-start(s32[64]{0:T(128)} %param.9) | copy-start | bytes 772
  27.5 28.9 %copy-start.3 = (bf16[2,2,2,128,128]{4,3,2,1,0:T(8,128)(2,1)S(1)}, bf16[2,2,2,128,128]{4,3,2,1,0:T(8,128)(2,1)}, u32[]{:S(2)}) copy-start(bf16[2,2,2,128,128]{4,3,2,1,0:T(8,128)(2,1)} %strain_ref) | copy-start | bytes 786436
  32.6 23.8 %collective-permute-start = (bf16[4,2,128,128]{3,2,1,0:T(8,128)(2,1)}, bf16[4,2,128,128]{3,2,1,0:T(8,128)(2,1)S(1)}, u32[]{:S(2)}, u32[]{:S(2)}) collective-permute-start(bf16[4,2,128,128]{3,2,1,0:T(8,128)(2,1)} %param.6), channel_id=1, source_target_pairs={{0,1},{1,0},{8,9},{9,8},{2,3},{3,2},{10,11},{11,10},{4,5},{5,4},{1... | collective-permute-start | bytes 786440 | tf_op jit(solution)/shard_map/ppermute | solution.py:144
  37.0 22.7 %collective-permute-start.1 = (bf16[4,2,128,128]{3,2,1,0:T(8,128)(2,1)}, bf16[4,2,128,128]{3,2,1,0:T(8,128)(2,1)S(1)}, u32[]{:S(2)}, u32[]{:S(2)}) collective-permute-start(bf16[4,2,128,128]{3,2,1,0:T(8,128)(2,1)} %param.6), channel_id=1, source_target_pairs={{0,8},{1,9},{8,0},{9,1},{2,10},{3,11},{10,2},{11,3},{4,12},{5,13},... | collective-permute-start | bytes 786440 | tf_op jit(solution)/shard_map/ppermute | solution.py:144
  39.9 19.8 %collective-permute-start.2 = (bf16[4,2,128,128]{3,2,1,0:T(8,128)(2,1)}, bf16[4,2,128,128]{3,2,1,0:T(8,128)(2,1)S(1)}, u32[]{:S(2)}, u32[]{:S(2)}) collective-permute-start(bf16[4,2,128,128]{3,2,1,0:T(8,128)(2,1)} %param.6), channel_id=1, source_target_pairs={{0,9},{1,8},{8,1},{9,0},{2,11},{3,10},{10,3},{11,2},{4,13},{5,12},... | collective-permute-start | bytes 786440 | tf_op jit(solution)/shard_map/ppermute | solution.py:144
  43.8 26.6 %collective-permute-start.3 = (bf16[2,2,2,128,128]{4,3,2,1,0:T(8,128)(2,1)}, bf16[2,2,2,128,128]{4,3,2,1,0:T(8,128)(2,1)S(1)}, u32[]{:S(2)}, u32[]{:S(2)}) collective-permute-start(bf16[2,2,2,128,128]{4,3,2,1,0:T(8,128)(2,1)} %strain_ref), channel_id=1, source_target_pairs={{0,2},{2,0},{4,6},{6,4},{1,3},{3,1},{5,7},{7,5},{8,10},{10,8},{12,... | collective-permute-start | bytes 786440 | tf_op jit(solution)/shard_map/ppermute | solution.py:144
  47.8 23.2 %collective-permute-start.4 = (bf16[2,2,2,128,128]{4,3,2,1,0:T(8,128)(2,1)}, bf16[2,2,2,128,128]{4,3,2,1,0:T(8,128)(2,1)S(1)}, u32[]{:S(2)}, u32[]{:S(2)}) collective-permute-start(bf16[2,2,2,128,128]{4,3,2,1,0:T(8,128)(2,1)} %strain_ref), channel_id=1, source_target_pairs={{0,4},{2,6},{4,0},{6,2},{1,5},{3,7},{5,1},{7,3},{8,12},{10,14},{12... | collective-permute-start | bytes 786440 | tf_op jit(solution)/shard_map/ppermute | solution.py:144
  56.4 3.6 %copy-start.1 = (f32[128,2,128]{2,0,1:T(8,128)}, f32[128,2,128]{2,0,1:T(8,128)S(1)}, u32[]{:S(2)}) copy-start(f32[128,2,128]{2,0,1:T(8,128)S(1)} %copy.23) | copy-start | bytes 393220
  56.4 19.4 %collective-permute-start.5 = (bf16[2,2,2,128,128]{4,3,2,1,0:T(8,128)(2,1)S(1)}, bf16[2,2,2,128,128]{4,3,2,1,0:T(8,128)(2,1)S(1)}, u32[]{:S(2)}, u32[]{:S(2)}) collective-permute-start(bf16[2,2,2,128,128]{4,3,2,1,0:T(8,128)(2,1)S(1)} %copy-done.3), channel_id=1, source_target_pairs={{0,6},{2,4},{4,2},{6,0},{1,7},{3,5},{5,3},{7,1},{8,14},{10,12},{12... | collective-permute-start | bytes 786440 | tf_op jit(solution)/shard_map/ppermute | solution.py:144
  59.8 1.0 copy-start
  77.4 24.3 %copy-start.5 = (s32[2]{0:T(128)S(1)}, s32[2]{0:T(128)}, u32[]{:S(2)}) copy-start(s32[2]{0:T(128)} %param.8) | copy-start | bytes 28
  97.5 11.9 %all-to-all-start = ((f32[4,2,16]{2,1,0:T(2,128)}), f32[4,2,16]{2,1,0:T(2,128)S(1)}, u32[]{:S(2)}, u32[]{:S(2)}) async-start(f32[4,2,16]{2,1,0:T(2,128)} %broadcast_select_fusion), calls=%async_computation | async-start | bytes 8192 | tf_op jit(solution)/shard_map/all_to_all | solution.py:181
  110.3 0.7 copy-start.2

commit v7 on v6

--- a/solution.py
+++ b/solution.py
@@ -2,6 +2,7 @@
 import math
 
 import jax
+import numpy as np
 import jax.numpy as jnp
 from jax import lax
 from jax.experimental import pallas as pl
@@ -17,20 +18,34 @@
 
 
 def make_tables():
-    row_idx = jnp.arange(N1, dtype=jnp.int32)
-    col_idx = jnp.arange(N2, dtype=jnp.int32)
-    ang_one = 2.0 * math.pi * (row_idx[:, None] * row_idx[None, :] % N1).astype(jnp.float32) / N1
-    cos_one, sin_one = (jnp.cos(ang_one), jnp.sin(ang_one))
-    first = jnp.concatenate(
-        [jnp.concatenate([cos_one, -sin_one], 1), jnp.concatenate([sin_one, cos_one], 1)], 0
-    ).astype(jnp.bfloat16)
-    ang_two = 2.0 * math.pi * (col_idx[:, None] * col_idx[None, :] % N2).astype(jnp.float32) / N2
-    cos_two, sin_two = (jnp.cos(ang_two), jnp.sin(ang_two))
-    second = jnp.concatenate(
-        [jnp.concatenate([cos_two, sin_two], 1), jnp.concatenate([-sin_two, cos_two], 1)], 0
-    ).astype(jnp.bfloat16)
-    ang_tw = 2.0 * math.pi * (row_idx[:, None] * col_idx[None, :] % BINS).astype(jnp.float32) / BINS
-    return (first, second, jnp.cos(ang_tw), jnp.sin(ang_tw))
+    f32 = np.float32
+    row_idx = np.arange(N1, dtype=np.int32)
+    col_idx = np.arange(N2, dtype=np.int32)
+
+    def angle(prod, n):
+        return (f32(2.0 * math.pi) * (prod % n).astype(f32)) / f32(n)
+
+    ang_one = angle(row_idx[:, None] * row_idx[None, :], N1)
+    cos_one = np.cos(ang_one.astype(np.float64)).astype(f32)
+    sin_one = np.sin(ang_one.astype(np.float64)).astype(f32)
+    first = np.concatenate(
+        [np.concatenate([cos_one, -sin_one], 1), np.concatenate([sin_one, cos_one], 1)], 0
+    )
+    ang_two = angle(col_idx[:, None] * col_idx[None, :], N2)
+    cos_two = np.cos(ang_two.astype(np.float64)).astype(f32)
+    sin_two = np.sin(ang_two.astype(np.float64)).astype(f32)
+    second = np.concatenate(
+        [np.concatenate([cos_two, sin_two], 1), np.concatenate([-sin_two, cos_two], 1)], 0
+    )
+    ang_tw = angle(row_idx[:, None] * col_idx[None, :], BINS)
+    tw_cos = np.cos(ang_tw.astype(np.float64)).astype(f32)
+    tw_sin = np.sin(ang_tw.astype(np.float64)).astype(f32)
+    return (
+        jnp.asarray(first, dtype=jnp.bfloat16),
+        jnp.asarray(second, dtype=jnp.bfloat16),
+        jnp.asarray(tw_cos),
+        jnp.asarray(tw_sin),
+    )
 
 
 def template_norm(tmpl, weights):
@@ -154,7 +169,7 @@
 
     rows_here = psd.shape[1]
     gathered = jnp.transpose(psd, (1, 0, 2)).reshape(rows_here, -1)
-    for axis in ("sc", "zl", "zh", "sx"):
+    for axis in ("sc", "z0", "z1", "zh", "sx"):
         gathered = lax.all_gather(gathered, axis, axis=0, tiled=True)
     gathered, strain, templates = lax.optimization_barrier((gathered, strain, templates))
     full_psd = jnp.transpose(gathered.reshape(-1, 2, N2), (1, 0, 2))
@@ -195,14 +210,13 @@
     n_seg, n_tpl = mesh.devices.shape
     n_y = 8
     n_xh = n_tpl // n_y
-    n_zl = 4
     n_zh = 2
-    n_sx = n_seg // (n_zh * n_zl * 2)
+    n_sx = n_seg // (n_zh * 2 * 2 * 2)
     sub = Mesh(
-        mesh.devices.reshape(n_sx, n_zh, n_zl, 2, n_xh, n_y // 2, 2),
-        ("sx", "zh", "zl", "sc", "xh", "ya", "yb"),
-    )
-    seg = ("sx", "zh", "zl", "sc")
+        mesh.devices.reshape(n_sx, n_zh, 2, 2, 2, n_xh, n_y // 2, 2),
+        ("sx", "zh", "z1", "z0", "sc", "xh", "ya", "yb"),
+    )
+    seg = ("sx", "zh", "z1", "z0", "sc")
     rows = seg + ("xh", "ya", "yb")
     placed = (
         P(rows, None, None, None, None),

time: 112 us -> 108 us (0.964)
  blocking collectives: 31.9 us -> 28.2 us
  other arithmetic: 6.91 us -> 4.69 us
  waiting for transfers between devices: 13.1 us -> 14.7 us
    all_gather x4 -> x5, blocking collectives: 31.9 us -> 28.2 us  [body(): gathered = lax.all_gather(gathered, axis, axis=0, tiled=True)]
    ppermute x6, waiting for transfers between devices: 5.45 us -> 6.97 us  [swapped(): return lax.ppermute(x, axes, [(i, i ^ k) for i in range(size)])]
  transfers between devices with their start and end apart: 7 -> 7, of which waited for: 3 -> 3; matrix products, arithmetic and copies ran while one was open for 5% -> 3% of each run, Pallas kernels for 7% -> 7%
where the time goes in v7:
time: 108 us
  starting transfers between devices  28.5 us (26%)
  blocking collectives  28.2 us (26%)
  Pallas kernels  25.5 us (24%)
  waiting for transfers between devices  14.7 us (14%)
  local copies, waits for them, and re-layouts  5.05 us (5%)
  other arithmetic  4.69 us (4%)
    all_gather x5, blocking collectives, body(): gathered = lax.all_gather(gathered, axis, axis=0, tiled=True)  28.2 us
    pallas_call x2, Pallas kernels, run_search(): pl.pallas_call(functools.partial(search_kernel, n_tb), out_shape=jax.Shap...  25.5 us
    ppermute x6, starting transfers between devices, swapped(): return lax.ppermute(x, axes, [(i, i ^ k) for i in range(size)])  24 us
    all_to_all x1, waiting for transfers between devices, body(): lax.all_to_all(grouped, 'ya', split_axis=0, concat_axis=0, tiled=True)  7.68 us
    ppermute x6, waiting for transfers between devices, swapped(): return lax.ppermute(x, axes, [(i, i ^ k) for i in range(size)])  6.97 us
    all_to_all x1, starting transfers between devices, body(): lax.all_to_all(grouped, 'ya', split_axis=0, concat_axis=0, tiled=True)  4.55 us
  transfers between devices with their start and end apart: 7, of which 3 were waited for; matrix products, arithmetic and copies ran while one was open for 3% of the time, Pallas kernels for 7%

profile of v7, /device:TPU:8, one launch (start us, length us, event | category | flops | bytes accessed | tf_op | source)
XLA Modules:
  0.0 107.5 jit_solution(5862256770235484296)
XLA Ops:
  0.6 0.0 copy-start.3
  0.6 0.0 copy-start.4
  0.7 2.1 %all-gather = f32[2,4,256]{2,1,0:T(4,128)S(1)} all-gather(f32[1,4,256]{2,1,0:T(4,128)} %bitcast.23), channel_id=1, replica_groups=mesh['sx'=2,'zh'=2,'z1'=2,'z0'=2,'sc'=2,'xh'=2,'ya'=4,'yb'=2] {'sc'}, dimensions={0}, use_global_device_ids=true | all-gather | bytes 12288 | tf_op jit(solution)/shard_map/all_gather | solution.py:173
  2.7 4.7 %all_gather.16 = f32[16,256]{1,0:T(8,128)S(1)} all-gather(f32[8,256]{1,0:T(8,128)S(1)} %reshape.127), channel_id=1, replica_groups=mesh['sx'=2,'zh'=2,'z1'=2,'z0'=2,'sc'=2,'xh'=2,'ya'=4,'yb'=2] {'z0'}, dimensions={0}, use_global_device_ids=true | all-gather | bytes 24576 | tf_op jit(solution)/shard_map/all_gather | solution.py:173
  7.4 6.5 %all_gather.17 = f32[32,256]{1,0:T(8,128)S(1)} all-gather(f32[16,256]{1,0:T(8,128)S(1)} %all_gather.16), channel_id=1, replica_groups=mesh['sx'=2,'zh'=2,'z1'=2,'z0'=2,'sc'=2,'xh'=2,'ya'=4,'yb'=2] {'z1'}, dimensions={0}, use_global_device_ids=true | all-gather | bytes 49152 | tf_op jit(solution)/shard_map/all_gather | solution.py:173
  14.0 10.0 %all_gather.18 = f32[64,256]{1,0:T(8,128)S(1)} all-gather(f32[32,256]{1,0:T(8,128)S(1)} %all_gather.17), channel_id=1, replica_groups=mesh['sx'=2,'zh'=2,'z1'=2,'z0'=2,'sc'=2,'xh'=2,'ya'=4,'yb'=2] {'zh'}, dimensions={0}, use_global_device_ids=true | all-gather | bytes 98304 | tf_op jit(solution)/shard_map/all_gather | solution.py:173
  24.0 4.9 %all_gather.19 = f32[128,256]{1,0:T(8,128)S(1)} all-gather(f32[64,256]{1,0:T(8,128)S(1)} %all_gather.18), channel_id=1, replica_groups=mesh['sx'=2,'zh'=2,'z1'=2,'z0'=2,'sc'=2,'xh'=2,'ya'=4,'yb'=2] {'sx'}, dimensions={0}, use_global_device_ids=true | all-gather | bytes 196608 | tf_op jit(solution)/shard_map/all_gather | solution.py:173
  28.9 5.0 %collective-permute-start = (bf16[4,2,128,128]{3,2,1,0:T(8,128)(2,1)}, bf16[4,2,128,128]{3,2,1,0:T(8,128)(2,1)S(1)}, u32[]{:S(2)}, u32[]{:S(2)}) collective-permute-start(bf16[4,2,128,128]{3,2,1,0:T(8,128)(2,1)} %param.10), channel_id=1, source_target_pairs={{0,1},{1,0},{8,9},{9,8},{2,3},{3,2},{10,11},{11,10},{4,5},{5,4},{1... | collective-permute-start | bytes 786440 | tf_op jit(solution)/shard_map/ppermute | solution.py:159
  33.9 2.3 %collective-permute-start.1 = (bf16[4,2,128,128]{3,2,1,0:T(8,128)(2,1)}, bf16[4,2,128,128]{3,2,1,0:T(8,128)(2,1)S(1)}, u32[]{:S(2)}, u32[]{:S(2)}) collective-permute-start(bf16[4,2,128,128]{3,2,1,0:T(8,128)(2,1)} %param.10), channel_id=1, source_target_pairs={{0,8},{1,9},{8,0},{9,1},{2,10},{3,11},{10,2},{11,3},{4,12},{5,13},... | collective-permute-start | bytes 786440 | tf_op jit(solution)/shard_map/ppermute | solution.py:159
  36.2 4.5 %collective-permute-start.2 = (bf16[4,2,128,128]{3,2,1,0:T(8,128)(2,1)}, bf16[4,2,128,128]{3,2,1,0:T(8,128)(2,1)S(1)}, u32[]{:S(2)}, u32[]{:S(2)}) collective-permute-start(bf16[4,2,128,128]{3,2,1,0:T(8,128)(2,1)} %param.10), channel_id=1, source_target_pairs={{0,9},{1,8},{8,1},{9,0},{2,11},{3,10},{10,3},{11,2},{4,13},{5,12},... | collective-permute-start | bytes 786440 | tf_op jit(solution)/shard_map/ppermute | solution.py:159
  40.7 3.4 %collective-permute-start.3 = (bf16[2,2,2,128,128]{4,3,2,1,0:T(8,128)(2,1)}, bf16[2,2,2,128,128]{4,3,2,1,0:T(8,128)(2,1)S(1)}, u32[]{:S(2)}, u32[]{:S(2)}) collective-permute-start(bf16[2,2,2,128,128]{4,3,2,1,0:T(8,128)(2,1)} %strain_ref), channel_id=1, source_target_pairs={{0,2},{2,0},{4,6},{6,4},{1,3},{3,1},{5,7},{7,5},{8,10},{10,8},{12,... | collective-permute-start | bytes 786440 | tf_op jit(solution)/shard_map/ppermute | solution.py:159
  44.1 5.0 %collective-permute-start.4 = (bf16[2,2,2,128,128]{4,3,2,1,0:T(8,128)(2,1)}, bf16[2,2,2,128,128]{4,3,2,1,0:T(8,128)(2,1)S(1)}, u32[]{:S(2)}, u32[]{:S(2)}) collective-permute-start(bf16[2,2,2,128,128]{4,3,2,1,0:T(8,128)(2,1)} %strain_ref), channel_id=1, source_target_pairs={{0,4},{2,6},{4,0},{6,2},{1,5},{3,7},{5,1},{7,3},{8,12},{10,14},{12... | collective-permute-start | bytes 786440 | tf_op jit(solution)/shard_map/ppermute | solution.py:159
  49.2 1.0 constant_dynamic-update-slice_fusion.3
  50.2 0.0 copy-done.4
  50.3 0.1 copy.26
  50.4 0.1 copy.27
  50.5 0.0 copy-start.1
  50.5 0.0 collective-permute-done
  50.5 0.0 copy-done.3
  50.5 3.7 %collective-permute-start.5 = (bf16[2,2,2,128,128]{4,3,2,1,0:T(8,128)(2,1)S(1)}, bf16[2,2,2,128,128]{4,3,2,1,0:T(8,128)(2,1)S(1)}, u32[]{:S(2)}, u32[]{:S(2)}) collective-permute-start(bf16[2,2,2,128,128]{4,3,2,1,0:T(8,128)(2,1)S(1)} %copy-done.3), channel_id=1, source_target_pairs={{0,6},{2,4},{4,2},{6,0},{1,7},{3,5},{5,3},{7,1},{8,14},{10,12},{12... | collective-permute-start | bytes 786440 | tf_op jit(solution)/shard_map/ppermute | solution.py:159
  54.3 0.0 collective-permute-done.1
  54.4 0.0 collective-permute-done.2
  54.4 0.0 copy-start
  54.4 0.2 add_bitcast_fusion
  54.6 0.0 copy-done.1
  54.6 0.8 copy-done
  55.4 0.3 multiply_reduce_fusion
  55.7 0.6 div.26.isig_ref
  56.3 0.5 iota.43.sidx_ref
  56.8 7.5 %shard_map.104 = f32[2,16,128]{2,1,0:T(8,128)} custom-call(s32[2]{0:T(128)} %iota.43.sidx_ref, f32[32]{0:T(128)} %div.26.isig_ref, bf16[2,2,2,128,128]{4,3,2,1,0:T(8,128)(2,1)} %strain_ref, bf16[16,2,128,128]{3,2,1,0:T(8,128)(2,1)} %copy-done, f32[2,128,128]{2,1,0:T(8,128)} %bitcast.17, bf16[256,256]{1,0:T(8,128)(2,1)} %constant.57.clone.m1_ref, ...), custom_call_target="tpu_custom_call" | custom-call | flops 2147483648 | bytes 1441792 | tf_op jit(solution)/shard_map/pallas_call | solution.py:140
  64.3 0.8 reduce_max.27
  65.1 0.0 collective-permute-done.3
  65.1 1.4 %collective-permute-done.4 = bf16[2,2,2,128,128]{4,3,2,1,0:T(8,128)(2,1)S(1)} collective-permute-done((bf16[2,2,2,128,128]{4,3,2,1,0:T(8,128)(2,1)}, bf16[2,2,2,128,128]{4,3,2,1,0:T(8,128)(2,1)S(1)}, u32[]{:S(2)}, u32[]{:S(2)}) %collective-permute-start.4) | collective-permute-done | bytes 262176 | tf_op jit(solution)/shard_map/ppermute | solution.py:159
  66.5 5.6 %collective-permute-done.5 = bf16[2,2,2,128,128]{4,3,2,1,0:T(8,128)(2,1)S(1)} collective-permute-done((bf16[2,2,2,128,128]{4,3,2,1,0:T(8,128)(2,1)S(1)}, bf16[2,2,2,128,128]{4,3,2,1,0:T(8,128)(2,1)S(1)}, u32[]{:S(2)}, u32[]{:S(2)}) %collective-permute-start.5) | collective-permute-done | bytes 262176 | tf_op jit(solution)/shard_map/ppermute | solution.py:159
  72.0 1.0 pad_maximum_fusion.strain_ref
  73.0 0.5 iota.44.sidx_ref
  73.6 18.0 %shard_map.105 = f32[6,16,128]{2,1,0:T(8,128)} custom-call(s32[6]{0:T(128)} %iota.44.sidx_ref, f32[32]{0:T(128)} %div.26.isig_ref, bf16[6,2,2,128,128]{4,3,2,1,0:T(8,128)(2,1)} %pad_maximum_fusion.strain_ref, bf16[16,2,128,128]{3,2,1,0:T(8,128)(2,1)} %copy-done, f32[2,128,128]{2,1,0:T(8,128)} %bitcast.18, bf16[256,256]{1,0:T(8,128)(2,1)} %constant.57.clone.m1_ref, ...), custom_call_target="tpu_custom_call" | custom-call | flops 6442450944 | bytes 1966080 | tf_op jit(solution)/shard_map/pallas_call | solution.py:140
  91.5 0.9 reduce_max.28
  92.4 0.6 gather_fusion
  93.0 0.7 broadcast_select_fusion
  93.7 4.6 %all-to-all-start = ((f32[4,2,16]{2,1,0:T(2,128)}), f32[4,2,16]{2,1,0:T(2,128)S(1)}, u32[]{:S(2)}, u32[]{:S(2)}) async-start(f32[4,2,16]{2,1,0:T(2,128)} %broadcast_select_fusion), calls=%async_computation | async-start | bytes 8192 | tf_op jit(solution)/shard_map/all_to_all | solution.py:196
  98.2 7.7 %all-to-all-done = f32[4,2,16]{2,1,0:T(2,128)S(1)} async-done(((f32[4,2,16]{2,1,0:T(2,128)}), f32[4,2,16]{2,1,0:T(2,128)S(1)}, u32[]{:S(2)}, u32[]{:S(2)}) %all-to-all-start) | async-done | bytes 544 | tf_op jit(solution)/shard_map/all_to_all | solution.py:196
  105.9 0.1 reshape.109
  106.0 0.6 gather_fusion.1
  106.6 0.1 sqrt_bitcast_fusion
  106.7 0.1 sqrt.15
  106.8 0.1 broadcast_multiply_fusion
  106.9 0.7 select_reduce_fusion
  (22 shorter events, 0.2 us)
Async XLA Ops:
  0.6 49.9 %copy-start.3 = (bf16[2,2,2,128,128]{4,3,2,1,0:T(8,128)(2,1)S(1)}, bf16[2,2,2,128,128]{4,3,2,1,0:T(8,128)(2,1)}, u32[]{:S(2)}) copy-start(bf16[2,2,2,128,128]{4,3,2,1,0:T(8,128)(2,1)} %strain_ref) | copy-start | bytes 786436
  0.6 49.6 %copy-start.4 = (s32[64]{0:T(128)S(1)}, s32[64]{0:T(128)}, u32[]{:S(2)}) copy-start(s32[64]{0:T(128)} %param.13) | copy-start | bytes 772
  28.9 21.6 %collective-permute-start = (bf16[4,2,128,128]{3,2,1,0:T(8,128)(2,1)}, bf16[4,2,128,128]{3,2,1,0:T(8,128)(2,1)S(1)}, u32[]{:S(2)}, u32[]{:S(2)}) collective-permute-start(bf16[4,2,128,128]{3,2,1,0:T(8,128)(2,1)} %param.10), channel_id=1, source_target_pairs={{0,1},{1,0},{8,9},{9,8},{2,3},{3,2},{10,11},{11,10},{4,5},{5,4},{1... | collective-permute-start | bytes 786440 | tf_op jit(solution)/shard_map/ppermute | solution.py:159
  33.9 20.5 %collective-permute-start.1 = (bf16[4,2,128,128]{3,2,1,0:T(8,128)(2,1)}, bf16[4,2,128,128]{3,2,1,0:T(8,128)(2,1)S(1)}, u32[]{:S(2)}, u32[]{:S(2)}) collective-permute-start(bf16[4,2,128,128]{3,2,1,0:T(8,128)(2,1)} %param.10), channel_id=1, source_target_pairs={{0,8},{1,9},{8,0},{9,1},{2,10},{3,11},{10,2},{11,3},{4,12},{5,13},... | collective-permute-start | bytes 786440 | tf_op jit(solution)/shard_map/ppermute | solution.py:159
  36.2 18.2 %collective-permute-start.2 = (bf16[4,2,128,128]{3,2,1,0:T(8,128)(2,1)}, bf16[4,2,128,128]{3,2,1,0:T(8,128)(2,1)S(1)}, u32[]{:S(2)}, u32[]{:S(2)}) collective-permute-start(bf16[4,2,128,128]{3,2,1,0:T(8,128)(2,1)} %param.10), channel_id=1, source_target_pairs={{0,9},{1,8},{8,1},{9,0},{2,11},{3,10},{10,3},{11,2},{4,13},{5,12},... | collective-permute-start | bytes 786440 | tf_op jit(solution)/shard_map/ppermute | solution.py:159
  40.7 24.4 %collective-permute-start.3 = (bf16[2,2,2,128,128]{4,3,2,1,0:T(8,128)(2,1)}, bf16[2,2,2,128,128]{4,3,2,1,0:T(8,128)(2,1)S(1)}, u32[]{:S(2)}, u32[]{:S(2)}) collective-permute-start(bf16[2,2,2,128,128]{4,3,2,1,0:T(8,128)(2,1)} %strain_ref), channel_id=1, source_target_pairs={{0,2},{2,0},{4,6},{6,4},{1,3},{3,1},{5,7},{7,5},{8,10},{10,8},{12,... | collective-permute-start | bytes 786440 | tf_op jit(solution)/shard_map/ppermute | solution.py:159
  44.1 22.3 %collective-permute-start.4 = (bf16[2,2,2,128,128]{4,3,2,1,0:T(8,128)(2,1)}, bf16[2,2,2,128,128]{4,3,2,1,0:T(8,128)(2,1)S(1)}, u32[]{:S(2)}, u32[]{:S(2)}) collective-permute-start(bf16[2,2,2,128,128]{4,3,2,1,0:T(8,128)(2,1)} %strain_ref), channel_id=1, source_target_pairs={{0,4},{2,6},{4,0},{6,2},{1,5},{3,7},{5,1},{7,3},{8,12},{10,14},{12... | collective-permute-start | bytes 786440 | tf_op jit(solution)/shard_map/ppermute | solution.py:159
  50.5 4.1 %copy-start.1 = (f32[128,2,128]{2,0,1:T(8,128)}, f32[128,2,128]{2,0,1:T(8,128)S(1)}, u32[]{:S(2)}) copy-start(f32[128,2,128]{2,0,1:T(8,128)S(1)} %copy.27) | copy-start | bytes 393220
  50.5 21.5 %collective-permute-start.5 = (bf16[2,2,2,128,128]{4,3,2,1,0:T(8,128)(2,1)S(1)}, bf16[2,2,2,128,128]{4,3,2,1,0:T(8,128)(2,1)S(1)}, u32[]{:S(2)}, u32[]{:S(2)}) collective-permute-start(bf16[2,2,2,128,128]{4,3,2,1,0:T(8,128)(2,1)S(1)} %copy-done.3), channel_id=1, source_target_pairs={{0,6},{2,4},{4,2},{6,0},{1,7},{3,5},{5,3},{7,1},{8,14},{10,12},{12... | collective-permute-start | bytes 786440 | tf_op jit(solution)/shard_map/ppermute | solution.py:159
  54.4 1.0 copy-start
  73.6 24.7 %copy-start.5 = (s32[2]{0:T(128)S(1)}, s32[2]{0:T(128)}, u32[]{:S(2)}) copy-start(s32[2]{0:T(128)} %param.12) | copy-start | bytes 28
  93.7 12.3 %all-to-all-start = ((f32[4,2,16]{2,1,0:T(2,128)}), f32[4,2,16]{2,1,0:T(2,128)S(1)}, u32[]{:S(2)}, u32[]{:S(2)}) async-start(f32[4,2,16]{2,1,0:T(2,128)} %broadcast_select_fusion), calls=%async_computation | async-start | bytes 8192 | tf_op jit(solution)/shard_map/all_to_all | solution.py:196
  106.9 0.7 copy-start.2

commit v8 on v7

--- a/solution.py
+++ b/solution.py
@@ -160,8 +160,8 @@
 
 
 def body(strain, templates, psd, flags, assign):
-    ya = lax.axis_index("ya")
-    n_ya = lax.axis_size("ya")
+    ya = lax.axis_index(("ya1", "ya0"))
+    n_ya = lax.axis_size(("ya1", "ya0"))
     n_xh = lax.axis_size("xh")
     n_yb = lax.axis_size("yb")
     n_g = n_xh * n_yb
@@ -179,7 +179,7 @@
     tmpl_rel = jnp.concatenate(
         [templates] + [swapped(templates, ("xh", "yb"), n_g, k) for k in range(1, n_g)], 0
     )
-    piece = jnp.concatenate([swapped(strain, "ya", n_ya, k) for k in range(1, n_ya)], 0)
+    piece = jnp.concatenate([swapped(strain, ("ya1", "ya0"), n_ya, k) for k in range(1, n_ya)], 0)
     sigma2 = jax.vmap(lambda tmpl: template_norm(tmpl, weights))(tmpl_rel)
     isig = (1.0 / sigma2).reshape(-1)
 
@@ -192,8 +192,10 @@
     slots = jnp.concatenate([own_rows, other_rows], 0).reshape(n_ya, own_count, -1)
 
     lanes = jnp.arange(n_ya, dtype=jnp.int32)
-    grouped = jnp.take(slots, ya ^ lanes, axis=0)
-    blocks = lax.all_to_all(grouped, "ya", split_axis=0, concat_axis=0, tiled=True)
+    every = slots[None]
+    for axis in ("ya0", "ya1"):
+        every = lax.all_gather(every, axis, axis=0, tiled=True)
+    blocks = every[lanes, ya ^ lanes]
     blocks = blocks.reshape(n_ya, own_count, n_g, -1)
     src_t = g ^ jnp.arange(n_g, dtype=jnp.int32)
     ordered = jnp.take(blocks, src_t, axis=2)
@@ -213,14 +215,14 @@
     n_zh = 2
     n_sx = n_seg // (n_zh * 2 * 2 * 2)
     sub = Mesh(
-        mesh.devices.reshape(n_sx, n_zh, 2, 2, 2, n_xh, n_y // 2, 2),
-        ("sx", "zh", "z1", "z0", "sc", "xh", "ya", "yb"),
+        mesh.devices.reshape(n_sx, n_zh, 2, 2, 2, n_xh, 2, n_y // 4, 2),
+        ("sx", "zh", "z1", "z0", "sc", "xh", "ya1", "ya0", "yb"),
     )
     seg = ("sx", "zh", "z1", "z0", "sc")
-    rows = seg + ("xh", "ya", "yb")
+    rows = seg + ("xh", "ya1", "ya0", "yb")
     placed = (
         P(rows, None, None, None, None),
-        P(("xh", "ya", "yb"), None, None, None),
+        P(("xh", "ya1", "ya0", "yb"), None, None, None),
         P(None, seg, None),
         P(rows),
         P(),

time: 108 us -> 109 us (level)
  blocking collectives: 28.2 us -> 41.7 us
  waiting for transfers between devices: 14.7 us -> 6.96 us
  starting transfers between devices: 28.5 us -> 24 us
    all_gather x0 -> x2, blocking collectives: none -> 13.5 us  [body(): every = lax.all_gather(every, axis, axis=0, tiled=True)]
    all_to_all x1 -> x0, waiting for transfers between devices: 7.68 us -> none  [body(): lax.all_to_all(grouped, 'ya', split_axis=0, concat_axis=0, tiled=True)]
    all_to_all x1 -> x0, starting transfers between devices: 4.55 us -> none  [body(): lax.all_to_all(grouped, 'ya', split_axis=0, concat_axis=0, tiled=True)]
  transfers between devices with their start and end apart: 7 -> 6, of which waited for: 3 -> 2; matrix products, arithmetic and copies ran while one was open for 3% -> 3% of each run, Pallas kernels for 7% -> 7%
where the time goes in v8:
time: 109 us; the launch traced here: 108 us
  blocking collectives  41.7 us (38%)
  Pallas kernels  25.4 us (23%)
  starting transfers between devices  24 us (22%)
  waiting for transfers between devices  6.96 us (6%)
  local copies, waits for them, and re-layouts  5.08 us (5%)
  other arithmetic  4.02 us (4%)
    all_gather x5, blocking collectives, body(): gathered = lax.all_gather(gathered, axis, axis=0, tiled=True)  28.2 us
    pallas_call x2, Pallas kernels, run_search(): pl.pallas_call(functools.partial(search_kernel, n_tb), out_shape=jax.Shap...  25.4 us
    ppermute x6, starting transfers between devices, swapped(): return lax.ppermute(x, axes, [(i, i ^ k) for i in range(size)])  24 us
    all_gather x2, blocking collectives, body(): every = lax.all_gather(every, axis, axis=0, tiled=True)  13.5 us
    ppermute x6, waiting for transfers between devices, swapped(): return lax.ppermute(x, axes, [(i, i ^ k) for i in range(size)])  6.96 us
  transfers between devices with their start and end apart: 6, of which 2 were waited for; matrix products, arithmetic and copies ran while one was open for 3% of the time, Pallas kernels for 7%

profile of v8, /device:TPU:8, one launch (start us, length us, event | category | flops | bytes accessed | tf_op | source)
XLA Modules:
  0.0 108.2 jit_solution(13099253030260073125)
XLA Ops:
  0.6 0.0 copy-start.3
  0.6 0.0 copy-start.4
  0.7 0.0 copy-start.5
  0.7 2.1 %all-gather = f32[2,4,256]{2,1,0:T(4,128)S(1)} all-gather(f32[1,4,256]{2,1,0:T(4,128)} %bitcast.23), channel_id=1, replica_groups=mesh['sx'=2,'zh'=2,'z1'=2,'z0'=2,'sc'=2,'xh'=2,'ya1'=2,'ya0'=2,'yb'=2] {..., dimensions={0}, use_global_device_ids=true | all-gather | bytes 12288 | tf_op jit(solution)/shard_map/all_gather | solution.py:173
  2.8 4.7 %all_gather.22 = f32[16,256]{1,0:T(8,128)S(1)} all-gather(f32[8,256]{1,0:T(8,128)S(1)} %reshape.116), channel_id=1, replica_groups=mesh['sx'=2,'zh'=2,'z1'=2,'z0'=2,'sc'=2,'xh'=2,'ya1'=2,'ya0'=2,'yb'=2] {..., dimensions={0}, use_global_device_ids=true | all-gather | bytes 24576 | tf_op jit(solution)/shard_map/all_gather | solution.py:173
  7.5 6.5 %all_gather.23 = f32[32,256]{1,0:T(8,128)S(1)} all-gather(f32[16,256]{1,0:T(8,128)S(1)} %all_gather.22), channel_id=1, replica_groups=mesh['sx'=2,'zh'=2,'z1'=2,'z0'=2,'sc'=2,'xh'=2,'ya1'=2,'ya0'=2,'yb'=2] {..., dimensions={0}, use_global_device_ids=true | all-gather | bytes 49152 | tf_op jit(solution)/shard_map/all_gather | solution.py:173
  14.0 10.0 %all_gather.24 = f32[64,256]{1,0:T(8,128)S(1)} all-gather(f32[32,256]{1,0:T(8,128)S(1)} %all_gather.23), channel_id=1, replica_groups=mesh['sx'=2,'zh'=2,'z1'=2,'z0'=2,'sc'=2,'xh'=2,'ya1'=2,'ya0'=2,'yb'=2] {..., dimensions={0}, use_global_device_ids=true | all-gather | bytes 98304 | tf_op jit(solution)/shard_map/all_gather | solution.py:173
  24.0 4.9 %all_gather.25 = f32[128,256]{1,0:T(8,128)S(1)} all-gather(f32[64,256]{1,0:T(8,128)S(1)} %all_gather.24), channel_id=1, replica_groups=mesh['sx'=2,'zh'=2,'z1'=2,'z0'=2,'sc'=2,'xh'=2,'ya1'=2,'ya0'=2,'yb'=2] {..., dimensions={0}, use_global_device_ids=true | all-gather | bytes 196608 | tf_op jit(solution)/shard_map/all_gather | solution.py:173
  28.9 5.0 %collective-permute-start = (bf16[4,2,128,128]{3,2,1,0:T(8,128)(2,1)}, bf16[4,2,128,128]{3,2,1,0:T(8,128)(2,1)S(1)}, u32[]{:S(2)}, u32[]{:S(2)}) collective-permute-start(bf16[4,2,128,128]{3,2,1,0:T(8,128)(2,1)} %param.10), channel_id=1, source_target_pairs={{0,1},{1,0},{8,9},{9,8},{2,3},{3,2},{10,11},{11,10},{4,5},{5,4},{1... | collective-permute-start | bytes 786440 | tf_op jit(solution)/shard_map/ppermute | solution.py:159
  33.9 2.3 %collective-permute-start.1 = (bf16[4,2,128,128]{3,2,1,0:T(8,128)(2,1)}, bf16[4,2,128,128]{3,2,1,0:T(8,128)(2,1)S(1)}, u32[]{:S(2)}, u32[]{:S(2)}) collective-permute-start(bf16[4,2,128,128]{3,2,1,0:T(8,128)(2,1)} %param.10), channel_id=1, source_target_pairs={{0,8},{1,9},{8,0},{9,1},{2,10},{3,11},{10,2},{11,3},{4,12},{5,13},... | collective-permute-start | bytes 786440 | tf_op jit(solution)/shard_map/ppermute | solution.py:159
  36.2 4.5 %collective-permute-start.2 = (bf16[4,2,128,128]{3,2,1,0:T(8,128)(2,1)}, bf16[4,2,128,128]{3,2,1,0:T(8,128)(2,1)S(1)}, u32[]{:S(2)}, u32[]{:S(2)}) collective-permute-start(bf16[4,2,128,128]{3,2,1,0:T(8,128)(2,1)} %param.10), channel_id=1, source_target_pairs={{0,9},{1,8},{8,1},{9,0},{2,11},{3,10},{10,3},{11,2},{4,13},{5,12},... | collective-permute-start | bytes 786440 | tf_op jit(solution)/shard_map/ppermute | solution.py:159
  40.7 3.4 %collective-permute-start.3 = (bf16[2,2,2,128,128]{4,3,2,1,0:T(8,128)(2,1)}, bf16[2,2,2,128,128]{4,3,2,1,0:T(8,128)(2,1)S(1)}, u32[]{:S(2)}, u32[]{:S(2)}) collective-permute-start(bf16[2,2,2,128,128]{4,3,2,1,0:T(8,128)(2,1)} %strain_ref), channel_id=1, source_target_pairs={{0,2},{2,0},{4,6},{6,4},{1,3},{3,1},{5,7},{7,5},{8,10},{10,8},{12,... | collective-permute-start | bytes 786440 | tf_op jit(solution)/shard_map/ppermute | solution.py:159
  44.1 5.0 %collective-permute-start.4 = (bf16[2,2,2,128,128]{4,3,2,1,0:T(8,128)(2,1)}, bf16[2,2,2,128,128]{4,3,2,1,0:T(8,128)(2,1)S(1)}, u32[]{:S(2)}, u32[]{:S(2)}) collective-permute-start(bf16[2,2,2,128,128]{4,3,2,1,0:T(8,128)(2,1)} %strain_ref), channel_id=1, source_target_pairs={{0,4},{2,6},{4,0},{6,2},{1,5},{3,7},{5,1},{7,3},{8,12},{10,14},{12... | collective-permute-start | bytes 786440 | tf_op jit(solution)/shard_map/ppermute | solution.py:159
  49.2 1.0 constant_dynamic-update-slice_fusion.3
  50.2 0.0 copy-done.4
  50.3 0.1 copy.35
  50.4 0.1 copy.36
  50.5 0.0 copy-done.5
  50.5 0.0 copy-start.1
  50.5 0.0 collective-permute-done
  50.5 0.0 copy-done.3
  50.5 3.7 %collective-permute-start.5 = (bf16[2,2,2,128,128]{4,3,2,1,0:T(8,128)(2,1)S(1)}, bf16[2,2,2,128,128]{4,3,2,1,0:T(8,128)(2,1)S(1)}, u32[]{:S(2)}, u32[]{:S(2)}) collective-permute-start(bf16[2,2,2,128,128]{4,3,2,1,0:T(8,128)(2,1)S(1)} %copy-done.3), channel_id=1, source_target_pairs={{0,6},{2,4},{4,2},{6,0},{1,7},{3,5},{5,3},{7,1},{8,14},{10,12},{12... | collective-permute-start | bytes 786440 | tf_op jit(solution)/shard_map/ppermute | solution.py:159
  54.3 0.0 collective-permute-done.1
  54.4 0.0 collective-permute-done.2
  54.4 0.0 copy-start
  54.5 0.2 add_bitcast_fusion
  54.7 0.8 copy-done
  55.4 0.3 multiply_reduce_fusion
  55.7 0.6 div.26.isig_ref
  56.3 0.5 iota.43.sidx_ref
  56.8 7.5 %shard_map.104 = f32[2,16,128]{2,1,0:T(8,128)} custom-call(s32[2]{0:T(128)} %iota.43.sidx_ref, f32[32]{0:T(128)} %div.26.isig_ref, bf16[2,2,2,128,128]{4,3,2,1,0:T(8,128)(2,1)} %strain_ref, bf16[16,2,128,128]{3,2,1,0:T(8,128)(2,1)} %copy-done, f32[2,128,128]{2,1,0:T(8,128)} %bitcast.17, bf16[256,256]{1,0:T(8,128)(2,1)} %constant.51.clone.m1_ref, ...), custom_call_target="tpu_custom_call" | custom-call | flops 2147483648 | bytes 1441792 | tf_op jit(solution)/shard_map/pallas_call | solution.py:140
  64.3 0.8 reduce_max.27
  65.1 0.0 collective-permute-done.3
  65.1 1.4 %collective-permute-done.4 = bf16[2,2,2,128,128]{4,3,2,1,0:T(8,128)(2,1)S(1)} collective-permute-done((bf16[2,2,2,128,128]{4,3,2,1,0:T(8,128)(2,1)}, bf16[2,2,2,128,128]{4,3,2,1,0:T(8,128)(2,1)S(1)}, u32[]{:S(2)}, u32[]{:S(2)}) %collective-permute-start.4) | collective-permute-done | bytes 262176 | tf_op jit(solution)/shard_map/ppermute | solution.py:159
  66.5 5.6 %collective-permute-done.5 = bf16[2,2,2,128,128]{4,3,2,1,0:T(8,128)(2,1)S(1)} collective-permute-done((bf16[2,2,2,128,128]{4,3,2,1,0:T(8,128)(2,1)S(1)}, bf16[2,2,2,128,128]{4,3,2,1,0:T(8,128)(2,1)S(1)}, u32[]{:S(2)}, u32[]{:S(2)}) %collective-permute-start.5) | collective-permute-done | bytes 262176 | tf_op jit(solution)/shard_map/ppermute | solution.py:159
  72.1 1.0 pad_maximum_fusion.strain_ref
  73.1 0.5 iota.44.sidx_ref
  73.6 18.0 %shard_map.105 = f32[6,16,128]{2,1,0:T(8,128)} custom-call(s32[6]{0:T(128)} %iota.44.sidx_ref, f32[32]{0:T(128)} %div.26.isig_ref, bf16[6,2,2,128,128]{4,3,2,1,0:T(8,128)(2,1)} %pad_maximum_fusion.strain_ref, bf16[16,2,128,128]{3,2,1,0:T(8,128)(2,1)} %copy-done, f32[2,128,128]{2,1,0:T(8,128)} %bitcast.18, bf16[256,256]{1,0:T(8,128)(2,1)} %constant.51.clone.m1_ref, ...), custom_call_target="tpu_custom_call" | custom-call | flops 6442450944 | bytes 1966080 | tf_op jit(solution)/shard_map/pallas_call | solution.py:140
  91.5 0.9 reduce_max.28
  92.4 5.3 %all_gather.26 = f32[2,4,2,16]{3,1,2,0:T(4,128)S(1)} all-gather(f32[1,4,2,16]{3,1,2,0:T(4,128)S(1)} %copy.37), channel_id=1, replica_groups=mesh['sx'=2,'zh'=2,'z1'=2,'z0'=2,'sc'=2,'xh'=2,'ya1'=2,'ya0'=2,'yb'=2] {..., dimensions={0}, use_global_device_ids=true | all-gather | bytes 1536 | tf_op jit(solution)/shard_map/all_gather | solution.py:197
  97.7 8.3 %all_gather.27 = f32[4,4,2,16]{3,1,2,0:T(4,128)S(1)} all-gather(f32[2,4,2,16]{3,1,2,0:T(4,128)S(1)} %all_gather.26), channel_id=1, replica_groups=mesh['sx'=2,'zh'=2,'z1'=2,'z0'=2,'sc'=2,'xh'=2,'ya1'=2,'ya0'=2,'yb'=2] {..., dimensions={0}, use_global_device_ids=true | all-gather | bytes 3072 | tf_op jit(solution)/shard_map/all_gather | solution.py:197
  106.0 0.6 gather_fusion
  106.6 0.1 reshape.100
  106.7 0.6 gather_fusion.1
  107.2 0.1 sqrt_bitcast_fusion
  107.3 0.1 sqrt.15
  107.4 0.1 broadcast_multiply_fusion
  107.5 0.7 select_reduce_fusion
  (21 shorter events, 0.2 us)
Async XLA Ops:
  0.6 49.9 %copy-start.3 = (bf16[2,2,2,128,128]{4,3,2,1,0:T(8,128)(2,1)S(1)}, bf16[2,2,2,128,128]{4,3,2,1,0:T(8,128)(2,1)}, u32[]{:S(2)}) copy-start(bf16[2,2,2,128,128]{4,3,2,1,0:T(8,128)(2,1)} %strain_ref) | copy-start | bytes 786436
  0.6 49.6 %copy-start.4 = (s32[64]{0:T(128)S(1)}, s32[64]{0:T(128)}, u32[]{:S(2)}) copy-start(s32[64]{0:T(128)} %param.13) | copy-start | bytes 772
  0.7 49.8 %copy-start.5 = (s32[2]{0:T(128)S(1)}, s32[2]{0:T(128)}, u32[]{:S(2)}) copy-start(s32[2]{0:T(128)} %param.12) | copy-start | bytes 28
  28.9 21.6 %collective-permute-start = (bf16[4,2,128,128]{3,2,1,0:T(8,128)(2,1)}, bf16[4,2,128,128]{3,2,1,0:T(8,128)(2,1)S(1)}, u32[]{:S(2)}, u32[]{:S(2)}) collective-permute-start(bf16[4,2,128,128]{3,2,1,0:T(8,128)(2,1)} %param.10), channel_id=1, source_target_pairs={{0,1},{1,0},{8,9},{9,8},{2,3},{3,2},{10,11},{11,10},{4,5},{5,4},{1... | collective-permute-start | bytes 786440 | tf_op jit(solution)/shard_map/ppermute | solution.py:159
  33.9 20.5 %collective-permute-start.1 = (bf16[4,2,128,128]{3,2,1,0:T(8,128)(2,1)}, bf16[4,2,128,128]{3,2,1,0:T(8,128)(2,1)S(1)}, u32[]{:S(2)}, u32[]{:S(2)}) collective-permute-start(bf16[4,2,128,128]{3,2,1,0:T(8,128)(2,1)} %param.10), channel_id=1, source_target_pairs={{0,8},{1,9},{8,0},{9,1},{2,10},{3,11},{10,2},{11,3},{4,12},{5,13},... | collective-permute-start | bytes 786440 | tf_op jit(solution)/shard_map/ppermute | solution.py:159
  36.2 18.2 %collective-permute-start.2 = (bf16[4,2,128,128]{3,2,1,0:T(8,128)(2,1)}, bf16[4,2,128,128]{3,2,1,0:T(8,128)(2,1)S(1)}, u32[]{:S(2)}, u32[]{:S(2)}) collective-permute-start(bf16[4,2,128,128]{3,2,1,0:T(8,128)(2,1)} %param.10), channel_id=1, source_target_pairs={{0,9},{1,8},{8,1},{9,0},{2,11},{3,10},{10,3},{11,2},{4,13},{5,12},... | collective-permute-start | bytes 786440 | tf_op jit(solution)/shard_map/ppermute | solution.py:159
  40.7 24.4 %collective-permute-start.3 = (bf16[2,2,2,128,128]{4,3,2,1,0:T(8,128)(2,1)}, bf16[2,2,2,128,128]{4,3,2,1,0:T(8,128)(2,1)S(1)}, u32[]{:S(2)}, u32[]{:S(2)}) collective-permute-start(bf16[2,2,2,128,128]{4,3,2,1,0:T(8,128)(2,1)} %strain_ref), channel_id=1, source_target_pairs={{0,2},{2,0},{4,6},{6,4},{1,3},{3,1},{5,7},{7,5},{8,10},{10,8},{12,... | collective-permute-start | bytes 786440 | tf_op jit(solution)/shard_map/ppermute | solution.py:159
  44.1 22.4 %collective-permute-start.4 = (bf16[2,2,2,128,128]{4,3,2,1,0:T(8,128)(2,1)}, bf16[2,2,2,128,128]{4,3,2,1,0:T(8,128)(2,1)S(1)}, u32[]{:S(2)}, u32[]{:S(2)}) collective-permute-start(bf16[2,2,2,128,128]{4,3,2,1,0:T(8,128)(2,1)} %strain_ref), channel_id=1, source_target_pairs={{0,4},{2,6},{4,0},{6,2},{1,5},{3,7},{5,1},{7,3},{8,12},{10,14},{12... | collective-permute-start | bytes 786440 | tf_op jit(solution)/shard_map/ppermute | solution.py:159
  50.5 4.1 %copy-start.1 = (f32[128,2,128]{2,0,1:T(8,128)}, f32[128,2,128]{2,0,1:T(8,128)S(1)}, u32[]{:S(2)}) copy-start(f32[128,2,128]{2,0,1:T(8,128)S(1)} %copy.36) | copy-start | bytes 393220
  50.5 21.5 %collective-permute-start.5 = (bf16[2,2,2,128,128]{4,3,2,1,0:T(8,128)(2,1)S(1)}, bf16[2,2,2,128,128]{4,3,2,1,0:T(8,128)(2,1)S(1)}, u32[]{:S(2)}, u32[]{:S(2)}) collective-permute-start(bf16[2,2,2,128,128]{4,3,2,1,0:T(8,128)(2,1)S(1)} %copy-done.3), channel_id=1, source_target_pairs={{0,6},{2,4},{4,2},{6,0},{1,7},{3,5},{5,3},{7,1},{8,14},{10,12},{12... | collective-permute-start | bytes 786440 | tf_op jit(solution)/shard_map/ppermute | solution.py:159
  54.4 1.0 copy-start
  107.5 0.7 copy-start.2

commit v9 on v7

--- a/solution.py
+++ b/solution.py
@@ -54,7 +54,7 @@
     return jnp.sum((h_re * h_re + h_im * h_im) * weights, axis=(1, 2))
 
 
-def search_kernel(n_tb, sidx_ref, isig_ref, strain_ref, tmpl_ref, w_ref, m1_ref, m2_ref,
+def search_kernel(n_tb, isig_ref, strain_ref, tmpl_ref, w_ref, m1_ref, m2_ref,
                   tc_ref, ts_ref, out_ref, q_ref, y_ref, z_ref, hw_ref, sd_ref):
     nb = 2 * TB
 
@@ -68,6 +68,7 @@
         return carry
 
     lax.fori_loop(0, tmpl_ref.shape[0], weigh, 0)
+    out_ref[...] = jnp.zeros(out_ref.shape, jnp.float32)
 
     def batch(i, slot):
         s = i // n_tb
@@ -105,14 +106,17 @@
                 x_im = x[r0:r0 + N1, N2:2 * N2]
                 p = (x_re * x_re + x_im * x_im) * isig_ref[2 * t + d]
                 acc = p if acc is None else acc + p
-            out_ref[s, pl.ds(t, 1), :] = jnp.max(acc, axis=0, keepdims=True)
+            best_t = jnp.max(jnp.max(acc, axis=0, keepdims=True), axis=1, keepdims=True)
+            lane = lax.broadcasted_iota(jnp.int32, (1, N2), 1)
+            row = out_ref[pl.ds(s, 1), :]
+            out_ref[pl.ds(s, 1), :] = jnp.where(lane == t, best_t, row)
 
     def step(j, carry):
         i = 2 * j
 
         @pl.when(i % n_tb == 0)
         def _():
-            seg = sidx_ref[i // n_tb]
+            seg = i // n_tb
             for d in range(2):
                 for part in range(2):
                     sd_ref[d, part] = strain_ref[seg, d, part].astype(jnp.float32)
@@ -121,12 +125,12 @@
         batch(i + 1, 1)
         return carry
 
-    lax.fori_loop(0, sidx_ref.shape[0] * n_tb // 2, step, 0)
-
-
-def run_search(sidx, isig, strain, tmpl, weights, tables):
+    lax.fori_loop(0, out_ref.shape[0] * n_tb // 2, step, 0)
+
+
+def run_search(isig, strain, tmpl, weights, tables):
     m1, m2, tc, ts = tables
-    n_s = sidx.shape[0]
+    n_s = strain.shape[0]
     n_t = tmpl.shape[0]
     n_tb = n_t // TB
     vmem = pltpu.VMEM
@@ -139,9 +143,8 @@
     )
     out = pl.pallas_call(
         functools.partial(search_kernel, n_tb),
-        out_shape=jax.ShapeDtypeStruct((n_s, n_t, N2), jnp.float32),
-        in_specs=[pl.BlockSpec(memory_space=smem), pl.BlockSpec(memory_space=smem)]
-        + [pl.BlockSpec(memory_space=vmem)] * 7,
+        out_shape=jax.ShapeDtypeStruct((n_s, N2), jnp.float32),
+        in_specs=[pl.BlockSpec(memory_space=smem)] + [pl.BlockSpec(memory_space=vmem)] * 7,
         out_specs=pl.BlockSpec(memory_space=vmem),
         scratch_shapes=[
             pltpu.VMEM((2, 2 * N1, 2 * TB * N2), jnp.bfloat16),
@@ -151,8 +154,8 @@
             pltpu.VMEM((2, 2, N1, N2), jnp.float32),
         ],
         cost_estimate=cost,
-    )(sidx, isig, strain, tmpl, weights, m1, m2, tc, ts)
-    return jnp.max(out, axis=-1)
+    )(isig, strain, tmpl, weights, m1, m2, tc, ts)
+    return out[:, :n_t]
 
 
 def swapped(x, axes, size, k):
@@ -184,11 +187,9 @@
     isig = (1.0 / sigma2).reshape(-1)
 
     own_count = strain.shape[0]
-    own_idx = jnp.arange(own_count, dtype=jnp.int32)
-    own_rows = run_search(own_idx, isig, strain, tmpl_rel, weights, tables)
+    own_rows = run_search(isig, strain, tmpl_rel, weights, tables)
     own_rows, piece = lax.optimization_barrier((own_rows, piece))
-    other_idx = jnp.arange(piece.shape[0], dtype=jnp.int32)
-    other_rows = run_search(other_idx, isig, piece, tmpl_rel, weights, tables)
+    other_rows = run_search(isig, piece, tmpl_rel, weights, tables)
     slots = jnp.concatenate([own_rows, other_rows], 0).reshape(n_ya, own_count, -1)
 
     lanes = jnp.arange(n_ya, dtype=jnp.int32)

time: 108 us -> 108 us (level)
  Pallas kernels: 25.5 us -> 26.6 us
    reduce_max x2 -> x0, other arithmetic: 1.68 us -> none  [run_search(): return jnp.max(out, axis=-1)]
    pallas_call x2, Pallas kernels: 25.5 us -> 26.6 us  [run_search(): pl.pallas_call(functools.partial(search_kernel, n_tb), out_shape=jax.Shap...]
  transfers between devices with their start and end apart: 7 -> 7, of which waited for: 3 -> 3; matrix products, arithmetic and copies ran while one was open for 3% -> 2% of each run, Pallas kernels for 7% -> 7%
where the time goes in v9:
time: 108 us
  starting transfers between devices  28.5 us (26%)
  blocking collectives  28.2 us (26%)
  Pallas kernels  26.6 us (25%)
  waiting for transfers between devices  15.7 us (15%)
  local copies, waits for them, and re-layouts  4.03 us (4%)
  other arithmetic  3.71 us (3%)
    all_gather x5, blocking collectives, body(): gathered = lax.all_gather(gathered, axis, axis=0, tiled=True)  28.2 us
    pallas_call x2, Pallas kernels, run_search(): pl.pallas_call(functools.partial(search_kernel, n_tb), out_shape=jax.Shap...  26.6 us
    ppermute x6, starting transfers between devices, swapped(): return lax.ppermute(x, axes, [(i, i ^ k) for i in range(size)])  24 us
    ppermute x6, waiting for transfers between devices, swapped(): return lax.ppermute(x, axes, [(i, i ^ k) for i in range(size)])  8.04 us
    all_to_all x1, waiting for transfers between devices, body(): lax.all_to_all(grouped, 'ya', split_axis=0, concat_axis=0, tiled=True)  7.68 us
    all_to_all x1, starting transfers between devices, body(): lax.all_to_all(grouped, 'ya', split_axis=0, concat_axis=0, tiled=True)  4.55 us
  transfers between devices with their start and end apart: 7, of which 3 were waited for; matrix products, arithmetic and copies ran while one was open for 2% of the time, Pallas kernels for 7%

profile of v9, /device:TPU:8, one launch (start us, length us, event | category | flops | bytes accessed | tf_op | source)
XLA Modules:
  0.0 107.7 jit_solution(4283262262429743950)
XLA Ops:
  0.6 0.0 copy-start.4
  0.6 0.0 copy-start.5
  0.7 2.1 %all-gather = f32[2,4,256]{2,1,0:T(4,128)S(1)} all-gather(f32[1,4,256]{2,1,0:T(4,128)} %bitcast.25), channel_id=1, replica_groups=mesh['sx'=2,'zh'=2,'z1'=2,'z0'=2,'sc'=2,'xh'=2,'ya'=4,'yb'=2] {'sc'}, dimensions={0}, use_global_device_ids=true | all-gather | bytes 12288 | tf_op jit(solution)/shard_map/all_gather | solution.py:176
  2.7 4.7 %all_gather.16 = f32[16,256]{1,0:T(8,128)S(1)} all-gather(f32[8,256]{1,0:T(8,128)S(1)} %reshape.127), channel_id=1, replica_groups=mesh['sx'=2,'zh'=2,'z1'=2,'z0'=2,'sc'=2,'xh'=2,'ya'=4,'yb'=2] {'z0'}, dimensions={0}, use_global_device_ids=true | all-gather | bytes 24576 | tf_op jit(solution)/shard_map/all_gather | solution.py:176
  7.4 6.5 %all_gather.17 = f32[32,256]{1,0:T(8,128)S(1)} all-gather(f32[16,256]{1,0:T(8,128)S(1)} %all_gather.16), channel_id=1, replica_groups=mesh['sx'=2,'zh'=2,'z1'=2,'z0'=2,'sc'=2,'xh'=2,'ya'=4,'yb'=2] {'z1'}, dimensions={0}, use_global_device_ids=true | all-gather | bytes 49152 | tf_op jit(solution)/shard_map/all_gather | solution.py:176
  14.0 10.0 %all_gather.18 = f32[64,256]{1,0:T(8,128)S(1)} all-gather(f32[32,256]{1,0:T(8,128)S(1)} %all_gather.17), channel_id=1, replica_groups=mesh['sx'=2,'zh'=2,'z1'=2,'z0'=2,'sc'=2,'xh'=2,'ya'=4,'yb'=2] {'zh'}, dimensions={0}, use_global_device_ids=true | all-gather | bytes 98304 | tf_op jit(solution)/shard_map/all_gather | solution.py:176
  24.0 4.9 %all_gather.19 = f32[128,256]{1,0:T(8,128)S(1)} all-gather(f32[64,256]{1,0:T(8,128)S(1)} %all_gather.18), channel_id=1, replica_groups=mesh['sx'=2,'zh'=2,'z1'=2,'z0'=2,'sc'=2,'xh'=2,'ya'=4,'yb'=2] {'sx'}, dimensions={0}, use_global_device_ids=true | all-gather | bytes 196608 | tf_op jit(solution)/shard_map/all_gather | solution.py:176
  28.9 5.0 %collective-permute-start = (bf16[4,2,128,128]{3,2,1,0:T(8,128)(2,1)}, bf16[4,2,128,128]{3,2,1,0:T(8,128)(2,1)S(1)}, u32[]{:S(2)}, u32[]{:S(2)}) collective-permute-start(bf16[4,2,128,128]{3,2,1,0:T(8,128)(2,1)} %param.10), channel_id=1, source_target_pairs={{0,1},{1,0},{8,9},{9,8},{2,3},{3,2},{10,11},{11,10},{4,5},{5,4},{1... | collective-permute-start | bytes 786440 | tf_op jit(solution)/shard_map/ppermute | solution.py:162
  33.9 2.3 %collective-permute-start.1 = (bf16[4,2,128,128]{3,2,1,0:T(8,128)(2,1)}, bf16[4,2,128,128]{3,2,1,0:T(8,128)(2,1)S(1)}, u32[]{:S(2)}, u32[]{:S(2)}) collective-permute-start(bf16[4,2,128,128]{3,2,1,0:T(8,128)(2,1)} %param.10), channel_id=1, source_target_pairs={{0,8},{1,9},{8,0},{9,1},{2,10},{3,11},{10,2},{11,3},{4,12},{5,13},... | collective-permute-start | bytes 786440 | tf_op jit(solution)/shard_map/ppermute | solution.py:162
  36.2 4.5 %collective-permute-start.2 = (bf16[4,2,128,128]{3,2,1,0:T(8,128)(2,1)}, bf16[4,2,128,128]{3,2,1,0:T(8,128)(2,1)S(1)}, u32[]{:S(2)}, u32[]{:S(2)}) collective-permute-start(bf16[4,2,128,128]{3,2,1,0:T(8,128)(2,1)} %param.10), channel_id=1, source_target_pairs={{0,9},{1,8},{8,1},{9,0},{2,11},{3,10},{10,3},{11,2},{4,13},{5,12},... | collective-permute-start | bytes 786440 | tf_op jit(solution)/shard_map/ppermute | solution.py:162
  40.7 3.4 %collective-permute-start.3 = (bf16[2,2,2,128,128]{4,3,2,1,0:T(8,128)(2,1)}, bf16[2,2,2,128,128]{4,3,2,1,0:T(8,128)(2,1)S(1)}, u32[]{:S(2)}, u32[]{:S(2)}) collective-permute-start(bf16[2,2,2,128,128]{4,3,2,1,0:T(8,128)(2,1)} %strain_ref), channel_id=1, source_target_pairs={{0,2},{2,0},{4,6},{6,4},{1,3},{3,1},{5,7},{7,5},{8,10},{10,8},{12,... | collective-permute-start | bytes 786440 | tf_op jit(solution)/shard_map/ppermute | solution.py:162
  44.1 5.0 %collective-permute-start.4 = (bf16[2,2,2,128,128]{4,3,2,1,0:T(8,128)(2,1)}, bf16[2,2,2,128,128]{4,3,2,1,0:T(8,128)(2,1)S(1)}, u32[]{:S(2)}, u32[]{:S(2)}) collective-permute-start(bf16[2,2,2,128,128]{4,3,2,1,0:T(8,128)(2,1)} %strain_ref), channel_id=1, source_target_pairs={{0,4},{2,6},{4,0},{6,2},{1,5},{3,7},{5,1},{7,3},{8,12},{10,14},{12... | collective-permute-start | bytes 786440 | tf_op jit(solution)/shard_map/ppermute | solution.py:162
  49.2 1.0 constant_dynamic-update-slice_fusion.3
  50.2 0.0 copy-done.5
  50.3 0.1 copy.26
  50.4 0.1 copy.27
  50.5 0.0 copy-start.1
  50.5 0.0 collective-permute-done
  50.5 0.0 copy-done.4
  50.5 3.7 %collective-permute-start.5 = (bf16[2,2,2,128,128]{4,3,2,1,0:T(8,128)(2,1)S(1)}, bf16[2,2,2,128,128]{4,3,2,1,0:T(8,128)(2,1)S(1)}, u32[]{:S(2)}, u32[]{:S(2)}) collective-permute-start(bf16[2,2,2,128,128]{4,3,2,1,0:T(8,128)(2,1)S(1)} %copy-done.4), channel_id=1, source_target_pairs={{0,6},{2,4},{4,2},{6,0},{1,7},{3,5},{5,3},{7,1},{8,14},{10,12},{12... | collective-permute-start | bytes 786440 | tf_op jit(solution)/shard_map/ppermute | solution.py:162
  54.3 0.0 collective-permute-done.1
  54.4 0.0 collective-permute-done.2
  54.4 0.0 copy-start
  54.4 0.2 add_bitcast_fusion
  54.6 0.8 copy-done
  55.4 0.0 copy-done.1
  55.4 0.3 multiply_reduce_fusion
  55.7 0.6 div.26.isig_ref
  56.3 7.8 %shard_map.104 = f32[2,128]{1,0:T(2,128)} custom-call(f32[32]{0:T(128)} %div.26.isig_ref, bf16[2,2,2,128,128]{4,3,2,1,0:T(8,128)(2,1)} %strain_ref, bf16[16,2,128,128]{3,2,1,0:T(8,128)(2,1)} %copy-done, f32[2,128,128]{2,1,0:T(8,128)} %bitcast.19, bf16[256,256]{1,0:T(8,128)(2,1)} %constant.57.clone.m1_ref, bf16[256,256]{1,0:T(8,128)(2,1)} %constant.58.clone.m2_ref, ...), custom_call_target="tpu_custom_call" | custom-call | flops 2147483648 | bytes 1441792 | tf_op jit(solution)/shard_map/pallas_call | solution.py:144
  64.0 0.0 collective-permute-done.3
  64.0 2.4 %collective-permute-done.4 = bf16[2,2,2,128,128]{4,3,2,1,0:T(8,128)(2,1)S(1)} collective-permute-done((bf16[2,2,2,128,128]{4,3,2,1,0:T(8,128)(2,1)}, bf16[2,2,2,128,128]{4,3,2,1,0:T(8,128)(2,1)S(1)}, u32[]{:S(2)}, u32[]{:S(2)}) %collective-permute-start.4) | collective-permute-done | bytes 262176 | tf_op jit(solution)/shard_map/ppermute | solution.py:162
  66.5 5.6 %collective-permute-done.5 = bf16[2,2,2,128,128]{4,3,2,1,0:T(8,128)(2,1)S(1)} collective-permute-done((bf16[2,2,2,128,128]{4,3,2,1,0:T(8,128)(2,1)S(1)}, bf16[2,2,2,128,128]{4,3,2,1,0:T(8,128)(2,1)S(1)}, u32[]{:S(2)}, u32[]{:S(2)}) %collective-permute-start.5) | collective-permute-done | bytes 262176 | tf_op jit(solution)/shard_map/ppermute | solution.py:162
  72.0 1.0 pad_maximum_fusion.strain_ref
  73.1 18.8 %shard_map.105 = f32[6,128]{1,0:T(8,128)} custom-call(f32[32]{0:T(128)} %div.26.isig_ref, bf16[6,2,2,128,128]{4,3,2,1,0:T(8,128)(2,1)} %pad_maximum_fusion.strain_ref, bf16[16,2,128,128]{3,2,1,0:T(8,128)(2,1)} %copy-done, f32[2,128,128]{2,1,0:T(8,128)} %bitcast.20, bf16[256,256]{1,0:T(8,128)(2,1)} %constant.57.clone.m1_ref, ...), custom_call_target="tpu_custom_call" | custom-call | flops 6442450944 | bytes 1966080 | tf_op jit(solution)/shard_map/pallas_call | solution.py:144
  91.9 0.0 copy-done.3
  91.9 0.7 pad_maximum_fusion.1
  92.6 0.6 gather_fusion
  93.2 0.7 broadcast_select_fusion
  93.8 4.6 %all-to-all-start = ((f32[4,2,16]{2,1,0:T(2,128)}), f32[4,2,16]{2,1,0:T(2,128)S(1)}, u32[]{:S(2)}, u32[]{:S(2)}) async-start(f32[4,2,16]{2,1,0:T(2,128)} %broadcast_select_fusion), calls=%async_computation | async-start | bytes 8192 | tf_op jit(solution)/shard_map/all_to_all | solution.py:197
  98.4 0.0 copy-done.6
  98.4 7.7 %all-to-all-done = f32[4,2,16]{2,1,0:T(2,128)S(1)} async-done(((f32[4,2,16]{2,1,0:T(2,128)}), f32[4,2,16]{2,1,0:T(2,128)S(1)}, u32[]{:S(2)}, u32[]{:S(2)}) %all-to-all-start) | async-done | bytes 544 | tf_op jit(solution)/shard_map/all_to_all | solution.py:197
  106.1 0.1 reshape.109
  106.2 0.6 gather_fusion.1
  106.8 0.1 sqrt_bitcast_fusion
  106.9 0.1 sqrt.15
  107.0 0.1 broadcast_multiply_fusion
  107.0 0.7 select_reduce_fusion
  107.7 0.0 copy-done.2
  (20 shorter events, 0.2 us)
Async XLA Ops:
  0.6 49.9 %copy-start.4 = (bf16[2,2,2,128,128]{4,3,2,1,0:T(8,128)(2,1)S(1)}, bf16[2,2,2,128,128]{4,3,2,1,0:T(8,128)(2,1)}, u32[]{:S(2)}) copy-start(bf16[2,2,2,128,128]{4,3,2,1,0:T(8,128)(2,1)} %strain_ref) | copy-start | bytes 786436
  0.6 49.6 %copy-start.5 = (s32[64]{0:T(128)S(1)}, s32[64]{0:T(128)}, u32[]{:S(2)}) copy-start(s32[64]{0:T(128)} %param.13) | copy-start | bytes 772
  28.9 21.6 %collective-permute-start = (bf16[4,2,128,128]{3,2,1,0:T(8,128)(2,1)}, bf16[4,2,128,128]{3,2,1,0:T(8,128)(2,1)S(1)}, u32[]{:S(2)}, u32[]{:S(2)}) collective-permute-start(bf16[4,2,128,128]{3,2,1,0:T(8,128)(2,1)} %param.10), channel_id=1, source_target_pairs={{0,1},{1,0},{8,9},{9,8},{2,3},{3,2},{10,11},{11,10},{4,5},{5,4},{1... | collective-permute-start | bytes 786440 | tf_op jit(solution)/shard_map/ppermute | solution.py:162
  33.9 20.5 %collective-permute-start.1 = (bf16[4,2,128,128]{3,2,1,0:T(8,128)(2,1)}, bf16[4,2,128,128]{3,2,1,0:T(8,128)(2,1)S(1)}, u32[]{:S(2)}, u32[]{:S(2)}) collective-permute-start(bf16[4,2,128,128]{3,2,1,0:T(8,128)(2,1)} %param.10), channel_id=1, source_target_pairs={{0,8},{1,9},{8,0},{9,1},{2,10},{3,11},{10,2},{11,3},{4,12},{5,13},... | collective-permute-start | bytes 786440 | tf_op jit(solution)/shard_map/ppermute | solution.py:162
  36.2 18.2 %collective-permute-start.2 = (bf16[4,2,128,128]{3,2,1,0:T(8,128)(2,1)}, bf16[4,2,128,128]{3,2,1,0:T(8,128)(2,1)S(1)}, u32[]{:S(2)}, u32[]{:S(2)}) collective-permute-start(bf16[4,2,128,128]{3,2,1,0:T(8,128)(2,1)} %param.10), channel_id=1, source_target_pairs={{0,9},{1,8},{8,1},{9,0},{2,11},{3,10},{10,3},{11,2},{4,13},{5,12},... | collective-permute-start | bytes 786440 | tf_op jit(solution)/shard_map/ppermute | solution.py:162
  40.7 23.3 %collective-permute-start.3 = (bf16[2,2,2,128,128]{4,3,2,1,0:T(8,128)(2,1)}, bf16[2,2,2,128,128]{4,3,2,1,0:T(8,128)(2,1)S(1)}, u32[]{:S(2)}, u32[]{:S(2)}) collective-permute-start(bf16[2,2,2,128,128]{4,3,2,1,0:T(8,128)(2,1)} %strain_ref), channel_id=1, source_target_pairs={{0,2},{2,0},{4,6},{6,4},{1,3},{3,1},{5,7},{7,5},{8,10},{10,8},{12,... | collective-permute-start | bytes 786440 | tf_op jit(solution)/shard_map/ppermute | solution.py:162
  44.1 22.3 %collective-permute-start.4 = (bf16[2,2,2,128,128]{4,3,2,1,0:T(8,128)(2,1)}, bf16[2,2,2,128,128]{4,3,2,1,0:T(8,128)(2,1)S(1)}, u32[]{:S(2)}, u32[]{:S(2)}) collective-permute-start(bf16[2,2,2,128,128]{4,3,2,1,0:T(8,128)(2,1)} %strain_ref), channel_id=1, source_target_pairs={{0,4},{2,6},{4,0},{6,2},{1,5},{3,7},{5,1},{7,3},{8,12},{10,14},{12... | collective-permute-start | bytes 786440 | tf_op jit(solution)/shard_map/ppermute | solution.py:162
  50.5 4.9 %copy-start.1 = (f32[128,2,128]{2,0,1:T(8,128)}, f32[128,2,128]{2,0,1:T(8,128)S(1)}, u32[]{:S(2)}) copy-start(f32[128,2,128]{2,0,1:T(8,128)S(1)} %copy.27) | copy-start | bytes 393220
  50.5 21.5 %collective-permute-start.5 = (bf16[2,2,2,128,128]{4,3,2,1,0:T(8,128)(2,1)S(1)}, bf16[2,2,2,128,128]{4,3,2,1,0:T(8,128)(2,1)S(1)}, u32[]{:S(2)}, u32[]{:S(2)}) collective-permute-start(bf16[2,2,2,128,128]{4,3,2,1,0:T(8,128)(2,1)S(1)} %copy-done.4), channel_id=1, source_target_pairs={{0,6},{2,4},{4,2},{6,0},{1,7},{3,5},{5,3},{7,1},{8,14},{10,12},{12... | collective-permute-start | bytes 786440 | tf_op jit(solution)/shard_map/ppermute | solution.py:162
  54.4 1.0 copy-start
  73.1 18.8 %copy-start.3 = (f32[2,128]{1,0:T(2,128)S(1)}, f32[2,128]{1,0:T(2,128)}, u32[]{:S(2)}) copy-start(f32[2,128]{1,0:T(2,128)} %shard_map.104) | copy-start | bytes 3076
  73.1 25.3 %copy-start.6 = (s32[2]{0:T(128)S(1)}, s32[2]{0:T(128)}, u32[]{:S(2)}) copy-start(s32[2]{0:T(128)} %param.12) | copy-start | bytes 28
  93.8 12.3 %all-to-all-start = ((f32[4,2,16]{2,1,0:T(2,128)}), f32[4,2,16]{2,1,0:T(2,128)S(1)}, u32[]{:S(2)}, u32[]{:S(2)}) async-start(f32[4,2,16]{2,1,0:T(2,128)} %broadcast_select_fusion), calls=%async_computation | async-start | bytes 8192 | tf_op jit(solution)/shard_map/all_to_all | solution.py:197
  107.0 0.7 copy-start.2

commit v10 on v9

--- a/solution.py
+++ b/solution.py
@@ -14,7 +14,7 @@
 N2 = 128
 BINS = 16384
 BLOCKS = 8
-TB = 4
+TB = 8
 
 
 def make_tables():

time: 108 us -> 107 us (level)
  Pallas kernels: 26.6 us -> 25.1 us
    pallas_call x2, Pallas kernels: 26.6 us -> 25.1 us  [run_search(): pl.pallas_call(functools.partial(search_kernel, n_tb), out_shape=jax.Shap...]
where the time goes in v10:
time: 107 us
  starting transfers between devices  28.5 us (27%)
  blocking collectives  28.2 us (26%)
  Pallas kernels  25.1 us (23%)
  waiting for transfers between devices  16.1 us (15%)
  local copies, waits for them, and re-layouts  4.03 us (4%)
  other arithmetic  3.71 us (3%)
    all_gather x5, blocking collectives, body(): gathered = lax.all_gather(gathered, axis, axis=0, tiled=True)  28.2 us
    pallas_call x2, Pallas kernels, run_search(): pl.pallas_call(functools.partial(search_kernel, n_tb), out_shape=jax.Shap...  25.1 us
    ppermute x6, starting transfers between devices, swapped(): return lax.ppermute(x, axes, [(i, i ^ k) for i in range(size)])  24 us
    ppermute x6, waiting for transfers between devices, swapped(): return lax.ppermute(x, axes, [(i, i ^ k) for i in range(size)])  8.4 us
    all_to_all x1, waiting for transfers between devices, body(): lax.all_to_all(grouped, 'ya', split_axis=0, concat_axis=0, tiled=True)  7.68 us
    all_to_all x1, starting transfers between devices, body(): lax.all_to_all(grouped, 'ya', split_axis=0, concat_axis=0, tiled=True)  4.56 us
  transfers between devices with their start and end apart: 7, of which 3 were waited for; matrix products, arithmetic and copies ran while one was open for 2% of the time, Pallas kernels for 7%

profile of v10, /device:TPU:8, one launch (start us, length us, event | category | flops | bytes accessed | tf_op | source)
XLA Modules:
  0.0 106.6 jit_solution(14652235888398132738)
XLA Ops:
  0.6 0.0 copy-start.4
  0.6 0.0 copy-start.5
  0.7 2.1 %all-gather = f32[2,4,256]{2,1,0:T(4,128)S(1)} all-gather(f32[1,4,256]{2,1,0:T(4,128)} %bitcast.25), channel_id=1, replica_groups=mesh['sx'=2,'zh'=2,'z1'=2,'z0'=2,'sc'=2,'xh'=2,'ya'=4,'yb'=2] {'sc'}, dimensions={0}, use_global_device_ids=true | all-gather | bytes 12288 | tf_op jit(solution)/shard_map/all_gather | solution.py:176
  2.7 4.7 %all_gather.16 = f32[16,256]{1,0:T(8,128)S(1)} all-gather(f32[8,256]{1,0:T(8,128)S(1)} %reshape.127), channel_id=1, replica_groups=mesh['sx'=2,'zh'=2,'z1'=2,'z0'=2,'sc'=2,'xh'=2,'ya'=4,'yb'=2] {'z0'}, dimensions={0}, use_global_device_ids=true | all-gather | bytes 24576 | tf_op jit(solution)/shard_map/all_gather | solution.py:176
  7.4 6.5 %all_gather.17 = f32[32,256]{1,0:T(8,128)S(1)} all-gather(f32[16,256]{1,0:T(8,128)S(1)} %all_gather.16), channel_id=1, replica_groups=mesh['sx'=2,'zh'=2,'z1'=2,'z0'=2,'sc'=2,'xh'=2,'ya'=4,'yb'=2] {'z1'}, dimensions={0}, use_global_device_ids=true | all-gather | bytes 49152 | tf_op jit(solution)/shard_map/all_gather | solution.py:176
  14.0 10.0 %all_gather.18 = f32[64,256]{1,0:T(8,128)S(1)} all-gather(f32[32,256]{1,0:T(8,128)S(1)} %all_gather.17), channel_id=1, replica_groups=mesh['sx'=2,'zh'=2,'z1'=2,'z0'=2,'sc'=2,'xh'=2,'ya'=4,'yb'=2] {'zh'}, dimensions={0}, use_global_device_ids=true | all-gather | bytes 98304 | tf_op jit(solution)/shard_map/all_gather | solution.py:176
  24.0 4.9 %all_gather.19 = f32[128,256]{1,0:T(8,128)S(1)} all-gather(f32[64,256]{1,0:T(8,128)S(1)} %all_gather.18), channel_id=1, replica_groups=mesh['sx'=2,'zh'=2,'z1'=2,'z0'=2,'sc'=2,'xh'=2,'ya'=4,'yb'=2] {'sx'}, dimensions={0}, use_global_device_ids=true | all-gather | bytes 196608 | tf_op jit(solution)/shard_map/all_gather | solution.py:176
  28.9 5.0 %collective-permute-start = (bf16[4,2,128,128]{3,2,1,0:T(8,128)(2,1)}, bf16[4,2,128,128]{3,2,1,0:T(8,128)(2,1)S(1)}, u32[]{:S(2)}, u32[]{:S(2)}) collective-permute-start(bf16[4,2,128,128]{3,2,1,0:T(8,128)(2,1)} %param.10), channel_id=1, source_target_pairs={{0,1},{1,0},{8,9},{9,8},{2,3},{3,2},{10,11},{11,10},{4,5},{5,4},{1... | collective-permute-start | bytes 786440 | tf_op jit(solution)/shard_map/ppermute | solution.py:162
  33.9 2.3 %collective-permute-start.1 = (bf16[4,2,128,128]{3,2,1,0:T(8,128)(2,1)}, bf16[4,2,128,128]{3,2,1,0:T(8,128)(2,1)S(1)}, u32[]{:S(2)}, u32[]{:S(2)}) collective-permute-start(bf16[4,2,128,128]{3,2,1,0:T(8,128)(2,1)} %param.10), channel_id=1, source_target_pairs={{0,8},{1,9},{8,0},{9,1},{2,10},{3,11},{10,2},{11,3},{4,12},{5,13},... | collective-permute-start | bytes 786440 | tf_op jit(solution)/shard_map/ppermute | solution.py:162
  36.2 4.5 %collective-permute-start.2 = (bf16[4,2,128,128]{3,2,1,0:T(8,128)(2,1)}, bf16[4,2,128,128]{3,2,1,0:T(8,128)(2,1)S(1)}, u32[]{:S(2)}, u32[]{:S(2)}) collective-permute-start(bf16[4,2,128,128]{3,2,1,0:T(8,128)(2,1)} %param.10), channel_id=1, source_target_pairs={{0,9},{1,8},{8,1},{9,0},{2,11},{3,10},{10,3},{11,2},{4,13},{5,12},... | collective-permute-start | bytes 786440 | tf_op jit(solution)/shard_map/ppermute | solution.py:162
  40.7 3.4 %collective-permute-start.3 = (bf16[2,2,2,128,128]{4,3,2,1,0:T(8,128)(2,1)}, bf16[2,2,2,128,128]{4,3,2,1,0:T(8,128)(2,1)S(1)}, u32[]{:S(2)}, u32[]{:S(2)}) collective-permute-start(bf16[2,2,2,128,128]{4,3,2,1,0:T(8,128)(2,1)} %strain_ref), channel_id=1, source_target_pairs={{0,2},{2,0},{4,6},{6,4},{1,3},{3,1},{5,7},{7,5},{8,10},{10,8},{12,... | collective-permute-start | bytes 786440 | tf_op jit(solution)/shard_map/ppermute | solution.py:162
  44.1 5.0 %collective-permute-start.4 = (bf16[2,2,2,128,128]{4,3,2,1,0:T(8,128)(2,1)}, bf16[2,2,2,128,128]{4,3,2,1,0:T(8,128)(2,1)S(1)}, u32[]{:S(2)}, u32[]{:S(2)}) collective-permute-start(bf16[2,2,2,128,128]{4,3,2,1,0:T(8,128)(2,1)} %strain_ref), channel_id=1, source_target_pairs={{0,4},{2,6},{4,0},{6,2},{1,5},{3,7},{5,1},{7,3},{8,12},{10,14},{12... | collective-permute-start | bytes 786440 | tf_op jit(solution)/shard_map/ppermute | solution.py:162
  49.2 1.0 constant_dynamic-update-slice_fusion.3
  50.2 0.0 copy-done.5
  50.3 0.1 copy.26
  50.4 0.1 copy.27
  50.5 0.0 copy-start.1
  50.5 0.0 collective-permute-done
  50.5 0.0 copy-done.4
  50.5 3.7 %collective-permute-start.5 = (bf16[2,2,2,128,128]{4,3,2,1,0:T(8,128)(2,1)S(1)}, bf16[2,2,2,128,128]{4,3,2,1,0:T(8,128)(2,1)S(1)}, u32[]{:S(2)}, u32[]{:S(2)}) collective-permute-start(bf16[2,2,2,128,128]{4,3,2,1,0:T(8,128)(2,1)S(1)} %copy-done.4), channel_id=1, source_target_pairs={{0,6},{2,4},{4,2},{6,0},{1,7},{3,5},{5,3},{7,1},{8,14},{10,12},{12... | collective-permute-start | bytes 786440 | tf_op jit(solution)/shard_map/ppermute | solution.py:162
  54.3 0.0 collective-permute-done.1
  54.4 0.0 collective-permute-done.2
  54.4 0.0 copy-start
  54.4 0.2 add_bitcast_fusion
  54.6 0.8 copy-done
  55.4 0.0 copy-done.1
  55.4 0.3 multiply_reduce_fusion
  55.7 0.6 div.26.isig_ref
  56.3 7.4 %shard_map.104 = f32[2,128]{1,0:T(2,128)} custom-call(f32[32]{0:T(128)} %div.26.isig_ref, bf16[2,2,2,128,128]{4,3,2,1,0:T(8,128)(2,1)} %strain_ref, bf16[16,2,128,128]{3,2,1,0:T(8,128)(2,1)} %copy-done, f32[2,128,128]{2,1,0:T(8,128)} %bitcast.19, bf16[256,256]{1,0:T(8,128)(2,1)} %constant.57.clone.m1_ref, bf16[256,256]{1,0:T(8,128)(2,1)} %constant.58.clone.m2_ref, ...), custom_call_target="tpu_custom_call" | custom-call | flops 2147483648 | bytes 1441792 | tf_op jit(solution)/shard_map/pallas_call | solution.py:144
  63.7 0.0 collective-permute-done.3
  63.7 2.8 %collective-permute-done.4 = bf16[2,2,2,128,128]{4,3,2,1,0:T(8,128)(2,1)S(1)} collective-permute-done((bf16[2,2,2,128,128]{4,3,2,1,0:T(8,128)(2,1)}, bf16[2,2,2,128,128]{4,3,2,1,0:T(8,128)(2,1)S(1)}, u32[]{:S(2)}, u32[]{:S(2)}) %collective-permute-start.4) | collective-permute-done | bytes 262176 | tf_op jit(solution)/shard_map/ppermute | solution.py:162
  66.5 5.6 %collective-permute-done.5 = bf16[2,2,2,128,128]{4,3,2,1,0:T(8,128)(2,1)S(1)} collective-permute-done((bf16[2,2,2,128,128]{4,3,2,1,0:T(8,128)(2,1)S(1)}, bf16[2,2,2,128,128]{4,3,2,1,0:T(8,128)(2,1)S(1)}, u32[]{:S(2)}, u32[]{:S(2)}) %collective-permute-start.5) | collective-permute-done | bytes 262176 | tf_op jit(solution)/shard_map/ppermute | solution.py:162
  72.0 1.0 pad_maximum_fusion.strain_ref
  73.1 17.7 %shard_map.105 = f32[6,128]{1,0:T(8,128)} custom-call(f32[32]{0:T(128)} %div.26.isig_ref, bf16[6,2,2,128,128]{4,3,2,1,0:T(8,128)(2,1)} %pad_maximum_fusion.strain_ref, bf16[16,2,128,128]{3,2,1,0:T(8,128)(2,1)} %copy-done, f32[2,128,128]{2,1,0:T(8,128)} %bitcast.20, bf16[256,256]{1,0:T(8,128)(2,1)} %constant.57.clone.m1_ref, ...), custom_call_target="tpu_custom_call" | custom-call | flops 6442450944 | bytes 1966080 | tf_op jit(solution)/shard_map/pallas_call | solution.py:144
  90.8 0.0 copy-done.3
  90.8 0.7 pad_maximum_fusion.1
  91.5 0.6 gather_fusion
  92.0 0.7 broadcast_select_fusion
  92.7 4.6 %all-to-all-start = ((f32[4,2,16]{2,1,0:T(2,128)}), f32[4,2,16]{2,1,0:T(2,128)S(1)}, u32[]{:S(2)}, u32[]{:S(2)}) async-start(f32[4,2,16]{2,1,0:T(2,128)} %broadcast_select_fusion), calls=%async_computation | async-start | bytes 8192 | tf_op jit(solution)/shard_map/all_to_all | solution.py:197
  97.3 0.0 copy-done.6
  97.3 7.7 %all-to-all-done = f32[4,2,16]{2,1,0:T(2,128)S(1)} async-done(((f32[4,2,16]{2,1,0:T(2,128)}), f32[4,2,16]{2,1,0:T(2,128)S(1)}, u32[]{:S(2)}, u32[]{:S(2)}) %all-to-all-start) | async-done | bytes 544 | tf_op jit(solution)/shard_map/all_to_all | solution.py:197
  105.0 0.1 reshape.109
  105.0 0.6 gather_fusion.1
  105.6 0.1 sqrt_bitcast_fusion
  105.7 0.1 sqrt.15
  105.8 0.1 broadcast_multiply_fusion
  105.9 0.7 select_reduce_fusion
  106.6 0.0 copy-done.2
  (20 shorter events, 0.2 us)
Async XLA Ops:
  0.6 49.9 %copy-start.4 = (bf16[2,2,2,128,128]{4,3,2,1,0:T(8,128)(2,1)S(1)}, bf16[2,2,2,128,128]{4,3,2,1,0:T(8,128)(2,1)}, u32[]{:S(2)}) copy-start(bf16[2,2,2,128,128]{4,3,2,1,0:T(8,128)(2,1)} %strain_ref) | copy-start | bytes 786436
  0.6 49.6 %copy-start.5 = (s32[64]{0:T(128)S(1)}, s32[64]{0:T(128)}, u32[]{:S(2)}) copy-start(s32[64]{0:T(128)} %param.13) | copy-start | bytes 772
  28.9 21.6 %collective-permute-start = (bf16[4,2,128,128]{3,2,1,0:T(8,128)(2,1)}, bf16[4,2,128,128]{3,2,1,0:T(8,128)(2,1)S(1)}, u32[]{:S(2)}, u32[]{:S(2)}) collective-permute-start(bf16[4,2,128,128]{3,2,1,0:T(8,128)(2,1)} %param.10), channel_id=1, source_target_pairs={{0,1},{1,0},{8,9},{9,8},{2,3},{3,2},{10,11},{11,10},{4,5},{5,4},{1... | collective-permute-start | bytes 786440 | tf_op jit(solution)/shard_map/ppermute | solution.py:162
  33.9 20.5 %collective-permute-start.1 = (bf16[4,2,128,128]{3,2,1,0:T(8,128)(2,1)}, bf16[4,2,128,128]{3,2,1,0:T(8,128)(2,1)S(1)}, u32[]{:S(2)}, u32[]{:S(2)}) collective-permute-start(bf16[4,2,128,128]{3,2,1,0:T(8,128)(2,1)} %param.10), channel_id=1, source_target_pairs={{0,8},{1,9},{8,0},{9,1},{2,10},{3,11},{10,2},{11,3},{4,12},{5,13},... | collective-permute-start | bytes 786440 | tf_op jit(solution)/shard_map/ppermute | solution.py:162
  36.2 18.2 %collective-permute-start.2 = (bf16[4,2,128,128]{3,2,1,0:T(8,128)(2,1)}, bf16[4,2,128,128]{3,2,1,0:T(8,128)(2,1)S(1)}, u32[]{:S(2)}, u32[]{:S(2)}) collective-permute-start(bf16[4,2,128,128]{3,2,1,0:T(8,128)(2,1)} %param.10), channel_id=1, source_target_pairs={{0,9},{1,8},{8,1},{9,0},{2,11},{3,10},{10,3},{11,2},{4,13},{5,12},... | collective-permute-start | bytes 786440 | tf_op jit(solution)/shard_map/ppermute | solution.py:162
  40.7 23.0 %collective-permute-start.3 = (bf16[2,2,2,128,128]{4,3,2,1,0:T(8,128)(2,1)}, bf16[2,2,2,128,128]{4,3,2,1,0:T(8,128)(2,1)S(1)}, u32[]{:S(2)}, u32[]{:S(2)}) collective-permute-start(bf16[2,2,2,128,128]{4,3,2,1,0:T(8,128)(2,1)} %strain_ref), channel_id=1, source_target_pairs={{0,2},{2,0},{4,6},{6,4},{1,3},{3,1},{5,7},{7,5},{8,10},{10,8},{12,... | collective-permute-start | bytes 786440 | tf_op jit(solution)/shard_map/ppermute | solution.py:162
  44.1 22.3 %collective-permute-start.4 = (bf16[2,2,2,128,128]{4,3,2,1,0:T(8,128)(2,1)}, bf16[2,2,2,128,128]{4,3,2,1,0:T(8,128)(2,1)S(1)}, u32[]{:S(2)}, u32[]{:S(2)}) collective-permute-start(bf16[2,2,2,128,128]{4,3,2,1,0:T(8,128)(2,1)} %strain_ref), channel_id=1, source_target_pairs={{0,4},{2,6},{4,0},{6,2},{1,5},{3,7},{5,1},{7,3},{8,12},{10,14},{12... | collective-permute-start | bytes 786440 | tf_op jit(solution)/shard_map/ppermute | solution.py:162
  50.5 4.9 %copy-start.1 = (f32[128,2,128]{2,0,1:T(8,128)}, f32[128,2,128]{2,0,1:T(8,128)S(1)}, u32[]{:S(2)}) copy-start(f32[128,2,128]{2,0,1:T(8,128)S(1)} %copy.27) | copy-start | bytes 393220
  50.5 21.5 %collective-permute-start.5 = (bf16[2,2,2,128,128]{4,3,2,1,0:T(8,128)(2,1)S(1)}, bf16[2,2,2,128,128]{4,3,2,1,0:T(8,128)(2,1)S(1)}, u32[]{:S(2)}, u32[]{:S(2)}) collective-permute-start(bf16[2,2,2,128,128]{4,3,2,1,0:T(8,128)(2,1)S(1)} %copy-done.4), channel_id=1, source_target_pairs={{0,6},{2,4},{4,2},{6,0},{1,7},{3,5},{5,3},{7,1},{8,14},{10,12},{12... | collective-permute-start | bytes 786440 | tf_op jit(solution)/shard_map/ppermute | solution.py:162
  54.4 1.0 copy-start
  73.1 17.7 %copy-start.3 = (f32[2,128]{1,0:T(2,128)S(1)}, f32[2,128]{1,0:T(2,128)}, u32[]{:S(2)}) copy-start(f32[2,128]{1,0:T(2,128)} %shard_map.104) | copy-start | bytes 3076
  73.1 24.2 %copy-start.6 = (s32[2]{0:T(128)S(1)}, s32[2]{0:T(128)}, u32[]{:S(2)}) copy-start(s32[2]{0:T(128)} %param.12) | copy-start | bytes 28
  92.7 12.3 %all-to-all-start = ((f32[4,2,16]{2,1,0:T(2,128)}), f32[4,2,16]{2,1,0:T(2,128)S(1)}, u32[]{:S(2)}, u32[]{:S(2)}) async-start(f32[4,2,16]{2,1,0:T(2,128)} %broadcast_select_fusion), calls=%async_computation | async-start | bytes 8192 | tf_op jit(solution)/shard_map/all_to_all | solution.py:197
  105.9 0.7 copy-start.2

commit v11 on v10

--- a/solution.py
+++ b/solution.py
@@ -182,14 +182,15 @@
     tmpl_rel = jnp.concatenate(
         [templates] + [swapped(templates, ("xh", "yb"), n_g, k) for k in range(1, n_g)], 0
     )
-    piece = jnp.concatenate([swapped(strain, "ya", n_ya, k) for k in range(1, n_ya)], 0)
+    pieces = [swapped(strain, "ya", n_ya, k) for k in range(1, n_ya)]
     sigma2 = jax.vmap(lambda tmpl: template_norm(tmpl, weights))(tmpl_rel)
     isig = (1.0 / sigma2).reshape(-1)
 
     own_count = strain.shape[0]
-    own_rows = run_search(isig, strain, tmpl_rel, weights, tables)
-    own_rows, piece = lax.optimization_barrier((own_rows, piece))
-    other_rows = run_search(isig, piece, tmpl_rel, weights, tables)
+    first = jnp.concatenate([strain, pieces[0]], 0)
+    own_rows = run_search(isig, first, tmpl_rel, weights, tables)
+    own_rows, late = lax.optimization_barrier((own_rows, pieces[1:]))
+    other_rows = run_search(isig, jnp.concatenate(late, 0), tmpl_rel, weights, tables)
     slots = jnp.concatenate([own_rows, other_rows], 0).reshape(n_ya, own_count, -1)
 
     lanes = jnp.arange(n_ya, dtype=jnp.int32)

time: 107 us -> 109 us (1.019)
  the two profiles are of different devices: /device:TPU:8 before, /device:TPU:4 now
where the time goes in v11:
time: 109 us; the launch traced here: 108 us
  starting transfers between devices  36.3 us (33%)
  blocking collectives  28.2 us (26%)
  Pallas kernels  25.2 us (23%)
  waiting for transfers between devices  9.1 us (8%)
  other arithmetic  4.4 us (4%)
  local copies, waits for them, and re-layouts  4.02 us (4%)
    all_gather x5, blocking collectives, body(): gathered = lax.all_gather(gathered, axis, axis=0, tiled=True)  28.2 us
    pallas_call x2, Pallas kernels, run_search(): pl.pallas_call(functools.partial(search_kernel, n_tb), out_shape=jax.Shap...  25.2 us
    ppermute x6, starting transfers between devices, swapped(): return lax.ppermute(x, axes, [(i, i ^ k) for i in range(size)])  23.1 us
    all_to_all x1, starting transfers between devices, body(): lax.all_to_all(grouped, 'ya', split_axis=0, concat_axis=0, tiled=True)  13.2 us
    all_to_all x1, waiting for transfers between devices, body(): lax.all_to_all(grouped, 'ya', split_axis=0, concat_axis=0, tiled=True)  7.68 us
  transfers between devices with their start and end apart: 7, of which 3 were waited for; matrix products, arithmetic and copies ran while one was open for 3% of the time, Pallas kernels for 12%

profile of v11, /device:TPU:4, one launch (start us, length us, event | category | flops | bytes accessed | tf_op | source)
XLA Modules:
  0.0 108.2 jit_solution(15562794348441040825)
XLA Ops:
  0.6 0.0 copy-start.2
  0.6 0.0 copy-start.5
  0.7 2.1 %all-gather = f32[2,4,256]{2,1,0:T(4,128)S(1)} all-gather(f32[1,4,256]{2,1,0:T(4,128)} %bitcast.25), channel_id=1, replica_groups=mesh['sx'=2,'zh'=2,'z1'=2,'z0'=2,'sc'=2,'xh'=2,'ya'=4,'yb'=2] {'sc'}, dimensions={0}, use_global_device_ids=true | all-gather | bytes 12288 | tf_op jit(solution)/shard_map/all_gather | solution.py:176
  2.7 4.7 %all_gather.16 = f32[16,256]{1,0:T(8,128)S(1)} all-gather(f32[8,256]{1,0:T(8,128)S(1)} %reshape.127), channel_id=1, replica_groups=mesh['sx'=2,'zh'=2,'z1'=2,'z0'=2,'sc'=2,'xh'=2,'ya'=4,'yb'=2] {'z0'}, dimensions={0}, use_global_device_ids=true | all-gather | bytes 24576 | tf_op jit(solution)/shard_map/all_gather | solution.py:176
  7.4 6.5 %all_gather.17 = f32[32,256]{1,0:T(8,128)S(1)} all-gather(f32[16,256]{1,0:T(8,128)S(1)} %all_gather.16), channel_id=1, replica_groups=mesh['sx'=2,'zh'=2,'z1'=2,'z0'=2,'sc'=2,'xh'=2,'ya'=4,'yb'=2] {'z1'}, dimensions={0}, use_global_device_ids=true | all-gather | bytes 49152 | tf_op jit(solution)/shard_map/all_gather | solution.py:176
  14.0 10.0 %all_gather.18 = f32[64,256]{1,0:T(8,128)S(1)} all-gather(f32[32,256]{1,0:T(8,128)S(1)} %all_gather.17), channel_id=1, replica_groups=mesh['sx'=2,'zh'=2,'z1'=2,'z0'=2,'sc'=2,'xh'=2,'ya'=4,'yb'=2] {'zh'}, dimensions={0}, use_global_device_ids=true | all-gather | bytes 98304 | tf_op jit(solution)/shard_map/all_gather | solution.py:176
  24.0 4.9 %all_gather.19 = f32[128,256]{1,0:T(8,128)S(1)} all-gather(f32[64,256]{1,0:T(8,128)S(1)} %all_gather.18), channel_id=1, replica_groups=mesh['sx'=2,'zh'=2,'z1'=2,'z0'=2,'sc'=2,'xh'=2,'ya'=4,'yb'=2] {'sx'}, dimensions={0}, use_global_device_ids=true | all-gather | bytes 196608 | tf_op jit(solution)/shard_map/all_gather | solution.py:176
  28.9 3.5 %collective-permute-start = (bf16[4,2,128,128]{3,2,1,0:T(8,128)(2,1)}, bf16[4,2,128,128]{3,2,1,0:T(8,128)(2,1)S(1)}, u32[]{:S(2)}, u32[]{:S(2)}) collective-permute-start(bf16[4,2,128,128]{3,2,1,0:T(8,128)(2,1)} %param.10), channel_id=1, source_target_pairs={{0,1},{1,0},{8,9},{9,8},{2,3},{3,2},{10,11},{11,10},{4,5},{5,4},{1... | collective-permute-start | bytes 786440 | tf_op jit(solution)/shard_map/ppermute | solution.py:162
  32.4 3.5 %collective-permute-start.1 = (bf16[4,2,128,128]{3,2,1,0:T(8,128)(2,1)}, bf16[4,2,128,128]{3,2,1,0:T(8,128)(2,1)S(1)}, u32[]{:S(2)}, u32[]{:S(2)}) collective-permute-start(bf16[4,2,128,128]{3,2,1,0:T(8,128)(2,1)} %param.10), channel_id=1, source_target_pairs={{0,8},{1,9},{8,0},{9,1},{2,10},{3,11},{10,2},{11,3},{4,12},{5,13},... | collective-permute-start | bytes 786440 | tf_op jit(solution)/shard_map/ppermute | solution.py:162
  35.8 3.8 %collective-permute-start.2 = (bf16[4,2,128,128]{3,2,1,0:T(8,128)(2,1)}, bf16[4,2,128,128]{3,2,1,0:T(8,128)(2,1)S(1)}, u32[]{:S(2)}, u32[]{:S(2)}) collective-permute-start(bf16[4,2,128,128]{3,2,1,0:T(8,128)(2,1)} %param.10), channel_id=1, source_target_pairs={{0,9},{1,8},{8,1},{9,0},{2,11},{3,10},{10,3},{11,2},{4,13},{5,12},... | collective-permute-start | bytes 786440 | tf_op jit(solution)/shard_map/ppermute | solution.py:162
  39.6 4.5 %collective-permute-start.3 = (bf16[2,2,2,128,128]{4,3,2,1,0:T(8,128)(2,1)}, bf16[2,2,2,128,128]{4,3,2,1,0:T(8,128)(2,1)S(1)}, u32[]{:S(2)}, u32[]{:S(2)}) collective-permute-start(bf16[2,2,2,128,128]{4,3,2,1,0:T(8,128)(2,1)} %param.9), channel_id=1, source_target_pairs={{0,2},{2,0},{4,6},{6,4},{1,3},{3,1},{5,7},{7,5},{8,10},{10,8},{12,... | collective-permute-start | bytes 786440 | tf_op jit(solution)/shard_map/ppermute | solution.py:162
  44.1 5.9 %collective-permute-start.4 = (bf16[2,2,2,128,128]{4,3,2,1,0:T(8,128)(2,1)}, bf16[2,2,2,128,128]{4,3,2,1,0:T(8,128)(2,1)S(1)}, u32[]{:S(2)}, u32[]{:S(2)}) collective-permute-start(bf16[2,2,2,128,128]{4,3,2,1,0:T(8,128)(2,1)} %param.9), channel_id=1, source_target_pairs={{0,4},{2,6},{4,0},{6,2},{1,5},{3,7},{5,1},{7,3},{8,12},{10,14},{12... | collective-permute-start | bytes 786440 | tf_op jit(solution)/shard_map/ppermute | solution.py:162
  50.1 1.0 constant_dynamic-update-slice_fusion.3
  51.1 0.0 copy-done.5
  51.2 0.1 copy.26
  51.3 0.1 copy.27
  51.4 0.0 copy-start.1
  51.4 0.0 collective-permute-done
  51.4 0.0 copy-done.2
  51.4 1.9 %collective-permute-start.5 = (bf16[2,2,2,128,128]{4,3,2,1,0:T(8,128)(2,1)S(1)}, bf16[2,2,2,128,128]{4,3,2,1,0:T(8,128)(2,1)S(1)}, u32[]{:S(2)}, u32[]{:S(2)}) collective-permute-start(bf16[2,2,2,128,128]{4,3,2,1,0:T(8,128)(2,1)S(1)} %copy-done.2), channel_id=1, source_target_pairs={{0,6},{2,4},{4,2},{6,0},{1,7},{3,5},{5,3},{7,1},{8,14},{10,12},{12... | collective-permute-start | bytes 786440 | tf_op jit(solution)/shard_map/ppermute | solution.py:162
  53.4 0.0 collective-permute-done.1
  53.5 0.5 collective-permute-done.2
  54.0 0.0 copy-start
  54.0 0.2 add_bitcast_fusion
  54.2 0.8 copy-done
  55.0 0.0 copy-done.1
  55.0 0.3 multiply_reduce_fusion
  55.2 0.6 div.26.isig_ref
  55.9 0.9 collective-permute-done.3
  56.7 0.9 pad_maximum_fusion.strain_ref
  57.6 12.6 %shard_map.104 = f32[4,128]{1,0:T(4,128)} custom-call(f32[32]{0:T(128)} %div.26.isig_ref, bf16[4,2,2,128,128]{4,3,2,1,0:T(8,128)(2,1)} %pad_maximum_fusion.strain_ref, bf16[16,2,128,128]{3,2,1,0:T(8,128)(2,1)} %copy-done, f32[2,128,128]{2,1,0:T(8,128)} %bitcast.19, bf16[256,256]{1,0:T(8,128)(2,1)} %constant.57.clone.m1_ref, ...), custom_call_target="tpu_custom_call" | custom-call | flops 4294967296 | bytes 1703936 | tf_op jit(solution)/shard_map/pallas_call | solution.py:144
  70.2 0.0 collective-permute-done.4
  70.2 0.0 collective-permute-done.5
  70.2 0.9 pad_maximum_fusion.1.strain_ref
  71.1 12.6 %shard_map.105 = f32[4,128]{1,0:T(4,128)} custom-call(f32[32]{0:T(128)} %div.26.isig_ref, bf16[4,2,2,128,128]{4,3,2,1,0:T(8,128)(2,1)} %pad_maximum_fusion.1.strain_ref, bf16[16,2,128,128]{3,2,1,0:T(8,128)(2,1)} %copy-done, f32[2,128,128]{2,1,0:T(8,128)} %bitcast.20, bf16[256,256]{1,0:T(8,128)(2,1)} %constant.57.clone.m1_ref, ...), custom_call_target="tpu_custom_call" | custom-call | flops 4294967296 | bytes 1703936 | tf_op jit(solution)/shard_map/pallas_call | solution.py:144
  83.7 0.0 copy-done.4
  83.7 0.7 pad_maximum_fusion.2
  84.3 0.6 gather_fusion
  84.9 0.7 broadcast_select_fusion
  85.6 13.2 %all-to-all-start = ((f32[4,2,16]{2,1,0:T(2,128)}), f32[4,2,16]{2,1,0:T(2,128)S(1)}, u32[]{:S(2)}, u32[]{:S(2)}) async-start(f32[4,2,16]{2,1,0:T(2,128)} %broadcast_select_fusion), calls=%async_computation | async-start | bytes 8192 | tf_op jit(solution)/shard_map/all_to_all | solution.py:198
  98.8 0.0 copy-done.6
  98.9 7.7 %all-to-all-done = f32[4,2,16]{2,1,0:T(2,128)S(1)} async-done(((f32[4,2,16]{2,1,0:T(2,128)}), f32[4,2,16]{2,1,0:T(2,128)S(1)}, u32[]{:S(2)}, u32[]{:S(2)}) %all-to-all-start) | async-done | bytes 544 | tf_op jit(solution)/shard_map/all_to_all | solution.py:198
  106.5 0.1 reshape.109
  106.6 0.6 gather_fusion.1
  107.2 0.1 sqrt_bitcast_fusion
  107.3 0.1 sqrt.15
  107.4 0.1 broadcast_multiply_fusion
  107.5 0.7 select_reduce_fusion
  (21 shorter events, 0.2 us)
Async XLA Ops:
  0.6 50.8 %copy-start.2 = (bf16[2,2,2,128,128]{4,3,2,1,0:T(8,128)(2,1)S(1)}, bf16[2,2,2,128,128]{4,3,2,1,0:T(8,128)(2,1)}, u32[]{:S(2)}) copy-start(bf16[2,2,2,128,128]{4,3,2,1,0:T(8,128)(2,1)} %param.9) | copy-start | bytes 786436
  0.6 50.5 %copy-start.5 = (s32[64]{0:T(128)S(1)}, s32[64]{0:T(128)}, u32[]{:S(2)}) copy-start(s32[64]{0:T(128)} %param.13) | copy-start | bytes 772
  28.9 22.5 %collective-permute-start = (bf16[4,2,128,128]{3,2,1,0:T(8,128)(2,1)}, bf16[4,2,128,128]{3,2,1,0:T(8,128)(2,1)S(1)}, u32[]{:S(2)}, u32[]{:S(2)}) collective-permute-start(bf16[4,2,128,128]{3,2,1,0:T(8,128)(2,1)} %param.10), channel_id=1, source_target_pairs={{0,1},{1,0},{8,9},{9,8},{2,3},{3,2},{10,11},{11,10},{4,5},{5,4},{1... | collective-permute-start | bytes 786440 | tf_op jit(solution)/shard_map/ppermute | solution.py:162
  32.4 21.0 %collective-permute-start.1 = (bf16[4,2,128,128]{3,2,1,0:T(8,128)(2,1)}, bf16[4,2,128,128]{3,2,1,0:T(8,128)(2,1)S(1)}, u32[]{:S(2)}, u32[]{:S(2)}) collective-permute-start(bf16[4,2,128,128]{3,2,1,0:T(8,128)(2,1)} %param.10), channel_id=1, source_target_pairs={{0,8},{1,9},{8,0},{9,1},{2,10},{3,11},{10,2},{11,3},{4,12},{5,13},... | collective-permute-start | bytes 786440 | tf_op jit(solution)/shard_map/ppermute | solution.py:162
  35.8 18.1 %collective-permute-start.2 = (bf16[4,2,128,128]{3,2,1,0:T(8,128)(2,1)}, bf16[4,2,128,128]{3,2,1,0:T(8,128)(2,1)S(1)}, u32[]{:S(2)}, u32[]{:S(2)}) collective-permute-start(bf16[4,2,128,128]{3,2,1,0:T(8,128)(2,1)} %param.10), channel_id=1, source_target_pairs={{0,9},{1,8},{8,1},{9,0},{2,11},{3,10},{10,3},{11,2},{4,13},{5,12},... | collective-permute-start | bytes 786440 | tf_op jit(solution)/shard_map/ppermute | solution.py:162
  39.6 17.1 %collective-permute-start.3 = (bf16[2,2,2,128,128]{4,3,2,1,0:T(8,128)(2,1)}, bf16[2,2,2,128,128]{4,3,2,1,0:T(8,128)(2,1)S(1)}, u32[]{:S(2)}, u32[]{:S(2)}) collective-permute-start(bf16[2,2,2,128,128]{4,3,2,1,0:T(8,128)(2,1)} %param.9), channel_id=1, source_target_pairs={{0,2},{2,0},{4,6},{6,4},{1,3},{3,1},{5,7},{7,5},{8,10},{10,8},{12,... | collective-permute-start | bytes 786440 | tf_op jit(solution)/shard_map/ppermute | solution.py:162
  44.1 26.1 %collective-permute-start.4 = (bf16[2,2,2,128,128]{4,3,2,1,0:T(8,128)(2,1)}, bf16[2,2,2,128,128]{4,3,2,1,0:T(8,128)(2,1)S(1)}, u32[]{:S(2)}, u32[]{:S(2)}) collective-permute-start(bf16[2,2,2,128,128]{4,3,2,1,0:T(8,128)(2,1)} %param.9), channel_id=1, source_target_pairs={{0,4},{2,6},{4,0},{6,2},{1,5},{3,7},{5,1},{7,3},{8,12},{10,14},{12... | collective-permute-start | bytes 786440 | tf_op jit(solution)/shard_map/ppermute | solution.py:162
  51.4 3.6 %copy-start.1 = (f32[128,2,128]{2,0,1:T(8,128)}, f32[128,2,128]{2,0,1:T(8,128)S(1)}, u32[]{:S(2)}) copy-start(f32[128,2,128]{2,0,1:T(8,128)S(1)} %copy.27) | copy-start | bytes 393220
  51.4 18.8 %collective-permute-start.5 = (bf16[2,2,2,128,128]{4,3,2,1,0:T(8,128)(2,1)S(1)}, bf16[2,2,2,128,128]{4,3,2,1,0:T(8,128)(2,1)S(1)}, u32[]{:S(2)}, u32[]{:S(2)}) collective-permute-start(bf16[2,2,2,128,128]{4,3,2,1,0:T(8,128)(2,1)S(1)} %copy-done.2), channel_id=1, source_target_pairs={{0,6},{2,4},{4,2},{6,0},{1,7},{3,5},{5,3},{7,1},{8,14},{10,12},{12... | collective-permute-start | bytes 786440 | tf_op jit(solution)/shard_map/ppermute | solution.py:162
  54.0 1.0 copy-start
  71.1 12.6 %copy-start.4 = (f32[4,128]{1,0:T(4,128)S(1)}, f32[4,128]{1,0:T(4,128)}, u32[]{:S(2)}) copy-start(f32[4,128]{1,0:T(4,128)} %shard_map.104) | copy-start | bytes 6148
  71.1 27.8 %copy-start.6 = (s32[2]{0:T(128)S(1)}, s32[2]{0:T(128)}, u32[]{:S(2)}) copy-start(s32[2]{0:T(128)} %param.12) | copy-start | bytes 28
  85.6 21.0 %all-to-all-start = ((f32[4,2,16]{2,1,0:T(2,128)}), f32[4,2,16]{2,1,0:T(2,128)S(1)}, u32[]{:S(2)}, u32[]{:S(2)}) async-start(f32[4,2,16]{2,1,0:T(2,128)} %broadcast_select_fusion), calls=%async_computation | async-start | bytes 8192 | tf_op jit(solution)/shard_map/all_to_all | solution.py:198
  107.5 0.7 copy-start.3

commit v12 on v10

--- a/solution.py
+++ b/solution.py
@@ -54,20 +54,26 @@
     return jnp.sum((h_re * h_re + h_im * h_im) * weights, axis=(1, 2))
 
 
-def search_kernel(n_tb, isig_ref, strain_ref, tmpl_ref, w_ref, m1_ref, m2_ref,
-                  tc_ref, ts_ref, out_ref, q_ref, y_ref, z_ref, hw_ref, sd_ref):
+def search_kernel(n_tb, n_tp, n_sp, isig_ref, *refs):
+    tmpl_refs = refs[:n_tp]
+    strain_refs = refs[n_tp:n_tp + n_sp]
+    (w_ref, m1_ref, m2_ref, tc_ref, ts_ref, out_ref, q_ref, y_ref, z_ref, hw_ref,
+     sd_ref) = refs[n_tp + n_sp:]
     nb = 2 * TB
 
-    def weigh(t, carry):
-        h_re = tmpl_ref[t, 0].astype(jnp.float32)
-        h_im = tmpl_ref[t, 1].astype(jnp.float32)
-        for d in range(2):
-            w = w_ref[d]
-            hw_ref[t, d, 0] = h_re * w
-            hw_ref[t, d, 1] = h_im * w
-        return carry
-
-    lax.fori_loop(0, tmpl_ref.shape[0], weigh, 0)
+    per_t = tmpl_refs[0].shape[0]
+    for p in range(n_tp):
+        def weigh(l, carry, p=p):
+            t = p * per_t + l
+            h_re = tmpl_refs[p][l, 0].astype(jnp.float32)
+            h_im = tmpl_refs[p][l, 1].astype(jnp.float32)
+            for d in range(2):
+                w = w_ref[d]
+                hw_ref[t, d, 0] = h_re * w
+                hw_ref[t, d, 1] = h_im * w
+            return carry
+
+        lax.fori_loop(0, per_t, weigh, 0)
     out_ref[...] = jnp.zeros(out_ref.shape, jnp.float32)
 
     def batch(i, slot):
@@ -117,9 +123,14 @@
         @pl.when(i % n_tb == 0)
         def _():
             seg = i // n_tb
-            for d in range(2):
-                for part in range(2):
-                    sd_ref[d, part] = strain_ref[seg, d, part].astype(jnp.float32)
+            per_s = strain_refs[0].shape[0]
+            for p in range(n_sp):
+                @pl.when(seg // per_s == p)
+                def _(p=p):
+                    local = seg - p * per_s
+                    for d in range(2):
+                        for part in range(2):
+                            sd_ref[d, part] = strain_refs[p][local, d, part].astype(jnp.float32)
 
         batch(i, 0)
         batch(i + 1, 1)
@@ -128,10 +139,10 @@
     lax.fori_loop(0, out_ref.shape[0] * n_tb // 2, step, 0)
 
 
-def run_search(isig, strain, tmpl, weights, tables):
+def run_search(isig, strains, tmpls, weights, tables):
     m1, m2, tc, ts = tables
-    n_s = strain.shape[0]
-    n_t = tmpl.shape[0]
+    n_s = sum(x.shape[0] for x in strains)
+    n_t = sum(x.shape[0] for x in tmpls)
     n_tb = n_t // TB
     vmem = pltpu.VMEM
     smem = pltpu.SMEM
@@ -139,12 +150,13 @@
     cost = pl.CostEstimate(
         flops=ffts * 2 * (2 * 256 * 256 * 128),
         transcendentals=0,
-        bytes_accessed=strain.size * 2 + tmpl.size * 2 + weights.size * 4,
+        bytes_accessed=n_s * strains[0][0].size * 2 + n_t * tmpls[0][0].size * 2 + weights.size * 4,
     )
     out = pl.pallas_call(
-        functools.partial(search_kernel, n_tb),
+        functools.partial(search_kernel, n_tb, len(tmpls), len(strains)),
         out_shape=jax.ShapeDtypeStruct((n_s, N2), jnp.float32),
-        in_specs=[pl.BlockSpec(memory_space=smem)] + [pl.BlockSpec(memory_space=vmem)] * 7,
+        in_specs=[pl.BlockSpec(memory_space=smem)]
+        + [pl.BlockSpec(memory_space=vmem)] * (len(tmpls) + len(strains) + 5),
         out_specs=pl.BlockSpec(memory_space=vmem),
         scratch_shapes=[
             pltpu.VMEM((2, 2 * N1, 2 * TB * N2), jnp.bfloat16),
@@ -154,7 +166,7 @@
             pltpu.VMEM((2, 2, N1, N2), jnp.float32),
         ],
         cost_estimate=cost,
-    )(isig, strain, tmpl, weights, m1, m2, tc, ts)
+    )(isig, *tmpls, *strains, weights, m1, m2, tc, ts)
     return out[:, :n_t]
 
 
@@ -179,17 +191,17 @@
     weights = 1.0 / full_psd
     tables = make_tables()
 
-    tmpl_rel = jnp.concatenate(
-        [templates] + [swapped(templates, ("xh", "yb"), n_g, k) for k in range(1, n_g)], 0
-    )
-    piece = jnp.concatenate([swapped(strain, "ya", n_ya, k) for k in range(1, n_ya)], 0)
-    sigma2 = jax.vmap(lambda tmpl: template_norm(tmpl, weights))(tmpl_rel)
+    tmpl_rel = [templates] + [swapped(templates, ("xh", "yb"), n_g, k) for k in range(1, n_g)]
+    pieces = [swapped(strain, "ya", n_ya, k) for k in range(1, n_ya)]
+    sigma2 = jnp.concatenate(
+        [jax.vmap(lambda tmpl: template_norm(tmpl, weights))(tp) for tp in tmpl_rel], 0
+    )
     isig = (1.0 / sigma2).reshape(-1)
 
     own_count = strain.shape[0]
-    own_rows = run_search(isig, strain, tmpl_rel, weights, tables)
-    own_rows, piece = lax.optimization_barrier((own_rows, piece))
-    other_rows = run_search(isig, piece, tmpl_rel, weights, tables)
+    own_rows = run_search(isig, [strain], tmpl_rel, weights, tables)
+    own_rows, pieces = lax.optimization_barrier((own_rows, pieces))
+    other_rows = run_search(isig, pieces, tmpl_rel, weights, tables)
     slots = jnp.concatenate([own_rows, other_rows], 0).reshape(n_ya, own_count, -1)
 
     lanes = jnp.arange(n_ya, dtype=jnp.int32)

time: 107 us -> 107 us (level)
  local copies, waits for them, and re-layouts: 4.03 us -> 6.67 us
  waiting for transfers between devices: 16.1 us -> 14.9 us
    unnamed x18 -> x27, local copies, waits for them, and re-layouts: 1.85 us -> 4.07 us
where the time goes in v12:
time: 107 us
  starting transfers between devices  28.4 us (27%)
  blocking collectives  28.2 us (26%)
  Pallas kernels  25 us (23%)
  waiting for transfers between devices  14.9 us (14%)
  local copies, waits for them, and re-layouts  6.67 us (6%)
  other arithmetic  2.77 us (3%)
    all_gather x5, blocking collectives, body(): gathered = lax.all_gather(gathered, axis, axis=0, tiled=True)  28.2 us
    pallas_call x2, Pallas kernels, run_search(): pl.pallas_call(functools.partial(search_kernel, n_tb, len(tmpls), len(str...  25 us
    ppermute x6, starting transfers between devices, swapped(): return lax.ppermute(x, axes, [(i, i ^ k) for i in range(size)])  24 us
    ppermute x6, waiting for transfers between devices, swapped(): return lax.ppermute(x, axes, [(i, i ^ k) for i in range(size)])  7.86 us
    all_to_all x1, waiting for transfers between devices, body(): lax.all_to_all(grouped, 'ya', split_axis=0, concat_axis=0, tiled=True)  7.05 us
    all_to_all x1, starting transfers between devices, body(): lax.all_to_all(grouped, 'ya', split_axis=0, concat_axis=0, tiled=True)  4.38 us
    unnamed x27, local copies, waits for them, and re-layouts  4.07 us
  transfers between devices with their start and end apart: 7, of which 3 were waited for; matrix products, arithmetic and copies ran while one was open for 2% of the time, Pallas kernels for 7%

profile of v12, /device:TPU:8, one launch (start us, length us, event | category | flops | bytes accessed | tf_op | source)
XLA Modules:
  0.0 106.9 jit_solution(17675512408027316692)
XLA Ops:
  0.6 0.0 copy-start.1
  0.6 2.1 %all-gather = f32[2,4,256]{2,1,0:T(4,128)S(1)} all-gather(f32[1,4,256]{2,1,0:T(4,128)} %bitcast.31), channel_id=1, replica_groups=mesh['sx'=2,'zh'=2,'z1'=2,'z0'=2,'sc'=2,'xh'=2,'ya'=4,'yb'=2] {'sc'}, dimensions={0}, use_global_device_ids=true | all-gather | bytes 12288 | tf_op jit(solution)/shard_map/all_gather | solution.py:188
  2.7 4.7 %all_gather.16 = f32[16,256]{1,0:T(8,128)S(1)} all-gather(f32[8,256]{1,0:T(8,128)S(1)} %reshape.127), channel_id=1, replica_groups=mesh['sx'=2,'zh'=2,'z1'=2,'z0'=2,'sc'=2,'xh'=2,'ya'=4,'yb'=2] {'z0'}, dimensions={0}, use_global_device_ids=true | all-gather | bytes 24576 | tf_op jit(solution)/shard_map/all_gather | solution.py:188
  7.4 6.5 %all_gather.17 = f32[32,256]{1,0:T(8,128)S(1)} all-gather(f32[16,256]{1,0:T(8,128)S(1)} %all_gather.16), channel_id=1, replica_groups=mesh['sx'=2,'zh'=2,'z1'=2,'z0'=2,'sc'=2,'xh'=2,'ya'=4,'yb'=2] {'z1'}, dimensions={0}, use_global_device_ids=true | all-gather | bytes 49152 | tf_op jit(solution)/shard_map/all_gather | solution.py:188
  14.0 10.0 %all_gather.18 = f32[64,256]{1,0:T(8,128)S(1)} all-gather(f32[32,256]{1,0:T(8,128)S(1)} %all_gather.17), channel_id=1, replica_groups=mesh['sx'=2,'zh'=2,'z1'=2,'z0'=2,'sc'=2,'xh'=2,'ya'=4,'yb'=2] {'zh'}, dimensions={0}, use_global_device_ids=true | all-gather | bytes 98304 | tf_op jit(solution)/shard_map/all_gather | solution.py:188
  24.0 4.9 %all_gather.19 = f32[128,256]{1,0:T(8,128)S(1)} all-gather(f32[64,256]{1,0:T(8,128)S(1)} %all_gather.18), channel_id=1, replica_groups=mesh['sx'=2,'zh'=2,'z1'=2,'z0'=2,'sc'=2,'xh'=2,'ya'=4,'yb'=2] {'sx'}, dimensions={0}, use_global_device_ids=true | all-gather | bytes 196608 | tf_op jit(solution)/shard_map/all_gather | solution.py:188
  28.9 5.0 %collective-permute-start = (bf16[4,2,128,128]{3,2,1,0:T(8,128)(2,1)S(1)}, bf16[4,2,128,128]{3,2,1,0:T(8,128)(2,1)S(1)}, u32[]{:S(2)}, u32[]{:S(2)}) collective-permute-start(bf16[4,2,128,128]{3,2,1,0:T(8,128)(2,1)S(1)} %copy-done.1), channel_id=1, source_target_pairs={{0,1},{1,0},{8,9},{9,8},{2,3},{3,2},{10,11},{11,10},{4,5},{5,4},{1... | collective-permute-start | bytes 786440 | tf_op jit(solution)/shard_map/ppermute | solution.py:174
  33.8 2.3 %collective-permute-start.1 = (bf16[4,2,128,128]{3,2,1,0:T(8,128)(2,1)S(1)}, bf16[4,2,128,128]{3,2,1,0:T(8,128)(2,1)S(1)}, u32[]{:S(2)}, u32[]{:S(2)}) collective-permute-start(bf16[4,2,128,128]{3,2,1,0:T(8,128)(2,1)S(1)} %copy-done.1), channel_id=1, source_target_pairs={{0,8},{1,9},{8,0},{9,1},{2,10},{3,11},{10,2},{11,3},{4,12},{5,13},... | collective-permute-start | bytes 786440 | tf_op jit(solution)/shard_map/ppermute | solution.py:174
  36.2 4.5 %collective-permute-start.2 = (bf16[4,2,128,128]{3,2,1,0:T(8,128)(2,1)S(1)}, bf16[4,2,128,128]{3,2,1,0:T(8,128)(2,1)S(1)}, u32[]{:S(2)}, u32[]{:S(2)}) collective-permute-start(bf16[4,2,128,128]{3,2,1,0:T(8,128)(2,1)S(1)} %copy-done.1), channel_id=1, source_target_pairs={{0,9},{1,8},{8,1},{9,0},{2,11},{3,10},{10,3},{11,2},{4,13},{5,12},... | collective-permute-start | bytes 786440 | tf_op jit(solution)/shard_map/ppermute | solution.py:174
  40.7 3.4 %collective-permute-start.3 = (bf16[2,2,2,128,128]{4,3,2,1,0:T(8,128)(2,1)}, bf16[2,2,2,128,128]{4,3,2,1,0:T(8,128)(2,1)S(1)}, u32[]{:S(2)}, u32[]{:S(2)}) collective-permute-start(bf16[2,2,2,128,128]{4,3,2,1,0:T(8,128)(2,1)} %refs_4_), channel_id=1, source_target_pairs={{0,2},{2,0},{4,6},{6,4},{1,3},{3,1},{5,7},{7,5},{8,10},{10,8},{12,... | collective-permute-start | bytes 786440 | tf_op jit(solution)/shard_map/ppermute | solution.py:174
  44.1 5.0 %collective-permute-start.4 = (bf16[2,2,2,128,128]{4,3,2,1,0:T(8,128)(2,1)}, bf16[2,2,2,128,128]{4,3,2,1,0:T(8,128)(2,1)S(1)}, u32[]{:S(2)}, u32[]{:S(2)}) collective-permute-start(bf16[2,2,2,128,128]{4,3,2,1,0:T(8,128)(2,1)} %refs_4_), channel_id=1, source_target_pairs={{0,4},{2,6},{4,0},{6,2},{1,5},{3,7},{5,1},{7,3},{8,12},{10,14},{12... | collective-permute-start | bytes 786440 | tf_op jit(solution)/shard_map/ppermute | solution.py:174
  49.3 0.0 copy-start.11
  49.3 0.6 copy-done.11
  50.0 0.0 copy-start.7
  50.0 0.1 copy.27
  50.1 0.1 copy.28
  50.2 0.0 collective-permute-done.refs_1_
  50.2 0.7 copy-done.7
  50.9 3.7 %collective-permute-start.5 = (bf16[2,2,2,128,128]{4,3,2,1,0:T(8,128)(2,1)S(1)}, bf16[2,2,2,128,128]{4,3,2,1,0:T(8,128)(2,1)S(1)}, u32[]{:S(2)}, u32[]{:S(2)}) collective-permute-start(bf16[2,2,2,128,128]{4,3,2,1,0:T(8,128)(2,1)S(1)} %copy-done.7), channel_id=1, source_target_pairs={{0,6},{2,4},{4,2},{6,0},{1,7},{3,5},{5,3},{7,1},{8,14},{10,12},{12... | collective-permute-start | bytes 786440 | tf_op jit(solution)/shard_map/ppermute | solution.py:174
  54.7 0.0 collective-permute-done.1.refs_2_
  54.9 0.5 copy-done.3
  55.4 0.1 copy-done.4
  55.5 0.3 multiply_reduce_fusion.3
  55.8 0.1 copy.32
  55.9 0.1 copy.31
  56.0 0.1 copy.30
  56.1 0.1 copy.29
  56.2 0.1 maximum_divide_fusion
  56.3 0.1 copy.33
  56.3 0.6 div.26.isig_ref
  57.0 7.4 %shard_map.104 = f32[2,128]{1,0:T(2,128)} custom-call(f32[32]{0:T(128)} %div.26.isig_ref, bf16[4,2,128,128]{3,2,1,0:T(8,128)(2,1)} %refs_0_.1, bf16[4,2,128,128]{3,2,1,0:T(8,128)(2,1)} %copy-done.2, bf16[4,2,128,128]{3,2,1,0:T(8,128)(2,1)} %copy-done.3, bf16[4,2,128,128]{3,2,1,0:T(8,128)(2,1)} %copy-done.4, bf16[2,2,2,128,128]{4,3,2,1,0:T(8,128)(2,1)} %refs_4_, ...), custom_call_target="tpu_custom_call" | custom-call | flops 2147483648 | bytes 1441792 | tf_op jit(solution)/shard_map/pallas_call | solution.py:155
  64.3 2.4 %collective-permute-done.4.refs_5_ = bf16[2,2,2,128,128]{4,3,2,1,0:T(8,128)(2,1)S(1)} collective-permute-done((bf16[2,2,2,128,128]{4,3,2,1,0:T(8,128)(2,1)}, bf16[2,2,2,128,128]{4,3,2,1,0:T(8,128)(2,1)S(1)}, u32[]{:S(2)}, u32[]{:S(2)}) %collective-permute-start.4) | collective-permute-done | bytes 262176 | tf_op jit(solution)/shard_map/ppermute | solution.py:174
  66.7 5.5 %collective-permute-done.5.refs_6_ = bf16[2,2,2,128,128]{4,3,2,1,0:T(8,128)(2,1)S(1)} collective-permute-done((bf16[2,2,2,128,128]{4,3,2,1,0:T(8,128)(2,1)S(1)}, bf16[2,2,2,128,128]{4,3,2,1,0:T(8,128)(2,1)S(1)}, u32[]{:S(2)}, u32[]{:S(2)}) %collective-permute-start.5) | collective-permute-done | bytes 262176 | tf_op jit(solution)/shard_map/ppermute | solution.py:174
  72.2 0.7 copy-done.10
  72.9 17.7 %shard_map.105 = f32[6,128]{1,0:T(8,128)} custom-call(f32[32]{0:T(128)} %div.26.isig_ref, bf16[4,2,128,128]{3,2,1,0:T(8,128)(2,1)} %refs_0_.1, bf16[4,2,128,128]{3,2,1,0:T(8,128)(2,1)} %copy-done.2, bf16[4,2,128,128]{3,2,1,0:T(8,128)(2,1)} %copy-done.3, bf16[4,2,128,128]{3,2,1,0:T(8,128)(2,1)} %copy-done.4, bf16[2,2,2,128,128]{4,3,2,1,0:T(8,128)(2,1)} %copy-done.8, ...), custom_call_target="tpu_custom_call" | custom-call | flops 6442450944 | bytes 1966080 | tf_op jit(solution)/shard_map/pallas_call | solution.py:155
  90.6 0.7 copy-done.6
  91.2 0.7 pad_maximum_fusion
  91.9 0.6 gather_fusion
  92.5 0.7 broadcast_select_fusion
  93.2 4.4 %all-to-all-start = ((f32[4,2,16]{2,1,0:T(2,128)}), f32[4,2,16]{2,1,0:T(2,128)S(1)}, u32[]{:S(2)}, u32[]{:S(2)}) async-start(f32[4,2,16]{2,1,0:T(2,128)} %broadcast_select_fusion), calls=%async_computation | async-start | bytes 8192 | tf_op jit(solution)/shard_map/all_to_all | solution.py:209
  97.6 0.6 copy-done.12
  98.2 7.1 %all-to-all-done = f32[4,2,16]{2,1,0:T(2,128)S(1)} async-done(((f32[4,2,16]{2,1,0:T(2,128)}), f32[4,2,16]{2,1,0:T(2,128)S(1)}, u32[]{:S(2)}, u32[]{:S(2)}) %all-to-all-start) | async-done | bytes 544 | tf_op jit(solution)/shard_map/all_to_all | solution.py:209
  105.2 0.1 reshape.109
  105.3 0.6 gather_fusion.1
  105.9 0.1 sqrt_bitcast_fusion
  106.0 0.1 sqrt.15
  106.1 0.1 broadcast_multiply_fusion
  106.2 0.7 select_reduce_fusion
  (35 shorter events, 0.3 us)
Async XLA Ops:
  0.6 28.2 %copy-start.1 = (bf16[4,2,128,128]{3,2,1,0:T(8,128)(2,1)S(1)}, bf16[4,2,128,128]{3,2,1,0:T(8,128)(2,1)}, u32[]{:S(2)}) copy-start(bf16[4,2,128,128]{3,2,1,0:T(8,128)(2,1)} %refs_0_.1) | copy-start | bytes 786436
  28.9 21.3 %collective-permute-start = (bf16[4,2,128,128]{3,2,1,0:T(8,128)(2,1)S(1)}, bf16[4,2,128,128]{3,2,1,0:T(8,128)(2,1)S(1)}, u32[]{:S(2)}, u32[]{:S(2)}) collective-permute-start(bf16[4,2,128,128]{3,2,1,0:T(8,128)(2,1)S(1)} %copy-done.1), channel_id=1, source_target_pairs={{0,1},{1,0},{8,9},{9,8},{2,3},{3,2},{10,11},{11,10},{4,5},{5,4},{1... | collective-permute-start | bytes 786440 | tf_op jit(solution)/shard_map/ppermute | solution.py:174
  33.8 20.9 %collective-permute-start.1 = (bf16[4,2,128,128]{3,2,1,0:T(8,128)(2,1)S(1)}, bf16[4,2,128,128]{3,2,1,0:T(8,128)(2,1)S(1)}, u32[]{:S(2)}, u32[]{:S(2)}) collective-permute-start(bf16[4,2,128,128]{3,2,1,0:T(8,128)(2,1)S(1)} %copy-done.1), channel_id=1, source_target_pairs={{0,8},{1,9},{8,0},{9,1},{2,10},{3,11},{10,2},{11,3},{4,12},{5,13},... | collective-permute-start | bytes 786440 | tf_op jit(solution)/shard_map/ppermute | solution.py:174
  36.2 18.7 %collective-permute-start.2 = (bf16[4,2,128,128]{3,2,1,0:T(8,128)(2,1)S(1)}, bf16[4,2,128,128]{3,2,1,0:T(8,128)(2,1)S(1)}, u32[]{:S(2)}, u32[]{:S(2)}) collective-permute-start(bf16[4,2,128,128]{3,2,1,0:T(8,128)(2,1)S(1)} %copy-done.1), channel_id=1, source_target_pairs={{0,9},{1,8},{8,1},{9,0},{2,11},{3,10},{10,3},{11,2},{4,13},{5,12},... | collective-permute-start | bytes 786440 | tf_op jit(solution)/shard_map/ppermute | solution.py:174
  40.7 23.7 %collective-permute-start.3 = (bf16[2,2,2,128,128]{4,3,2,1,0:T(8,128)(2,1)}, bf16[2,2,2,128,128]{4,3,2,1,0:T(8,128)(2,1)S(1)}, u32[]{:S(2)}, u32[]{:S(2)}) collective-permute-start(bf16[2,2,2,128,128]{4,3,2,1,0:T(8,128)(2,1)} %refs_4_), channel_id=1, source_target_pairs={{0,2},{2,0},{4,6},{6,4},{1,3},{3,1},{5,7},{7,5},{8,10},{10,8},{12,... | collective-permute-start | bytes 786440 | tf_op jit(solution)/shard_map/ppermute | solution.py:174
  44.1 22.6 %collective-permute-start.4 = (bf16[2,2,2,128,128]{4,3,2,1,0:T(8,128)(2,1)}, bf16[2,2,2,128,128]{4,3,2,1,0:T(8,128)(2,1)S(1)}, u32[]{:S(2)}, u32[]{:S(2)}) collective-permute-start(bf16[2,2,2,128,128]{4,3,2,1,0:T(8,128)(2,1)} %refs_4_), channel_id=1, source_target_pairs={{0,4},{2,6},{4,0},{6,2},{1,5},{3,7},{5,1},{7,3},{8,12},{10,14},{12... | collective-permute-start | bytes 786440 | tf_op jit(solution)/shard_map/ppermute | solution.py:174
  49.3 0.7 copy-start.11
  50.0 1.0 copy-start.7
  50.2 5.2 %copy-start = (f32[128,2,128]{2,0,1:T(8,128)}, f32[128,2,128]{2,0,1:T(8,128)S(1)}, u32[]{:S(2)}) copy-start(f32[128,2,128]{2,0,1:T(8,128)S(1)} %copy.28) | copy-start | bytes 393220
  50.9 3.9 %copy-start.2 = (bf16[4,2,128,128]{3,2,1,0:T(8,128)(2,1)}, bf16[4,2,128,128]{3,2,1,0:T(8,128)(2,1)S(1)}, u32[]{:S(2)}) copy-start(bf16[4,2,128,128]{3,2,1,0:T(8,128)(2,1)S(1)} %collective-permute-done.refs_1_) | copy-start | bytes 786436
  50.9 21.3 %collective-permute-start.5 = (bf16[2,2,2,128,128]{4,3,2,1,0:T(8,128)(2,1)S(1)}, bf16[2,2,2,128,128]{4,3,2,1,0:T(8,128)(2,1)S(1)}, u32[]{:S(2)}, u32[]{:S(2)}) collective-permute-start(bf16[2,2,2,128,128]{4,3,2,1,0:T(8,128)(2,1)S(1)} %copy-done.7), channel_id=1, source_target_pairs={{0,6},{2,4},{4,2},{6,0},{1,7},{3,5},{5,3},{7,1},{8,14},{10,12},{12... | collective-permute-start | bytes 786440 | tf_op jit(solution)/shard_map/ppermute | solution.py:174
  54.7 0.7 copy-start.3
  54.8 0.7 copy-start.4
  64.3 7.9 %copy-start.8 = (bf16[2,2,2,128,128]{4,3,2,1,0:T(8,128)(2,1)}, bf16[2,2,2,128,128]{4,3,2,1,0:T(8,128)(2,1)S(1)}, u32[]{:S(2)}) copy-start(bf16[2,2,2,128,128]{4,3,2,1,0:T(8,128)(2,1)S(1)} %collective-permute-done.3.refs_4_) | copy-start | bytes 786436
  66.7 5.5 %copy-start.9 = (bf16[2,2,2,128,128]{4,3,2,1,0:T(8,128)(2,1)}, bf16[2,2,2,128,128]{4,3,2,1,0:T(8,128)(2,1)S(1)}, u32[]{:S(2)}) copy-start(bf16[2,2,2,128,128]{4,3,2,1,0:T(8,128)(2,1)S(1)} %collective-permute-done.4.refs_5_) | copy-start | bytes 786436
  72.2 0.7 copy-start.10
  90.6 0.7 copy-start.6
  93.2 12.1 %all-to-all-start = ((f32[4,2,16]{2,1,0:T(2,128)}), f32[4,2,16]{2,1,0:T(2,128)S(1)}, u32[]{:S(2)}, u32[]{:S(2)}) async-start(f32[4,2,16]{2,1,0:T(2,128)} %broadcast_select_fusion), calls=%async_computation | async-start | bytes 8192 | tf_op jit(solution)/shard_map/all_to_all | solution.py:209
  97.5 0.7 copy-start.12
  106.2 0.7 copy-start.5

commit v13 on v10

--- a/solution.py
+++ b/solution.py
@@ -14,7 +14,7 @@
 N2 = 128
 BINS = 16384
 BLOCKS = 8
-TB = 8
+TB = 16
 
 
 def make_tables():
@@ -70,14 +70,14 @@
     lax.fori_loop(0, tmpl_ref.shape[0], weigh, 0)
     out_ref[...] = jnp.zeros(out_ref.shape, jnp.float32)
 
-    def batch(i, slot):
+    def batch(i, slot, src):
         s = i // n_tb
         tb = i % n_tb
         for k in range(TB):
             t = tb * TB + k
             for d in range(2):
-                d_re = sd_ref[d, 0]
-                d_im = sd_ref[d, 1]
+                d_re = sd_ref[src, d, 0]
+                d_im = sd_ref[src, d, 1]
                 hw_re = hw_ref[t, d, 0]
                 hw_im = hw_ref[t, d, 1]
                 q_re = d_re * hw_re + d_im * hw_im
@@ -114,15 +114,23 @@
     def step(j, carry):
         i = 2 * j
 
-        @pl.when(i % n_tb == 0)
-        def _():
-            seg = i // n_tb
-            for d in range(2):
-                for part in range(2):
-                    sd_ref[d, part] = strain_ref[seg, d, part].astype(jnp.float32)
-
-        batch(i, 0)
-        batch(i + 1, 1)
+        if n_tb == 1:
+            for slot in range(2):
+                for d in range(2):
+                    for part in range(2):
+                        sd_ref[slot, d, part] = strain_ref[i + slot, d, part].astype(jnp.float32)
+            batch(i, 0, 0)
+            batch(i + 1, 1, 1)
+        else:
+            @pl.when(i % n_tb == 0)
+            def _():
+                seg = i // n_tb
+                for d in range(2):
+                    for part in range(2):
+                        sd_ref[0, d, part] = strain_ref[seg, d, part].astype(jnp.float32)
+
+            batch(i, 0, 0)
+            batch(i + 1, 1, 0)
         return carry
 
     lax.fori_loop(0, out_ref.shape[0] * n_tb // 2, step, 0)
@@ -151,7 +159,7 @@
             pltpu.VMEM((2, 2 * N1, 2 * TB * N2), jnp.float32),
             pltpu.VMEM((2, 2 * TB * N1, 2 * N2), jnp.bfloat16),
             pltpu.VMEM((n_t, 2, 2, N1, N2), jnp.float32),
-            pltpu.VMEM((2, 2, N1, N2), jnp.float32),
+            pltpu.VMEM((2, 2, 2, N1, N2), jnp.float32),
         ],
         cost_estimate=cost,
     )(isig, strain, tmpl, weights, m1, m2, tc, ts)

time: 107 us -> 107 us (level)
  no operation moved by 1% of the time
where the time goes in v13:
time: 107 us; the launch traced here: 106 us
  starting transfers between devices  28.5 us (27%)
  blocking collectives  28.2 us (26%)
  Pallas kernels  24.5 us (23%)
  waiting for transfers between devices  16.2 us (15%)
  local copies, waits for them, and re-layouts  4.03 us (4%)
  other arithmetic  3.71 us (3%)
    all_gather x5, blocking collectives, body(): gathered = lax.all_gather(gathered, axis, axis=0, tiled=True)  28.2 us
    pallas_call x2, Pallas kernels, run_search(): pl.pallas_call(functools.partial(search_kernel, n_tb), out_shape=jax.Shap...  24.5 us
    ppermute x6, starting transfers between devices, swapped(): return lax.ppermute(x, axes, [(i, i ^ k) for i in range(size)])  24 us
    ppermute x6, waiting for transfers between devices, swapped(): return lax.ppermute(x, axes, [(i, i ^ k) for i in range(size)])  8.54 us
    all_to_all x1, waiting for transfers between devices, body(): lax.all_to_all(grouped, 'ya', split_axis=0, concat_axis=0, tiled=True)  7.68 us
    all_to_all x1, starting transfers between devices, body(): lax.all_to_all(grouped, 'ya', split_axis=0, concat_axis=0, tiled=True)  4.55 us
  transfers between devices with their start and end apart: 7, of which 3 were waited for; matrix products, arithmetic and copies ran while one was open for 2% of the time, Pallas kernels for 7%

profile of v13, /device:TPU:8, one launch (start us, length us, event | category | flops | bytes accessed | tf_op | source)
XLA Modules:
  0.0 106.2 jit_solution(14107538750453790518)
XLA Ops:
  0.6 0.0 copy-start.4
  0.6 0.0 copy-start.5
  0.7 2.1 %all-gather = f32[2,4,256]{2,1,0:T(4,128)S(1)} all-gather(f32[1,4,256]{2,1,0:T(4,128)} %bitcast.25), channel_id=1, replica_groups=mesh['sx'=2,'zh'=2,'z1'=2,'z0'=2,'sc'=2,'xh'=2,'ya'=4,'yb'=2] {'sc'}, dimensions={0}, use_global_device_ids=true | all-gather | bytes 12288 | tf_op jit(solution)/shard_map/all_gather | solution.py:184
  2.7 4.7 %all_gather.16 = f32[16,256]{1,0:T(8,128)S(1)} all-gather(f32[8,256]{1,0:T(8,128)S(1)} %reshape.127), channel_id=1, replica_groups=mesh['sx'=2,'zh'=2,'z1'=2,'z0'=2,'sc'=2,'xh'=2,'ya'=4,'yb'=2] {'z0'}, dimensions={0}, use_global_device_ids=true | all-gather | bytes 24576 | tf_op jit(solution)/shard_map/all_gather | solution.py:184
  7.4 6.5 %all_gather.17 = f32[32,256]{1,0:T(8,128)S(1)} all-gather(f32[16,256]{1,0:T(8,128)S(1)} %all_gather.16), channel_id=1, replica_groups=mesh['sx'=2,'zh'=2,'z1'=2,'z0'=2,'sc'=2,'xh'=2,'ya'=4,'yb'=2] {'z1'}, dimensions={0}, use_global_device_ids=true | all-gather | bytes 49152 | tf_op jit(solution)/shard_map/all_gather | solution.py:184
  14.0 10.0 %all_gather.18 = f32[64,256]{1,0:T(8,128)S(1)} all-gather(f32[32,256]{1,0:T(8,128)S(1)} %all_gather.17), channel_id=1, replica_groups=mesh['sx'=2,'zh'=2,'z1'=2,'z0'=2,'sc'=2,'xh'=2,'ya'=4,'yb'=2] {'zh'}, dimensions={0}, use_global_device_ids=true | all-gather | bytes 98304 | tf_op jit(solution)/shard_map/all_gather | solution.py:184
  24.0 4.9 %all_gather.19 = f32[128,256]{1,0:T(8,128)S(1)} all-gather(f32[64,256]{1,0:T(8,128)S(1)} %all_gather.18), channel_id=1, replica_groups=mesh['sx'=2,'zh'=2,'z1'=2,'z0'=2,'sc'=2,'xh'=2,'ya'=4,'yb'=2] {'sx'}, dimensions={0}, use_global_device_ids=true | all-gather | bytes 196608 | tf_op jit(solution)/shard_map/all_gather | solution.py:184
  28.9 5.0 %collective-permute-start = (bf16[4,2,128,128]{3,2,1,0:T(8,128)(2,1)}, bf16[4,2,128,128]{3,2,1,0:T(8,128)(2,1)S(1)}, u32[]{:S(2)}, u32[]{:S(2)}) collective-permute-start(bf16[4,2,128,128]{3,2,1,0:T(8,128)(2,1)} %param.10), channel_id=1, source_target_pairs={{0,1},{1,0},{8,9},{9,8},{2,3},{3,2},{10,11},{11,10},{4,5},{5,4},{1... | collective-permute-start | bytes 786440 | tf_op jit(solution)/shard_map/ppermute | solution.py:170
  33.9 2.3 %collective-permute-start.1 = (bf16[4,2,128,128]{3,2,1,0:T(8,128)(2,1)}, bf16[4,2,128,128]{3,2,1,0:T(8,128)(2,1)S(1)}, u32[]{:S(2)}, u32[]{:S(2)}) collective-permute-start(bf16[4,2,128,128]{3,2,1,0:T(8,128)(2,1)} %param.10), channel_id=1, source_target_pairs={{0,8},{1,9},{8,0},{9,1},{2,10},{3,11},{10,2},{11,3},{4,12},{5,13},... | collective-permute-start | bytes 786440 | tf_op jit(solution)/shard_map/ppermute | solution.py:170
  36.2 4.5 %collective-permute-start.2 = (bf16[4,2,128,128]{3,2,1,0:T(8,128)(2,1)}, bf16[4,2,128,128]{3,2,1,0:T(8,128)(2,1)S(1)}, u32[]{:S(2)}, u32[]{:S(2)}) collective-permute-start(bf16[4,2,128,128]{3,2,1,0:T(8,128)(2,1)} %param.10), channel_id=1, source_target_pairs={{0,9},{1,8},{8,1},{9,0},{2,11},{3,10},{10,3},{11,2},{4,13},{5,12},... | collective-permute-start | bytes 786440 | tf_op jit(solution)/shard_map/ppermute | solution.py:170
  40.7 3.4 %collective-permute-start.3 = (bf16[2,2,2,128,128]{4,3,2,1,0:T(8,128)(2,1)}, bf16[2,2,2,128,128]{4,3,2,1,0:T(8,128)(2,1)S(1)}, u32[]{:S(2)}, u32[]{:S(2)}) collective-permute-start(bf16[2,2,2,128,128]{4,3,2,1,0:T(8,128)(2,1)} %strain_ref), channel_id=1, source_target_pairs={{0,2},{2,0},{4,6},{6,4},{1,3},{3,1},{5,7},{7,5},{8,10},{10,8},{12,... | collective-permute-start | bytes 786440 | tf_op jit(solution)/shard_map/ppermute | solution.py:170
  44.1 5.0 %collective-permute-start.4 = (bf16[2,2,2,128,128]{4,3,2,1,0:T(8,128)(2,1)}, bf16[2,2,2,128,128]{4,3,2,1,0:T(8,128)(2,1)S(1)}, u32[]{:S(2)}, u32[]{:S(2)}) collective-permute-start(bf16[2,2,2,128,128]{4,3,2,1,0:T(8,128)(2,1)} %strain_ref), channel_id=1, source_target_pairs={{0,4},{2,6},{4,0},{6,2},{1,5},{3,7},{5,1},{7,3},{8,12},{10,14},{12... | collective-permute-start | bytes 786440 | tf_op jit(solution)/shard_map/ppermute | solution.py:170
  49.2 1.0 constant_dynamic-update-slice_fusion.3
  50.2 0.0 copy-done.5
  50.3 0.1 copy.26
  50.4 0.1 copy.27
  50.5 0.0 copy-start.1
  50.5 0.0 collective-permute-done
  50.5 0.0 copy-done.4
  50.5 3.7 %collective-permute-start.5 = (bf16[2,2,2,128,128]{4,3,2,1,0:T(8,128)(2,1)S(1)}, bf16[2,2,2,128,128]{4,3,2,1,0:T(8,128)(2,1)S(1)}, u32[]{:S(2)}, u32[]{:S(2)}) collective-permute-start(bf16[2,2,2,128,128]{4,3,2,1,0:T(8,128)(2,1)S(1)} %copy-done.4), channel_id=1, source_target_pairs={{0,6},{2,4},{4,2},{6,0},{1,7},{3,5},{5,3},{7,1},{8,14},{10,12},{12... | collective-permute-start | bytes 786440 | tf_op jit(solution)/shard_map/ppermute | solution.py:170
  54.3 0.0 collective-permute-done.1
  54.4 0.0 collective-permute-done.2
  54.4 0.0 copy-start
  54.4 0.2 add_bitcast_fusion
  54.6 0.8 copy-done
  55.4 0.0 copy-done.1
  55.4 0.3 multiply_reduce_fusion
  55.7 0.6 div.26.isig_ref
  56.3 7.3 %shard_map.104 = f32[2,128]{1,0:T(2,128)} custom-call(f32[32]{0:T(128)} %div.26.isig_ref, bf16[2,2,2,128,128]{4,3,2,1,0:T(8,128)(2,1)} %strain_ref, bf16[16,2,128,128]{3,2,1,0:T(8,128)(2,1)} %copy-done, f32[2,128,128]{2,1,0:T(8,128)} %bitcast.19, bf16[256,256]{1,0:T(8,128)(2,1)} %constant.57.clone.m1_ref, bf16[256,256]{1,0:T(8,128)(2,1)} %constant.58.clone.m2_ref, ...), custom_call_target="tpu_custom_call" | custom-call | flops 2147483648 | bytes 1441792 | tf_op jit(solution)/shard_map/pallas_call | solution.py:152
  63.5 0.0 collective-permute-done.3
  63.5 3.0 %collective-permute-done.4 = bf16[2,2,2,128,128]{4,3,2,1,0:T(8,128)(2,1)S(1)} collective-permute-done((bf16[2,2,2,128,128]{4,3,2,1,0:T(8,128)(2,1)}, bf16[2,2,2,128,128]{4,3,2,1,0:T(8,128)(2,1)S(1)}, u32[]{:S(2)}, u32[]{:S(2)}) %collective-permute-start.4) | collective-permute-done | bytes 262176 | tf_op jit(solution)/shard_map/ppermute | solution.py:170
  66.5 5.6 %collective-permute-done.5 = bf16[2,2,2,128,128]{4,3,2,1,0:T(8,128)(2,1)S(1)} collective-permute-done((bf16[2,2,2,128,128]{4,3,2,1,0:T(8,128)(2,1)S(1)}, bf16[2,2,2,128,128]{4,3,2,1,0:T(8,128)(2,1)S(1)}, u32[]{:S(2)}, u32[]{:S(2)}) %collective-permute-start.5) | collective-permute-done | bytes 262176 | tf_op jit(solution)/shard_map/ppermute | solution.py:170
  72.0 1.0 pad_maximum_fusion.strain_ref
  73.1 17.3 %shard_map.105 = f32[6,128]{1,0:T(8,128)} custom-call(f32[32]{0:T(128)} %div.26.isig_ref, bf16[6,2,2,128,128]{4,3,2,1,0:T(8,128)(2,1)} %pad_maximum_fusion.strain_ref, bf16[16,2,128,128]{3,2,1,0:T(8,128)(2,1)} %copy-done, f32[2,128,128]{2,1,0:T(8,128)} %bitcast.20, bf16[256,256]{1,0:T(8,128)(2,1)} %constant.57.clone.m1_ref, ...), custom_call_target="tpu_custom_call" | custom-call | flops 6442450944 | bytes 1966080 | tf_op jit(solution)/shard_map/pallas_call | solution.py:152
  90.4 0.0 copy-done.3
  90.4 0.7 pad_maximum_fusion.1
  91.0 0.6 gather_fusion
  91.6 0.7 broadcast_select_fusion
  92.3 4.5 %all-to-all-start = ((f32[4,2,16]{2,1,0:T(2,128)}), f32[4,2,16]{2,1,0:T(2,128)S(1)}, u32[]{:S(2)}, u32[]{:S(2)}) async-start(f32[4,2,16]{2,1,0:T(2,128)} %broadcast_select_fusion), calls=%async_computation | async-start | bytes 8192 | tf_op jit(solution)/shard_map/all_to_all | solution.py:205
  96.8 0.0 copy-done.6
  96.9 7.7 %all-to-all-done = f32[4,2,16]{2,1,0:T(2,128)S(1)} async-done(((f32[4,2,16]{2,1,0:T(2,128)}), f32[4,2,16]{2,1,0:T(2,128)S(1)}, u32[]{:S(2)}, u32[]{:S(2)}) %all-to-all-start) | async-done | bytes 544 | tf_op jit(solution)/shard_map/all_to_all | solution.py:205
  104.5 0.1 reshape.109
  104.6 0.6 gather_fusion.1
  105.2 0.1 sqrt_bitcast_fusion
  105.3 0.1 sqrt.15
  105.4 0.1 broadcast_multiply_fusion
  105.5 0.7 select_reduce_fusion
  106.2 0.0 copy-done.2
  (20 shorter events, 0.2 us)
Async XLA Ops:
  0.6 49.9 %copy-start.4 = (bf16[2,2,2,128,128]{4,3,2,1,0:T(8,128)(2,1)S(1)}, bf16[2,2,2,128,128]{4,3,2,1,0:T(8,128)(2,1)}, u32[]{:S(2)}) copy-start(bf16[2,2,2,128,128]{4,3,2,1,0:T(8,128)(2,1)} %strain_ref) | copy-start | bytes 786436
  0.6 49.6 %copy-start.5 = (s32[64]{0:T(128)S(1)}, s32[64]{0:T(128)}, u32[]{:S(2)}) copy-start(s32[64]{0:T(128)} %param.13) | copy-start | bytes 772
  28.9 21.6 %collective-permute-start = (bf16[4,2,128,128]{3,2,1,0:T(8,128)(2,1)}, bf16[4,2,128,128]{3,2,1,0:T(8,128)(2,1)S(1)}, u32[]{:S(2)}, u32[]{:S(2)}) collective-permute-start(bf16[4,2,128,128]{3,2,1,0:T(8,128)(2,1)} %param.10), channel_id=1, source_target_pairs={{0,1},{1,0},{8,9},{9,8},{2,3},{3,2},{10,11},{11,10},{4,5},{5,4},{1... | collective-permute-start | bytes 786440 | tf_op jit(solution)/shard_map/ppermute | solution.py:170
  33.9 20.5 %collective-permute-start.1 = (bf16[4,2,128,128]{3,2,1,0:T(8,128)(2,1)}, bf16[4,2,128,128]{3,2,1,0:T(8,128)(2,1)S(1)}, u32[]{:S(2)}, u32[]{:S(2)}) collective-permute-start(bf16[4,2,128,128]{3,2,1,0:T(8,128)(2,1)} %param.10), channel_id=1, source_target_pairs={{0,8},{1,9},{8,0},{9,1},{2,10},{3,11},{10,2},{11,3},{4,12},{5,13},... | collective-permute-start | bytes 786440 | tf_op jit(solution)/shard_map/ppermute | solution.py:170
  36.2 18.2 %collective-permute-start.2 = (bf16[4,2,128,128]{3,2,1,0:T(8,128)(2,1)}, bf16[4,2,128,128]{3,2,1,0:T(8,128)(2,1)S(1)}, u32[]{:S(2)}, u32[]{:S(2)}) collective-permute-start(bf16[4,2,128,128]{3,2,1,0:T(8,128)(2,1)} %param.10), channel_id=1, source_target_pairs={{0,9},{1,8},{8,1},{9,0},{2,11},{3,10},{10,3},{11,2},{4,13},{5,12},... | collective-permute-start | bytes 786440 | tf_op jit(solution)/shard_map/ppermute | solution.py:170
  40.7 22.8 %collective-permute-start.3 = (bf16[2,2,2,128,128]{4,3,2,1,0:T(8,128)(2,1)}, bf16[2,2,2,128,128]{4,3,2,1,0:T(8,128)(2,1)S(1)}, u32[]{:S(2)}, u32[]{:S(2)}) collective-permute-start(bf16[2,2,2,128,128]{4,3,2,1,0:T(8,128)(2,1)} %strain_ref), channel_id=1, source_target_pairs={{0,2},{2,0},{4,6},{6,4},{1,3},{3,1},{5,7},{7,5},{8,10},{10,8},{12,... | collective-permute-start | bytes 786440 | tf_op jit(solution)/shard_map/ppermute | solution.py:170
  44.1 22.3 %collective-permute-start.4 = (bf16[2,2,2,128,128]{4,3,2,1,0:T(8,128)(2,1)}, bf16[2,2,2,128,128]{4,3,2,1,0:T(8,128)(2,1)S(1)}, u32[]{:S(2)}, u32[]{:S(2)}) collective-permute-start(bf16[2,2,2,128,128]{4,3,2,1,0:T(8,128)(2,1)} %strain_ref), channel_id=1, source_target_pairs={{0,4},{2,6},{4,0},{6,2},{1,5},{3,7},{5,1},{7,3},{8,12},{10,14},{12... | collective-permute-start | bytes 786440 | tf_op jit(solution)/shard_map/ppermute | solution.py:170
  50.5 4.9 %copy-start.1 = (f32[128,2,128]{2,0,1:T(8,128)}, f32[128,2,128]{2,0,1:T(8,128)S(1)}, u32[]{:S(2)}) copy-start(f32[128,2,128]{2,0,1:T(8,128)S(1)} %copy.27) | copy-start | bytes 393220
  50.5 21.5 %collective-permute-start.5 = (bf16[2,2,2,128,128]{4,3,2,1,0:T(8,128)(2,1)S(1)}, bf16[2,2,2,128,128]{4,3,2,1,0:T(8,128)(2,1)S(1)}, u32[]{:S(2)}, u32[]{:S(2)}) collective-permute-start(bf16[2,2,2,128,128]{4,3,2,1,0:T(8,128)(2,1)S(1)} %copy-done.4), channel_id=1, source_target_pairs={{0,6},{2,4},{4,2},{6,0},{1,7},{3,5},{5,3},{7,1},{8,14},{10,12},{12... | collective-permute-start | bytes 786440 | tf_op jit(solution)/shard_map/ppermute | solution.py:170
  54.4 1.0 copy-start
  73.1 17.3 %copy-start.3 = (f32[2,128]{1,0:T(2,128)S(1)}, f32[2,128]{1,0:T(2,128)}, u32[]{:S(2)}) copy-start(f32[2,128]{1,0:T(2,128)} %shard_map.104) | copy-start | bytes 3076
  73.1 23.8 %copy-start.6 = (s32[2]{0:T(128)S(1)}, s32[2]{0:T(128)}, u32[]{:S(2)}) copy-start(s32[2]{0:T(128)} %param.12) | copy-start | bytes 28
  92.3 12.3 %all-to-all-start = ((f32[4,2,16]{2,1,0:T(2,128)}), f32[4,2,16]{2,1,0:T(2,128)S(1)}, u32[]{:S(2)}, u32[]{:S(2)}) async-start(f32[4,2,16]{2,1,0:T(2,128)} %broadcast_select_fusion), calls=%async_computation | async-start | bytes 8192 | tf_op jit(solution)/shard_map/all_to_all | solution.py:205
  105.5 0.7 copy-start.2
